TPU v7x, 512 devices: a whole 4x4x16 slice. The times are simulated.
512 devices in a mesh: clip: 64 (over x, y, z_hi, core), tm: 8 (over z_lo).
Axes of the slice: x: 4, y: 4, z: 16 (z_hi: 2, z_lo: 8; z = z_hi * 8 + z_lo), core: 2. Of those that a mesh axis runs over, the one named last changes fastest.
Arguments:
- clip_in: bfloat16 [64, 16, 32, 32, 128], P('clip', 'tm'), may hold values from -6 to 6
- cotangent: bfloat16 [64, 16, 32, 32, 128], P('clip', 'tm'), may hold values from -6 to 6
- spatial_w: bfloat16 [3, 3, 128, 128], replicated, may hold values from -0.1875 to 0.1875
- spatial_b: float32 [128], replicated, may hold values from -3 to 3
- temporal_w: bfloat16 [3, 128, 128], replicated, may hold values from -0.3125 to 0.3125
Outputs:
- grad_input: bfloat16 [64, 16, 32, 32, 128], P('clip', 'tm')
- grad_spatial_w: float32 [3, 3, 128, 128], replicated
- grad_spatial_b: float32 [128], replicated
- grad_temporal_w: float32 [3, 128, 128], replicated
All inputs are finite; a program needn't handle non-finite values.
Results may differ from a plain program's by a relative error of at most 0.006.
Values may be sent and summed in bfloat16 or wider, within the bound.
No kernel may reach another device: no remote copies, remote signals or barrier semaphores. Data moves between devices by JAX's collectives and lax.ppermute only.
A program may use at most 64 MiB of HBM per device.

v0:
```python
import jax
import jax.numpy as jnp
from jax import lax
from jax.sharding import PartitionSpec as P


def spatial_forward(frames, weights, bias):
    count, height, width, chan = frames.shape
    padded = jnp.pad(frames, ((0, 0), (1, 1), (1, 1), (0, 0)))
    total = jnp.zeros((count * height * width, chan), jnp.float32)
    for i in range(3):
        for j in range(3):
            window = padded[:, i : i + height, j : j + width, :].reshape(-1, chan)
            total = total + jnp.dot(window, weights[i, j], preferred_element_type=jnp.float32)
    return (total + bias).reshape(count, height, width, chan)


def spatial_transpose(grads, weights):
    count, height, width, chan = grads.shape
    padded = jnp.pad(grads, ((0, 0), (1, 1), (1, 1), (0, 0)))
    total = jnp.zeros((count * height * width, chan), jnp.float32)
    for i in range(3):
        for j in range(3):
            window = padded[:, 2 - i : 2 - i + height, 2 - j : 2 - j + width, :].reshape(-1, chan)
            total = total + jnp.dot(window, weights[i, j].T, preferred_element_type=jnp.float32)
    return total.reshape(count, height, width, chan)


def spatial_weight_grad(frames, grads):
    count, height, width, chan = frames.shape
    padded = jnp.pad(frames, ((0, 0), (1, 1), (1, 1), (0, 0)))
    flat_grads = grads.reshape(-1, chan)
    result = []
    for i in range(3):
        row_terms = []
        for j in range(3):
            window = padded[:, i : i + height, j : j + width, :].reshape(-1, chan)
            row_terms.append(
                lax.dot_general(
                    window, flat_grads, (((0,), (0,)), ((), ())), preferred_element_type=jnp.float32
                )
            )
        result.append(jnp.stack(row_terms))
    return jnp.stack(result)


def temporal_back(act_before, act, cot, cot_after, temporal_w):
    count, height, width, chan = act.shape
    earlier = jnp.concatenate([act_before, act], axis=0)
    later = jnp.concatenate([cot, cot_after], axis=0)
    flat_cot = cot.reshape(-1, chan)
    grad_act = jnp.zeros((count * height * width, chan), jnp.float32)
    lag_terms = []
    for k in range(3):
        grad_act = grad_act + jnp.dot(
            later[k : k + count].reshape(-1, chan),
            temporal_w[k].T,
            preferred_element_type=jnp.float32,
        )
        shifted = earlier[2 - k : 2 - k + count].reshape(-1, chan)
        lag_terms.append(
            lax.dot_general(
                shifted, flat_cot, (((0,), (0,)), ((), ())), preferred_element_type=jnp.float32
            )
        )
    grad_act = grad_act.astype(jnp.bfloat16).reshape(count, height, width, chan)
    return (grad_act, jnp.stack(lag_terms))


def local(clip_in, cotangent, spatial_w, spatial_b, temporal_w):
    frames = clip_in[0]
    cot = cotangent[0]
    count, height, width, chan = frames.shape
    pre = spatial_forward(frames, spatial_w, spatial_b)
    act = jax.nn.silu(pre).astype(jnp.bfloat16)
    rows_act, rows_cot = (
        lax.all_to_all(act[None], "tm", split_axis=2, concat_axis=1, tiled=True),
        lax.all_to_all(cot[None], "tm", split_axis=2, concat_axis=1, tiled=True),
    )
    band_act = rows_act[0]
    band_cot = rows_cot[0]
    blank = jnp.zeros((2,) + band_act.shape[1:], jnp.bfloat16)
    band_grad, grad_tw = temporal_back(blank, band_act, band_cot, blank, temporal_w)
    grad_act = lax.all_to_all(band_grad[None], "tm", split_axis=1, concat_axis=2, tiled=True)[0]
    sig = jax.nn.sigmoid(pre)
    grad_pre = (grad_act.astype(jnp.float32) * sig * (1.0 + pre * (1.0 - sig))).astype(jnp.bfloat16)
    grad_in = (cot.astype(jnp.float32) + spatial_transpose(grad_pre, spatial_w)).astype(
        jnp.bfloat16
    )
    grad_sw = spatial_weight_grad(frames, grad_pre)
    grad_sb = jnp.sum(grad_pre.astype(jnp.float32).reshape(-1, chan), axis=0)
    grad_sw, grad_sb, grad_tw = lax.psum((grad_sw, grad_sb, grad_tw), ("clip", "tm"))
    total_cells = lax.axis_size("clip") * count * lax.axis_size("tm") * height * width
    norm = 1.0 / jnp.sqrt(jnp.float32(total_cells))
    return (grad_in[None], grad_sw * norm, grad_sb * norm, grad_tw * norm)


def solution(mesh):
    in_specs = (P("clip", "tm", None, None, None), P("clip", "tm", None, None, None), P(), P(), P())
    out_specs = (P("clip", "tm", None, None, None), P(), P(), P())
    return jax.shard_map(local, mesh=mesh, in_specs=in_specs, out_specs=out_specs, check_vma=False)
```

profile of v0, /device:TPU:1, one launch (start us, length us, event | category | flops | bytes accessed | tf_op | source)
XLA Modules:
  0.0 700.9 jit_solution(778138313744445646)
XLA Ops:
  7.2 1.9 copy.15
  9.1 13.2 %all-to-all-start = ((bf16[1,2,32,32,128]{4,3,1,0,2:T(8,128)(2,1)}), bf16[1,2,32,32,128]{4,3,1,0,2:T(8,128)(2,1)S(1)}, u32[]{:S(2)}, u32[]{:S(2)}) async-start(bf16[1,2,32,32,128]{4,3,1,0,2:T(8,128)(2,1)} %copy.15), calls=%async_computation | async-start | bytes 1048576 | tf_op jit(solution)/shard_map/all_to_all | solution.py:78
  22.3 2.1 pad_slice_fusion.8
  24.7 18.5 %all-to-all-done = bf16[1,2,32,32,128]{4,3,1,0,2:T(8,128)(2,1)S(1)} async-done(((bf16[1,2,32,32,128]{4,3,1,0,2:T(8,128)(2,1)}), bf16[1,2,32,32,128]{4,3,1,0,2:T(8,128)(2,1)S(1)}, u32[]{:S(2)}, u32[]{:S(2)}) %all-to-all-start) | async-done | bytes 524320 | tf_op jit(solution)/shard_map/all_to_all | solution.py:78
  44.8 1.1 fusion.1
  45.9 11.7 %all-to-all-start.1 = ((bf16[1,16,4,32,128]{4,3,2,0,1:T(8,128)(2,1)}), bf16[1,16,4,32,128]{4,3,2,0,1:T(8,128)(2,1)S(1)}, u32[]{:S(2)}, u32[]{:S(2)}) async-start(bf16[1,16,4,32,128]{4,3,2,0,1:T(8,128)(2,1)} %bitcast.262), calls=%async_computation.1 | async-start | bytes 1048576 | tf_op jit(solution)/shard_map/all_to_all | solution.py:84
  57.6 1.4 convolution_add_fusion.15
  63.4 1.2 convolution_add_fusion.9
  64.7 13.7 %all-to-all-done.1 = bf16[1,16,4,32,128]{4,3,2,0,1:T(8,128)(2,1)S(1)} async-done(((bf16[1,16,4,32,128]{4,3,2,0,1:T(8,128)(2,1)}), bf16[1,16,4,32,128]{4,3,2,0,1:T(8,128)(2,1)S(1)}, u32[]{:S(2)}, u32[]{:S(2)}) %all-to-all-start.1) | async-done | bytes 524320 | tf_op jit(solution)/shard_map/all_to_all | solution.py:84
  79.4 1.4 convert_reduce_fusion
  81.2 1.0 convolution_bitcast_fusion.10
  82.2 1.0 convolution_bitcast_fusion.11
  83.1 1.0 convolution_bitcast_fusion.6
  84.1 1.0 convolution_bitcast_fusion.8
  85.1 1.0 convolution_bitcast_fusion.9
  86.0 1.0 convolution_bitcast_fusion.3
  88.0 1.0 convolution_bitcast_fusion.5
  88.9 2.2 pad_slice_fusion
  91.1 1.1 multiply_convert_fusion
  92.2 11.6 %all-to-all-start.2 = ((bf16[1,2,32,32,128]{4,3,1,0,2:T(8,128)(2,1)}), bf16[1,2,32,32,128]{4,3,1,0,2:T(8,128)(2,1)S(1)}, u32[]{:S(2)}, u32[]{:S(2)}) async-start(bf16[1,2,32,32,128]{4,3,1,0,2:T(8,128)(2,1)} %multiply_convert_fusion), calls=%async_computation.2 | async-start | bytes 1048576 | tf_op jit(solution)/shard_map/all_to_all | solution.py:77
  104.5 108.0 %psum.22 = f32[128]{0:T(128)S(1)} all-reduce(f32[128]{0:T(128)S(1)} %get-tuple-element.6), channel_id=1, replica_groups=mesh['clip'=64,'tm'=8] {'clip','tm'}, use_global_device_ids=true, to_apply=%region_2.3 | all-reduce | flops 128 | bytes 1024 | tf_op jit(solution)/shard_map/psum | solution.py:92
  212.5 1.4 convolution_add_fusion.7
  226.1 465.3 %all-reduce.7.cloned.1.call-done = (f32[3,3,128,128]{3,2,1,0:T(8,128)}, f32[3,128,128]{2,1,0:T(8,128)}) async-done(((f32[3,3,128,128]{3,2,1,0:T(8,128)}, f32[3,128,128]{2,1,0:T(8,128)}), (f32[3,3,128,128]{3,2,1,0:T(8,128)}, f32[3,128,128]{2,1,0:T(8,128)})) %all-reduce.7.cloned.1.call-update) | async-done | bytes 786448 | tf_op jit(solution)/shard_map/psum | solution.py:92
  691.4 2.0 broadcast_multiply_fusion
  (95 shorter events, 22.0 us)
Async XLA Ops:
  9.1 13.2 %copy-start = (bf16[1,2,32,32,128]{4,3,2,1,0:T(8,128)(2,1)S(1)}, bf16[1,2,32,32,128]{4,3,2,1,0:T(8,128)(2,1)}, u32[]{:S(2)}) copy-start(bf16[1,2,32,32,128]{4,3,2,1,0:T(8,128)(2,1)} %param.5) | copy-start | bytes 1572868
  9.1 34.1 %all-to-all-start = ((bf16[1,2,32,32,128]{4,3,1,0,2:T(8,128)(2,1)}), bf16[1,2,32,32,128]{4,3,1,0,2:T(8,128)(2,1)S(1)}, u32[]{:S(2)}, u32[]{:S(2)}) async-start(bf16[1,2,32,32,128]{4,3,1,0,2:T(8,128)(2,1)} %copy.15), calls=%async_computation | async-start | bytes 1048576 | tf_op jit(solution)/shard_map/all_to_all | solution.py:78
  22.3 2.1 copy-start.15
  45.9 32.5 %all-to-all-start.1 = ((bf16[1,16,4,32,128]{4,3,2,0,1:T(8,128)(2,1)}), bf16[1,16,4,32,128]{4,3,2,0,1:T(8,128)(2,1)S(1)}, u32[]{:S(2)}, u32[]{:S(2)}) async-start(bf16[1,16,4,32,128]{4,3,2,0,1:T(8,128)(2,1)} %bitcast.262), calls=%async_computation.1 | async-start | bytes 1048576 | tf_op jit(solution)/shard_map/all_to_all | solution.py:84
  57.6 1.4 copy-start.10
  59.0 1.0 copy-start.9
  60.3 1.0 copy-start.8
  61.3 1.0 copy-start.7
  62.4 1.0 copy-start.6
  64.7 13.8 %copy-start.16 = (f32[2048,128]{1,0:T(8,128)S(1)}, f32[2048,128]{1,0:T(8,128)}, u32[]{:S(2)}) copy-start(f32[2048,128]{1,0:T(8,128)} %convolution_add_fusion.9) | copy-start | bytes 3145732
  78.4 1.0 copy-start.17
  92.2 11.7 %copy-start.13 = (bf16[2048,128]{1,0:T(8,128)(2,1)S(1)}, bf16[2048,128]{1,0:T(8,128)(2,1)}, u32[]{:S(2)}) copy-start(bf16[2048,128]{1,0:T(8,128)(2,1)} %get-tuple-element.7) | copy-start | bytes 1572868
  92.2 130.4 %all-to-all-start.2 = ((bf16[1,2,32,32,128]{4,3,1,0,2:T(8,128)(2,1)}), bf16[1,2,32,32,128]{4,3,1,0,2:T(8,128)(2,1)S(1)}, u32[]{:S(2)}, u32[]{:S(2)}) async-start(bf16[1,2,32,32,128]{4,3,1,0,2:T(8,128)(2,1)} %multiply_convert_fusion), calls=%async_computation.2 | async-start | bytes 1048576 | tf_op jit(solution)/shard_map/all_to_all | solution.py:77
  103.8 587.6 %all-reduce.7.cloned.1.call-start = ((), (), s32[]{:S(2)}) async-start(), calls=%async_computation.3 | async-start | bytes 1572864 | tf_op jit(solution)/shard_map/psum | solution.py:92
  212.5 1.4 copy-start.11
  214.8 1.0 copy-start.24
  215.8 1.3 copy-start.5
  217.1 1.0 copy-start.14
  218.1 1.0 copy-start.4
  219.2 1.0 copy-start.3
  220.2 1.0 copy-start.2
  221.2 1.0 copy-start.1
  223.9 1.3 copy-start.12
  691.4 2.0 copy-start.18
  (9 other events, 7.9 us)
Sparse Core Ops, SparseCore 0:
  224.8 466.5 all-reduce.6
where the time goes:
time: 703 us; the launch traced here: 701 us
  waiting for transfers between devices  498 us (71%)
  blocking collectives  108 us (15%)
  starting transfers between devices  36.5 us (5%)
  matrix products  20.1 us (3%)
  local copies, waits for them, and re-layouts  17.1 us (2%)
  between operations  14.4 us (2%)
  other arithmetic  7.21 us (1%)
    psum x1, waiting for transfers between devices, local(): lax.psum((grad_sw, grad_sb, grad_tw), ('clip', 'tm'))  465 us
    psum x1, blocking collectives, local(): lax.psum((grad_sw, grad_sb, grad_tw), ('clip', 'tm'))  108 us
    all_to_all x1, waiting for transfers between devices, local(): lax.all_to_all(cot[None], 'tm', split_axis=2, concat_axis=1, tiled=True)  18.5 us
  transfers between devices with their start and end apart: 4, of which 3 were waited for; matrix products, arithmetic and copies ran while one was open for 2% of the time, Pallas kernels for 0%

commit v1 on v0

--- a/solution.py
+++ b/solution.py
@@ -2,6 +2,8 @@
 import jax.numpy as jnp
 from jax import lax
 from jax.sharding import PartitionSpec as P
+
+GRAY4 = (0, 1, 3, 2)
 
 
 def spatial_forward(frames, weights, bias):
@@ -44,44 +46,87 @@
     return jnp.stack(result)
 
 
-def temporal_back(act_before, act, cot, cot_after, temporal_w):
+def temporal_back(act, later, temporal_w):
     count, height, width, chan = act.shape
-    earlier = jnp.concatenate([act_before, act], axis=0)
-    later = jnp.concatenate([cot, cot_after], axis=0)
-    flat_cot = cot.reshape(-1, chan)
+    flat_act = act.reshape(-1, chan)
     grad_act = jnp.zeros((count * height * width, chan), jnp.float32)
     lag_terms = []
     for k in range(3):
-        grad_act = grad_act + jnp.dot(
-            later[k : k + count].reshape(-1, chan),
-            temporal_w[k].T,
-            preferred_element_type=jnp.float32,
-        )
-        shifted = earlier[2 - k : 2 - k + count].reshape(-1, chan)
+        window = later[k : k + count].reshape(-1, chan)
+        grad_act = grad_act + jnp.dot(window, temporal_w[k].T, preferred_element_type=jnp.float32)
         lag_terms.append(
             lax.dot_general(
-                shifted, flat_cot, (((0,), (0,)), ((), ())), preferred_element_type=jnp.float32
+                flat_act, window, (((0,), (0,)), ((), ())), preferred_element_type=jnp.float32
             )
         )
     grad_act = grad_act.astype(jnp.bfloat16).reshape(count, height, width, chan)
-    return (grad_act, jnp.stack(lag_terms))
+    return grad_act, jnp.stack(lag_terms)
+
+
+def butterfly_steps(n_clip, n_tm):
+    n_x = n_clip // 16
+    steps = []
+
+    def clip_step(field, size, stride, labels, bit, halve):
+        perm, bits = [], []
+        pos = {lab: r for r, lab in enumerate(labels)}
+        for c in range(n_clip):
+            r = (c // stride) % size
+            lab = labels[r]
+            r2 = pos[lab ^ (1 << bit)]
+            perm.append((c, c + (r2 - r) * stride))
+            bits.append((lab >> bit) & 1)
+        steps.append(("clip", tuple(perm), tuple(bits), halve))
+
+    clip_step("core", 2, 1, (0, 1), 0, True)
+    for b in range(2):
+        clip_step("x", n_x, 16, GRAY4, b, True)
+    for b in range(2):
+        clip_step("y", 4, 4, GRAY4, b, False)
+    clip_step("zh", 2, 2, (0, 1), 0, False)
+    b = 0
+    while (1 << b) < n_tm:
+        perm = tuple((t, t ^ (1 << b)) for t in range(n_tm))
+        bits = tuple((t >> b) & 1 for t in range(n_tm))
+        steps.append(("tm", perm, bits, False))
+        b += 1
+    return steps
+
+
+def all_reduce(x, n_clip, n_tm):
+    steps = butterfly_steps(n_clip, n_tm)
+    halved = []
+    for axis, perm, bits, halve in steps:
+        if halve:
+            bit = jnp.asarray(bits, jnp.int32)[lax.axis_index(axis)]
+            h = x.shape[0] // 2
+            keep = lax.dynamic_slice_in_dim(x, bit * h, h)
+            send = lax.dynamic_slice_in_dim(x, (1 - bit) * h, h)
+            x = keep + lax.ppermute(send, axis, perm)
+            halved.append((axis, perm, bits))
+        else:
+            x = x + lax.ppermute(x, axis, perm)
+    for axis, perm, bits in halved[::-1]:
+        bit = jnp.asarray(bits, jnp.int32)[lax.axis_index(axis)]
+        other = lax.ppermute(x, axis, perm)
+        both = jnp.stack([x, other])
+        first = lax.dynamic_index_in_dim(both, bit, keepdims=False)
+        second = lax.dynamic_index_in_dim(both, 1 - bit, keepdims=False)
+        x = jnp.concatenate([first, second], 0)
+    return x
 
 
 def local(clip_in, cotangent, spatial_w, spatial_b, temporal_w):
     frames = clip_in[0]
     cot = cotangent[0]
     count, height, width, chan = frames.shape
+    n_tm = lax.axis_size("tm")
+    n_clip = lax.axis_size("clip")
+    after = lax.ppermute(cot, "tm", [(t, t - 1) for t in range(1, n_tm)])
     pre = spatial_forward(frames, spatial_w, spatial_b)
     act = jax.nn.silu(pre).astype(jnp.bfloat16)
-    rows_act, rows_cot = (
-        lax.all_to_all(act[None], "tm", split_axis=2, concat_axis=1, tiled=True),
-        lax.all_to_all(cot[None], "tm", split_axis=2, concat_axis=1, tiled=True),
-    )
-    band_act = rows_act[0]
-    band_cot = rows_cot[0]
-    blank = jnp.zeros((2,) + band_act.shape[1:], jnp.bfloat16)
-    band_grad, grad_tw = temporal_back(blank, band_act, band_cot, blank, temporal_w)
-    grad_act = lax.all_to_all(band_grad[None], "tm", split_axis=1, concat_axis=2, tiled=True)[0]
+    later = jnp.concatenate([cot, after], axis=0)
+    grad_act, grad_tw = temporal_back(act, later, temporal_w)
     sig = jax.nn.sigmoid(pre)
     grad_pre = (grad_act.astype(jnp.float32) * sig * (1.0 + pre * (1.0 - sig))).astype(jnp.bfloat16)
     grad_in = (cot.astype(jnp.float32) + spatial_transpose(grad_pre, spatial_w)).astype(
@@ -89,10 +134,27 @@
     )
     grad_sw = spatial_weight_grad(frames, grad_pre)
     grad_sb = jnp.sum(grad_pre.astype(jnp.float32).reshape(-1, chan), axis=0)
-    grad_sw, grad_sb, grad_tw = lax.psum((grad_sw, grad_sb, grad_tw), ("clip", "tm"))
-    total_cells = lax.axis_size("clip") * count * lax.axis_size("tm") * height * width
+    n_sw = 9 * chan
+    n_tw = 3 * chan
+    rows = n_sw + n_tw + 1
+    quantum = 64
+    padded_rows = -(-rows // quantum) * quantum
+    packed = jnp.concatenate(
+        [
+            grad_sw.reshape(n_sw, chan),
+            grad_tw.reshape(n_tw, chan),
+            grad_sb[None],
+            jnp.zeros((padded_rows - rows, chan), jnp.float32),
+        ],
+        axis=0,
+    )
+    total = all_reduce(packed, n_clip, n_tm)
+    total_cells = n_clip * count * n_tm * height * width
     norm = 1.0 / jnp.sqrt(jnp.float32(total_cells))
-    return (grad_in[None], grad_sw * norm, grad_sb * norm, grad_tw * norm)
+    out_sw = total[:n_sw].reshape(3, 3, chan, chan) * norm
+    out_tw = total[n_sw : n_sw + n_tw].reshape(3, chan, chan) * norm
+    out_sb = total[n_sw + n_tw] * norm
+    return (grad_in[None], out_sw, out_sb, out_tw)
 
 
 def solution(mesh):

time: 703 us -> 141 us (0.20)
  waiting for transfers between devices: 498 us -> 34.6 us
  blocking collectives: 108 us -> 0 us
  starting transfers between devices: 36.5 us -> 59.7 us
  matrix products: 20.1 us -> 11.4 us
    psum x1 -> x0, waiting for transfers between devices: 465 us -> none  [local(): lax.psum((grad_sw, grad_sb, grad_tw), ('clip', 'tm'))]
    psum x1 -> x0, blocking collectives: 108 us -> none  [local(): lax.psum((grad_sw, grad_sb, grad_tw), ('clip', 'tm'))]
    ppermute x0 -> x13, starting transfers between devices: none -> 59.7 us  [the longest x6 30.7 us: all_reduce(): x = x + lax.ppermute(x, axis, perm)]
    all_to_all x3 -> x0, starting transfers between devices: 36.5 us -> none  [the longest x1 13.2 us: local(): lax.all_to_all(cot[None], 'tm', split_axis=2, concat_axis=1, tiled=True)]
    ppermute x0 -> x13, waiting for transfers between devices: none -> 34.6 us  [the longest x6 23.8 us: all_reduce(): x = x + lax.ppermute(x, axis, perm)]
    all_to_all x3 -> x0, waiting for transfers between devices: 32.2 us -> none  [the longest x1 18.5 us: local(): lax.all_to_all(cot[None], 'tm', split_axis=2, concat_axis=1, tiled=True)]
  transfers between devices with their start and end apart: 4 -> 13, of which waited for: 3 -> 10; matrix products, arithmetic and copies ran while one was open for 2% -> 11% of each run, Pallas kernels for 0% -> 0%
where the time goes in v1:
time: 141 us; the launch traced here: 140 us
  starting transfers between devices  59.7 us (42%)
  waiting for transfers between devices  34.6 us (25%)
  local copies, waits for them, and re-layouts  15.4 us (11%)
  between operations  14.8 us (10%)
  matrix products  11.4 us (8%)
  other arithmetic  4.24 us (3%)
    ppermute x6, starting transfers between devices, all_reduce(): x = x + lax.ppermute(x, axis, perm)  30.7 us
    ppermute x6, waiting for transfers between devices, all_reduce(): x = x + lax.ppermute(x, axis, perm)  23.8 us
    ppermute x3, starting transfers between devices, all_reduce(): other = lax.ppermute(x, axis, perm)  15.1 us
    ppermute x3, starting transfers between devices, all_reduce(): x = keep + lax.ppermute(send, axis, perm)  12.6 us
    unnamed x24, local copies, waits for them, and re-layouts  6.54 us
    ppermute x3, waiting for transfers between devices, all_reduce(): other = lax.ppermute(x, axis, perm)  5.95 us
    slice x1, local copies, waits for them, and re-layouts, spatial_forward(): window = padded[:, i:i + height, j:j + width, :].reshape(-1, chan)  5.9 us
    ppermute x3, waiting for transfers between devices, all_reduce(): x = keep + lax.ppermute(send, axis, perm)  4.86 us
  transfers between devices with their start and end apart: 13, of which 10 were waited for; matrix products, arithmetic and copies ran while one was open for 11% of the time, Pallas kernels for 0%

profile of v1, /device:TPU:1, one launch (start us, length us, event | category | flops | bytes accessed | tf_op | source)
XLA Modules:
  0.0 140.1 jit_solution(692844634299221665)
XLA Ops:
  0.6 1.3 collective-permute-start
  1.9 5.9 %pad_slice_fusion.8 = (bf16[2,32,32,128]{3,2,1,0:T(8,128)(2,1)}, bf16[2,32,32,128]{3,2,1,0:T(8,128)(2,1)}, bf16[2,32,32,128]{3,2,1,0:T(8,128)(2,1)S(1)}, bf16[2,...) fusion(bf16[2,32,32,128]{3,2,1,0:T(8,128)(2,1)} %bitcast.228), kind=kLoop, calls=%fused_computation.53 | loop fusion | bytes 4718592 | tf_op jit(solution)/shard_map/slice | solution.py:15
  14.8 1.0 fusion.37
  24.4 8.7 %collective-permute-start.1 = (f32[800,128]{1,0:T(8,128)S(1)}, f32[800,128]{1,0:T(8,128)S(1)}, u32[]{:S(2)}, u32[]{:S(2)}) collective-permute-start(f32[800,128]{1,0:T(8,128)S(1)} %constant_dynamic-slice_fusion.2), channel_id=1, source_target_pairs={{0,8},{8,0},{16,24},{24,16},{32,40},{40,32},{48,56},{56,48},{64,72... | collective-permute-start | bytes 1228808 | tf_op jit(solution)/shard_map/ppermute | solution.py:105
  35.8 1.9 %collective-permute-start.2 = (f32[400,128]{1,0:T(8,128)S(1)}, f32[400,128]{1,0:T(8,128)S(1)}, u32[]{:S(2)}, u32[]{:S(2)}) collective-permute-start(f32[400,128]{1,0:T(8,128)S(1)} %constant_dynamic-slice_fusion.1), channel_id=1, source_target_pairs={{0,128},{8,136},{16,144},{24,152},{32,160},{40,168},{48,176},{56,1... | collective-permute-start | bytes 614408 | tf_op jit(solution)/shard_map/ppermute | solution.py:105
  50.7 1.9 %collective-permute-start.3 = (f32[200,128]{1,0:T(8,128)S(1)}, f32[200,128]{1,0:T(8,128)S(1)}, u32[]{:S(2)}, u32[]{:S(2)}) collective-permute-start(f32[200,128]{1,0:T(8,128)S(1)} %constant_dynamic-slice_fusion), channel_id=1, source_target_pairs={{0,384},{8,392},{16,400},{24,408},{32,416},{40,424},{48,432},{56,4... | collective-permute-start | bytes 307208 | tf_op jit(solution)/shard_map/ppermute | solution.py:105
  53.3 4.9 %collective-permute-done.3 = f32[200,128]{1,0:T(8,128)S(1)} collective-permute-done((f32[200,128]{1,0:T(8,128)S(1)}, f32[200,128]{1,0:T(8,128)S(1)}, u32[]{:S(2)}, u32[]{:S(2)}) %collective-permute-start.3) | collective-permute-done | bytes 102432 | tf_op jit(solution)/shard_map/ppermute | solution.py:105
  58.2 1.9 %collective-permute-start.4 = (f32[200,128]{1,0:T(8,128)S(1)}, f32[200,128]{1,0:T(8,128)S(1)}, u32[]{:S(2)}, u32[]{:S(2)}) collective-permute-start(f32[200,128]{1,0:T(8,128)S(1)} %dynamic-slice_add_fusion.2), channel_id=1, source_target_pairs={{0,32},{8,40},{16,48},{24,56},{32,0},{40,8},{48,16},{56,24},{64,96... | collective-permute-start | bytes 307208 | tf_op jit(solution)/shard_map/ppermute | solution.py:108
  60.5 3.2 %collective-permute-done.4 = f32[200,128]{1,0:T(8,128)S(1)} collective-permute-done((f32[200,128]{1,0:T(8,128)S(1)}, f32[200,128]{1,0:T(8,128)S(1)}, u32[]{:S(2)}, u32[]{:S(2)}) %collective-permute-start.4) | collective-permute-done | bytes 102432 | tf_op jit(solution)/shard_map/ppermute | solution.py:108
  63.6 1.9 %collective-permute-start.5 = (f32[200,128]{1,0:T(8,128)S(1)}, f32[200,128]{1,0:T(8,128)S(1)}, u32[]{:S(2)}, u32[]{:S(2)}) collective-permute-start(f32[200,128]{1,0:T(8,128)S(1)} %add.201), channel_id=1, source_target_pairs={{0,96},{8,104},{16,112},{24,120},{32,64},{40,72},{48,80},{56,88},{... | collective-permute-start | bytes 307208 | tf_op jit(solution)/shard_map/ppermute | solution.py:108
  65.9 4.4 %collective-permute-done.5 = f32[200,128]{1,0:T(8,128)S(1)} collective-permute-done((f32[200,128]{1,0:T(8,128)S(1)}, f32[200,128]{1,0:T(8,128)S(1)}, u32[]{:S(2)}, u32[]{:S(2)}) %collective-permute-start.5) | collective-permute-done | bytes 102432 | tf_op jit(solution)/shard_map/ppermute | solution.py:108
  70.3 11.1 %collective-permute-start.6 = (f32[200,128]{1,0:T(8,128)S(1)}, f32[200,128]{1,0:T(8,128)S(1)}, u32[]{:S(2)}, u32[]{:S(2)}) collective-permute-start(f32[200,128]{1,0:T(8,128)S(1)} %add.202), channel_id=1, source_target_pairs={{0,16},{8,24},{16,0},{24,8},{32,48},{40,56},{48,32},{56,40},{64,80... | collective-permute-start | bytes 307208 | tf_op jit(solution)/shard_map/ppermute | solution.py:108
  81.7 3.0 %collective-permute-done.6 = f32[200,128]{1,0:T(8,128)S(1)} collective-permute-done((f32[200,128]{1,0:T(8,128)S(1)}, f32[200,128]{1,0:T(8,128)S(1)}, u32[]{:S(2)}, u32[]{:S(2)}) %collective-permute-start.6) | collective-permute-done | bytes 102432 | tf_op jit(solution)/shard_map/ppermute | solution.py:108
  84.7 5.2 %collective-permute-start.7 = (f32[200,128]{1,0:T(8,128)S(1)}, f32[200,128]{1,0:T(8,128)S(1)}, u32[]{:S(2)}, u32[]{:S(2)}) collective-permute-start(f32[200,128]{1,0:T(8,128)S(1)} %add.203), channel_id=1, source_target_pairs={{0,1},{1,0},{2,3},{3,2},{4,5},{5,4},{6,7},{7,6},{8,9},{9,8},{10,11... | collective-permute-start | bytes 307208 | tf_op jit(solution)/shard_map/ppermute | solution.py:108
  90.2 5.2 %collective-permute-done.7 = f32[200,128]{1,0:T(8,128)S(1)} collective-permute-done((f32[200,128]{1,0:T(8,128)S(1)}, f32[200,128]{1,0:T(8,128)S(1)}, u32[]{:S(2)}, u32[]{:S(2)}) %collective-permute-start.7) | collective-permute-done | bytes 102432 | tf_op jit(solution)/shard_map/ppermute | solution.py:108
  95.4 2.5 %collective-permute-start.8 = (f32[200,128]{1,0:T(8,128)S(1)}, f32[200,128]{1,0:T(8,128)S(1)}, u32[]{:S(2)}, u32[]{:S(2)}) collective-permute-start(f32[200,128]{1,0:T(8,128)S(1)} %add.204), channel_id=1, source_target_pairs={{0,2},{1,3},{2,0},{3,1},{4,6},{5,7},{6,4},{7,5},{8,10},{9,11},{10,... | collective-permute-start | bytes 307208 | tf_op jit(solution)/shard_map/ppermute | solution.py:108
  98.2 3.9 %collective-permute-done.8 = f32[200,128]{1,0:T(8,128)S(1)} collective-permute-done((f32[200,128]{1,0:T(8,128)S(1)}, f32[200,128]{1,0:T(8,128)S(1)}, u32[]{:S(2)}, u32[]{:S(2)}) %collective-permute-start.8) | collective-permute-done | bytes 102432 | tf_op jit(solution)/shard_map/ppermute | solution.py:108
  102.1 8.1 %collective-permute-start.9 = (f32[200,128]{1,0:T(8,128)S(1)}, f32[200,128]{1,0:T(8,128)S(1)}, u32[]{:S(2)}, u32[]{:S(2)}) collective-permute-start(f32[200,128]{1,0:T(8,128)S(1)} %add.205), channel_id=1, source_target_pairs={{0,4},{1,5},{2,6},{3,7},{4,0},{5,1},{6,2},{7,3},{8,12},{9,13},{10,... | collective-permute-start | bytes 307208 | tf_op jit(solution)/shard_map/ppermute | solution.py:108
  110.6 4.1 %collective-permute-done.9 = f32[200,128]{1,0:T(8,128)S(1)} collective-permute-done((f32[200,128]{1,0:T(8,128)S(1)}, f32[200,128]{1,0:T(8,128)S(1)}, u32[]{:S(2)}, u32[]{:S(2)}) %collective-permute-start.9) | collective-permute-done | bytes 102432 | tf_op jit(solution)/shard_map/ppermute | solution.py:108
  114.6 4.2 %collective-permute-start.10 = (f32[200,128]{1,0:T(8,128)S(1)}, f32[200,128]{1,0:T(8,128)S(1)}, u32[]{:S(2)}, u32[]{:S(2)}) collective-permute-start(f32[200,128]{1,0:T(8,128)S(1)} %add.206), channel_id=1, source_target_pairs={{0,384},{8,392},{16,400},{24,408},{32,416},{40,424},{48,432},{56,4... | collective-permute-start | bytes 307208 | tf_op jit(solution)/shard_map/ppermute | solution.py:111
  119.1 2.1 %collective-permute-done.10 = f32[200,128]{1,0:T(8,128)S(1)} collective-permute-done((f32[200,128]{1,0:T(8,128)S(1)}, f32[200,128]{1,0:T(8,128)S(1)}, u32[]{:S(2)}, u32[]{:S(2)}) %collective-permute-start.10) | collective-permute-done | bytes 102432 | tf_op jit(solution)/shard_map/ppermute | solution.py:111
  121.4 7.1 %collective-permute-start.11 = (f32[400,128]{1,0:T(8,128)S(1)}, f32[400,128]{1,0:T(8,128)S(1)}, u32[]{:S(2)}, u32[]{:S(2)}) collective-permute-start(f32[400,128]{1,0:T(8,128)S(1)} %get-tuple-element.30), channel_id=1, source_target_pairs={{0,128},{8,136},{16,144},{24,152},{32,160},{40,168},{48,176},{56,1... | collective-permute-start | bytes 614408 | tf_op jit(solution)/shard_map/ppermute | solution.py:111
  128.7 3.7 %collective-permute-done.11 = f32[400,128]{1,0:T(8,128)S(1)} collective-permute-done((f32[400,128]{1,0:T(8,128)S(1)}, f32[400,128]{1,0:T(8,128)S(1)}, u32[]{:S(2)}, u32[]{:S(2)}) %collective-permute-start.11) | collective-permute-done | bytes 204832 | tf_op jit(solution)/shard_map/ppermute | solution.py:111
  132.6 3.9 %collective-permute-start.12 = (f32[800,128]{1,0:T(8,128)S(1)}, f32[800,128]{1,0:T(8,128)S(1)}, u32[]{:S(2)}, u32[]{:S(2)}) collective-permute-start(f32[800,128]{1,0:T(8,128)S(1)} %get-tuple-element.26), channel_id=1, source_target_pairs={{0,8},{8,0},{16,24},{24,16},{32,40},{40,32},{48,56},{56,48},{64,72... | collective-permute-start | bytes 1228808 | tf_op jit(solution)/shard_map/ppermute | solution.py:111
  (93 shorter events, 24.1 us)
Async XLA Ops:
  0.6 15.5 %collective-permute-start = (bf16[2,32,32,128]{3,2,1,0:T(8,128)(2,1)}, bf16[2,32,32,128]{3,2,1,0:T(8,128)(2,1)S(1)}, u32[]{:S(2)}, u32[]{:S(2)}) collective-permute-start(bf16[2,32,32,128]{3,2,1,0:T(8,128)(2,1)} %bitcast.224), channel_id=1, source_target_pairs={{1,0},{2,1},{3,2},{4,3},{5,4},{6,5},{7,6},{9,8},{10,9},{11,10},{12... | collective-permute-start | bytes 1572872 | tf_op jit(solution)/shard_map/ppermute | solution.py:125
  1.9 7.8 %copy-start.4 = (bf16[3,3,128,128]{3,2,1,0:T(8,128)(2,1)S(1)}, bf16[3,3,128,128]{3,2,1,0:T(8,128)(2,1)}, u32[]{:S(2)}) copy-start(bf16[3,3,128,128]{3,2,1,0:T(8,128)(2,1)} %param.13) | copy-start | bytes 884740
  9.8 1.0 copy-start.3
  11.4 1.0 copy-start.1
  12.7 1.0 copy-start.2
  13.7 1.0 copy-start
  16.1 0.9 copy-start.7
  17.3 1.0 copy-start.6
  17.6 0.7 copy-start.8
  24.4 11.3 %collective-permute-start.1 = (f32[800,128]{1,0:T(8,128)S(1)}, f32[800,128]{1,0:T(8,128)S(1)}, u32[]{:S(2)}, u32[]{:S(2)}) collective-permute-start(f32[800,128]{1,0:T(8,128)S(1)} %constant_dynamic-slice_fusion.2), channel_id=1, source_target_pairs={{0,8},{8,0},{16,24},{24,16},{32,40},{40,32},{48,56},{56,48},{64,72... | collective-permute-start | bytes 1228808 | tf_op jit(solution)/shard_map/ppermute | solution.py:105
  33.8 0.7 copy-start.10
  35.8 14.8 %collective-permute-start.2 = (f32[400,128]{1,0:T(8,128)S(1)}, f32[400,128]{1,0:T(8,128)S(1)}, u32[]{:S(2)}, u32[]{:S(2)}) collective-permute-start(f32[400,128]{1,0:T(8,128)S(1)} %constant_dynamic-slice_fusion.1), channel_id=1, source_target_pairs={{0,128},{8,136},{16,144},{24,152},{32,160},{40,168},{48,176},{56,1... | collective-permute-start | bytes 614408 | tf_op jit(solution)/shard_map/ppermute | solution.py:105
  38.3 0.7 copy-start.9
  50.7 7.5 %collective-permute-start.3 = (f32[200,128]{1,0:T(8,128)S(1)}, f32[200,128]{1,0:T(8,128)S(1)}, u32[]{:S(2)}, u32[]{:S(2)}) collective-permute-start(f32[200,128]{1,0:T(8,128)S(1)} %constant_dynamic-slice_fusion), channel_id=1, source_target_pairs={{0,384},{8,392},{16,400},{24,408},{32,416},{40,424},{48,432},{56,4... | collective-permute-start | bytes 307208 | tf_op jit(solution)/shard_map/ppermute | solution.py:105
  53.3 6.8 %copy-start.5 = (bf16[3,3,128,128]{3,2,1,0:T(8,128)(2,1)S(1)}, bf16[3,3,128,128]{3,2,1,0:T(8,128)(2,1)}, u32[]{:S(2)}) copy-start(bf16[3,3,128,128]{3,2,1,0:T(8,128)(2,1)} %param.13) | copy-start | bytes 884740
  58.2 5.4 %collective-permute-start.4 = (f32[200,128]{1,0:T(8,128)S(1)}, f32[200,128]{1,0:T(8,128)S(1)}, u32[]{:S(2)}, u32[]{:S(2)}) collective-permute-start(f32[200,128]{1,0:T(8,128)S(1)} %dynamic-slice_add_fusion.2), channel_id=1, source_target_pairs={{0,32},{8,40},{16,48},{24,56},{32,0},{40,8},{48,16},{56,24},{64,96... | collective-permute-start | bytes 307208 | tf_op jit(solution)/shard_map/ppermute | solution.py:108
  63.6 6.6 %collective-permute-start.5 = (f32[200,128]{1,0:T(8,128)S(1)}, f32[200,128]{1,0:T(8,128)S(1)}, u32[]{:S(2)}, u32[]{:S(2)}) collective-permute-start(f32[200,128]{1,0:T(8,128)S(1)} %add.201), channel_id=1, source_target_pairs={{0,96},{8,104},{16,112},{24,120},{32,64},{40,72},{48,80},{56,88},{... | collective-permute-start | bytes 307208 | tf_op jit(solution)/shard_map/ppermute | solution.py:108
  70.3 14.4 %collective-permute-start.6 = (f32[200,128]{1,0:T(8,128)S(1)}, f32[200,128]{1,0:T(8,128)S(1)}, u32[]{:S(2)}, u32[]{:S(2)}) collective-permute-start(f32[200,128]{1,0:T(8,128)S(1)} %add.202), channel_id=1, source_target_pairs={{0,16},{8,24},{16,0},{24,8},{32,48},{40,56},{48,32},{56,40},{64,80... | collective-permute-start | bytes 307208 | tf_op jit(solution)/shard_map/ppermute | solution.py:108
  84.7 10.7 %collective-permute-start.7 = (f32[200,128]{1,0:T(8,128)S(1)}, f32[200,128]{1,0:T(8,128)S(1)}, u32[]{:S(2)}, u32[]{:S(2)}) collective-permute-start(f32[200,128]{1,0:T(8,128)S(1)} %add.203), channel_id=1, source_target_pairs={{0,1},{1,0},{2,3},{3,2},{4,5},{5,4},{6,7},{7,6},{8,9},{9,8},{10,11... | collective-permute-start | bytes 307208 | tf_op jit(solution)/shard_map/ppermute | solution.py:108
  95.4 6.7 %collective-permute-start.8 = (f32[200,128]{1,0:T(8,128)S(1)}, f32[200,128]{1,0:T(8,128)S(1)}, u32[]{:S(2)}, u32[]{:S(2)}) collective-permute-start(f32[200,128]{1,0:T(8,128)S(1)} %add.204), channel_id=1, source_target_pairs={{0,2},{1,3},{2,0},{3,1},{4,6},{5,7},{6,4},{7,5},{8,10},{9,11},{10,... | collective-permute-start | bytes 307208 | tf_op jit(solution)/shard_map/ppermute | solution.py:108
  102.1 12.5 %collective-permute-start.9 = (f32[200,128]{1,0:T(8,128)S(1)}, f32[200,128]{1,0:T(8,128)S(1)}, u32[]{:S(2)}, u32[]{:S(2)}) collective-permute-start(f32[200,128]{1,0:T(8,128)S(1)} %add.205), channel_id=1, source_target_pairs={{0,4},{1,5},{2,6},{3,7},{4,0},{5,1},{6,2},{7,3},{8,12},{9,13},{10,... | collective-permute-start | bytes 307208 | tf_op jit(solution)/shard_map/ppermute | solution.py:108
  114.6 6.6 %collective-permute-start.10 = (f32[200,128]{1,0:T(8,128)S(1)}, f32[200,128]{1,0:T(8,128)S(1)}, u32[]{:S(2)}, u32[]{:S(2)}) collective-permute-start(f32[200,128]{1,0:T(8,128)S(1)} %add.206), channel_id=1, source_target_pairs={{0,384},{8,392},{16,400},{24,408},{32,416},{40,424},{48,432},{56,4... | collective-permute-start | bytes 307208 | tf_op jit(solution)/shard_map/ppermute | solution.py:111
  121.4 11.1 %collective-permute-start.11 = (f32[400,128]{1,0:T(8,128)S(1)}, f32[400,128]{1,0:T(8,128)S(1)}, u32[]{:S(2)}, u32[]{:S(2)}) collective-permute-start(f32[400,128]{1,0:T(8,128)S(1)} %get-tuple-element.30), channel_id=1, source_target_pairs={{0,128},{8,136},{16,144},{24,152},{32,160},{40,168},{48,176},{56,1... | collective-permute-start | bytes 614408 | tf_op jit(solution)/shard_map/ppermute | solution.py:111
  132.6 5.3 %collective-permute-start.12 = (f32[800,128]{1,0:T(8,128)S(1)}, f32[800,128]{1,0:T(8,128)S(1)}, u32[]{:S(2)}, u32[]{:S(2)}) collective-permute-start(f32[800,128]{1,0:T(8,128)S(1)} %get-tuple-element.26), channel_id=1, source_target_pairs={{0,8},{8,0},{16,24},{24,16},{32,40},{40,32},{48,56},{56,48},{64,72... | collective-permute-start | bytes 1228808 | tf_op jit(solution)/shard_map/ppermute | solution.py:111
  (1 other events, 0.7 us)

commit v2 on v1

--- a/solution.py
+++ b/solution.py
@@ -6,44 +6,31 @@
 GRAY4 = (0, 1, 3, 2)
 
 
+CONV_DIMS = ("NHWC", "HWIO", "NHWC")
+
+
 def spatial_forward(frames, weights, bias):
-    count, height, width, chan = frames.shape
-    padded = jnp.pad(frames, ((0, 0), (1, 1), (1, 1), (0, 0)))
-    total = jnp.zeros((count * height * width, chan), jnp.float32)
-    for i in range(3):
-        for j in range(3):
-            window = padded[:, i : i + height, j : j + width, :].reshape(-1, chan)
-            total = total + jnp.dot(window, weights[i, j], preferred_element_type=jnp.float32)
-    return (total + bias).reshape(count, height, width, chan)
+    total = lax.conv_general_dilated(
+        frames, weights, (1, 1), ((1, 1), (1, 1)), dimension_numbers=CONV_DIMS,
+        preferred_element_type=jnp.float32,
+    )
+    return total + bias
 
 
 def spatial_transpose(grads, weights):
-    count, height, width, chan = grads.shape
-    padded = jnp.pad(grads, ((0, 0), (1, 1), (1, 1), (0, 0)))
-    total = jnp.zeros((count * height * width, chan), jnp.float32)
-    for i in range(3):
-        for j in range(3):
-            window = padded[:, 2 - i : 2 - i + height, 2 - j : 2 - j + width, :].reshape(-1, chan)
-            total = total + jnp.dot(window, weights[i, j].T, preferred_element_type=jnp.float32)
-    return total.reshape(count, height, width, chan)
+    flipped = jnp.transpose(weights[::-1, ::-1], (0, 1, 3, 2))
+    return lax.conv_general_dilated(
+        grads, flipped, (1, 1), ((1, 1), (1, 1)), dimension_numbers=CONV_DIMS,
+        preferred_element_type=jnp.float32,
+    )
 
 
 def spatial_weight_grad(frames, grads):
-    count, height, width, chan = frames.shape
-    padded = jnp.pad(frames, ((0, 0), (1, 1), (1, 1), (0, 0)))
-    flat_grads = grads.reshape(-1, chan)
-    result = []
-    for i in range(3):
-        row_terms = []
-        for j in range(3):
-            window = padded[:, i : i + height, j : j + width, :].reshape(-1, chan)
-            row_terms.append(
-                lax.dot_general(
-                    window, flat_grads, (((0,), (0,)), ((), ())), preferred_element_type=jnp.float32
-                )
-            )
-        result.append(jnp.stack(row_terms))
-    return jnp.stack(result)
+    result = lax.conv_general_dilated(
+        frames, grads, (1, 1), ((1, 1), (1, 1)), dimension_numbers=("CHWN", "IHWO", "NHWC"),
+        preferred_element_type=jnp.float32,
+    )
+    return jnp.transpose(result, (1, 2, 0, 3))
 
 
 def temporal_back(act, later, temporal_w):

time: 141 us -> 140 us (level)
  starting transfers between devices: 59.7 us -> 70.1 us
  local copies, waits for them, and re-layouts: 15.4 us -> 7.5 us
  waiting for transfers between devices: 34.6 us -> 28.1 us
  other arithmetic: 4.24 us -> 5.97 us
    dot_general x27 -> x0, matrix products: 8.56 us -> none  [the longest x9 3.05 us: spatial_weight_grad(): lax.dot_general(window, flat_grads, (((0,), (0,)), ((), ())), preferred_e...]
    slice x2 -> x0, local copies, waits for them, and re-layouts: 6.63 us -> none  [the longest x1 5.9 us: spatial_forward(): window = padded[:, i:i + height, j:j + width, :].reshape(-1, chan)]
    ppermute x3, waiting for transfers between devices: 5.95 us -> 0.01 us  [all_reduce(): other = lax.ppermute(x, axis, perm)]
    ppermute x6, starting transfers between devices: 30.7 us -> 35.2 us  [all_reduce(): x = x + lax.ppermute(x, axis, perm)]
    transpose x0 -> x1, matrix products: none -> 3.98 us  [spatial_weight_grad(): return jnp.transpose(result, (1, 2, 0, 3))]
    conv_general_dilated x0 -> x2, matrix products: none -> 3.65 us  [the longest x1 1.95 us: spatial_forward(): lax.conv_general_dilated(frames, weights, (1, 1), ((1, 1), (1, 1)), dimen...]
    ppermute x3, starting transfers between devices: 15.1 us -> 18.4 us  [all_reduce(): other = lax.ppermute(x, axis, perm)]
    unnamed x24 -> x28, local copies, waits for them, and re-layouts: 6.54 us -> 3.29 us
  transfers between devices with their start and end apart: 13 -> 13, of which waited for: 10 -> 9; matrix products, arithmetic and copies ran while one was open for 11% -> 9% of each run, Pallas kernels for 0% -> 0%
where the time goes in v2:
time: 140 us; the launch traced here: 139 us
  starting transfers between devices  70.1 us (50%)
  waiting for transfers between devices  28.1 us (20%)
  between operations  14.8 us (11%)
  matrix products  12.7 us (9%)
  local copies, waits for them, and re-layouts  7.5 us (5%)
  other arithmetic  5.97 us (4%)
    ppermute x6, starting transfers between devices, all_reduce(): x = x + lax.ppermute(x, axis, perm)  35.2 us
    ppermute x6, waiting for transfers between devices, all_reduce(): x = x + lax.ppermute(x, axis, perm)  21 us
    ppermute x3, starting transfers between devices, all_reduce(): other = lax.ppermute(x, axis, perm)  18.4 us
    ppermute x3, starting transfers between devices, all_reduce(): x = keep + lax.ppermute(send, axis, perm)  15 us
    ppermute x3, waiting for transfers between devices, all_reduce(): x = keep + lax.ppermute(send, axis, perm)  6.38 us
    transpose x1, matrix products, spatial_weight_grad(): return jnp.transpose(result, (1, 2, 0, 3))  3.98 us
    unnamed x28, local copies, waits for them, and re-layouts  3.29 us
    dot_general x3, matrix products, temporal_back(): lax.dot_general(flat_act, window, (((0,), (0,)), ((), ())), preferred_ele...  3.17 us
  transfers between devices with their start and end apart: 13, of which 9 were waited for; matrix products, arithmetic and copies ran while one was open for 9% of the time, Pallas kernels for 0%

profile of v2, /device:TPU:1, one launch (start us, length us, event | category | flops | bytes accessed | tf_op | source)
XLA Modules:
  0.0 139.3 jit_solution(2258820353464727384)
XLA Ops:
  4.1 1.9 %multiply_convert_fusion = (bf16[32,16,5,128]{3,1,2,0:T(8,128)(2,1)S(1)}, f32[32,16,5,128]{3,1,2,0:T(8,128)S(1)}, f32[32,16,5,128]{3,1,2,0:T(8,128)S(1)}) fusion(f32[128]{0:T(128)S(1)} %copy-done.8, bf16[3,3,128,128]{3,2,1,0:T(8,128)(2,1)S(1)} %copy-done, bf16[32,2,8,7,128]{4,0,3,2,1:T(8,128)(2,1)S(1)} %fusion.12, pred[16,5]{0,1:T(8,128)(4,1)S(1)} %copy-done.12), kind=kOutput, calls=%fused_computation.11 | convolution fusion | flops 742522880 | bytes 4489808 | tf_op jit(solution)/shard_map/conv_general_dilated | solution.py:13
  16.1 4.0 %fusion.22 = f32[3,3,128,128]{3,2,1,0:T(8,128)S(1)} fusion(bf16[2,32,32,128]{3,2,1,0:T(8,128)(2,1)S(1)} %bitcast.150, bf16[2,32,32,128]{3,1,2,0:T(8,128)(2,1)S(1)} %get-tuple-element.5), kind=kOutput, calls=%fused_computation.44 | convolution fusion | flops 579076096 | bytes 1638400 | tf_op jit(solution)/shard_map/transpose | solution.py:33
  22.0 8.9 %collective-permute-start.1 = (f32[800,128]{1,0:T(8,128)S(1)}, f32[800,128]{1,0:T(8,128)S(1)}, u32[]{:S(2)}, u32[]{:S(2)}) collective-permute-start(f32[800,128]{1,0:T(8,128)S(1)} %constant_dynamic-slice_fusion.2), channel_id=1, source_target_pairs={{0,8},{8,0},{16,24},{24,16},{32,40},{40,32},{48,56},{56,48},{64,72... | collective-permute-start | bytes 1228808 | tf_op jit(solution)/shard_map/ppermute | solution.py:92
  32.9 2.5 %collective-permute-start.2 = (f32[400,128]{1,0:T(8,128)S(1)}, f32[400,128]{1,0:T(8,128)S(1)}, u32[]{:S(2)}, u32[]{:S(2)}) collective-permute-start(f32[400,128]{1,0:T(8,128)S(1)} %constant_dynamic-slice_fusion.1), channel_id=1, source_target_pairs={{0,128},{8,136},{16,144},{24,152},{32,160},{40,168},{48,176},{56,1... | collective-permute-start | bytes 614408 | tf_op jit(solution)/shard_map/ppermute | solution.py:92
  37.3 4.1 %collective-permute-done.2 = f32[400,128]{1,0:T(8,128)S(1)} collective-permute-done((f32[400,128]{1,0:T(8,128)S(1)}, f32[400,128]{1,0:T(8,128)S(1)}, u32[]{:S(2)}, u32[]{:S(2)}) %collective-permute-start.2) | collective-permute-done | bytes 204832 | tf_op jit(solution)/shard_map/ppermute | solution.py:92
  41.5 3.7 %collective-permute-start.3 = (f32[200,128]{1,0:T(8,128)S(1)}, f32[200,128]{1,0:T(8,128)S(1)}, u32[]{:S(2)}, u32[]{:S(2)}) collective-permute-start(f32[200,128]{1,0:T(8,128)S(1)} %constant_dynamic-slice_fusion), channel_id=1, source_target_pairs={{0,384},{8,392},{16,400},{24,408},{32,416},{40,424},{48,432},{56,4... | collective-permute-start | bytes 307208 | tf_op jit(solution)/shard_map/ppermute | solution.py:92
  45.8 2.2 %collective-permute-done.3 = f32[200,128]{1,0:T(8,128)S(1)} collective-permute-done((f32[200,128]{1,0:T(8,128)S(1)}, f32[200,128]{1,0:T(8,128)S(1)}, u32[]{:S(2)}, u32[]{:S(2)}) %collective-permute-start.3) | collective-permute-done | bytes 102432 | tf_op jit(solution)/shard_map/ppermute | solution.py:92
  48.1 2.5 %collective-permute-start.4 = (f32[200,128]{1,0:T(8,128)S(1)}, f32[200,128]{1,0:T(8,128)S(1)}, u32[]{:S(2)}, u32[]{:S(2)}) collective-permute-start(f32[200,128]{1,0:T(8,128)S(1)} %dynamic-slice_add_fusion.2), channel_id=1, source_target_pairs={{0,32},{8,40},{16,48},{24,56},{32,0},{40,8},{48,16},{56,24},{64,96... | collective-permute-start | bytes 307208 | tf_op jit(solution)/shard_map/ppermute | solution.py:95
  50.6 2.9 %collective-permute-done.4 = f32[200,128]{1,0:T(8,128)S(1)} collective-permute-done((f32[200,128]{1,0:T(8,128)S(1)}, f32[200,128]{1,0:T(8,128)S(1)}, u32[]{:S(2)}, u32[]{:S(2)}) %collective-permute-start.4) | collective-permute-done | bytes 102432 | tf_op jit(solution)/shard_map/ppermute | solution.py:95
  53.5 4.1 %collective-permute-start.5 = (f32[200,128]{1,0:T(8,128)S(1)}, f32[200,128]{1,0:T(8,128)S(1)}, u32[]{:S(2)}, u32[]{:S(2)}) collective-permute-start(f32[200,128]{1,0:T(8,128)S(1)} %add.119), channel_id=1, source_target_pairs={{0,96},{8,104},{16,112},{24,120},{32,64},{40,72},{48,80},{56,88},{... | collective-permute-start | bytes 307208 | tf_op jit(solution)/shard_map/ppermute | solution.py:95
  57.7 2.6 %collective-permute-done.5 = f32[200,128]{1,0:T(8,128)S(1)} collective-permute-done((f32[200,128]{1,0:T(8,128)S(1)}, f32[200,128]{1,0:T(8,128)S(1)}, u32[]{:S(2)}, u32[]{:S(2)}) %collective-permute-start.5) | collective-permute-done | bytes 102432 | tf_op jit(solution)/shard_map/ppermute | solution.py:95
  60.3 14.6 %collective-permute-start.6 = (f32[200,128]{1,0:T(8,128)S(1)}, f32[200,128]{1,0:T(8,128)S(1)}, u32[]{:S(2)}, u32[]{:S(2)}) collective-permute-start(f32[200,128]{1,0:T(8,128)S(1)} %add.120), channel_id=1, source_target_pairs={{0,16},{8,24},{16,0},{24,8},{32,48},{40,56},{48,32},{56,40},{64,80... | collective-permute-start | bytes 307208 | tf_op jit(solution)/shard_map/ppermute | solution.py:95
  75.0 2.3 %collective-permute-done.6 = f32[200,128]{1,0:T(8,128)S(1)} collective-permute-done((f32[200,128]{1,0:T(8,128)S(1)}, f32[200,128]{1,0:T(8,128)S(1)}, u32[]{:S(2)}, u32[]{:S(2)}) %collective-permute-start.6) | collective-permute-done | bytes 102432 | tf_op jit(solution)/shard_map/ppermute | solution.py:95
  77.3 2.3 %collective-permute-start.7 = (f32[200,128]{1,0:T(8,128)S(1)}, f32[200,128]{1,0:T(8,128)S(1)}, u32[]{:S(2)}, u32[]{:S(2)}) collective-permute-start(f32[200,128]{1,0:T(8,128)S(1)} %add.121), channel_id=1, source_target_pairs={{0,1},{1,0},{2,3},{3,2},{4,5},{5,4},{6,7},{7,6},{8,9},{9,8},{10,11... | collective-permute-start | bytes 307208 | tf_op jit(solution)/shard_map/ppermute | solution.py:95
  79.7 4.6 %collective-permute-done.7 = f32[200,128]{1,0:T(8,128)S(1)} collective-permute-done((f32[200,128]{1,0:T(8,128)S(1)}, f32[200,128]{1,0:T(8,128)S(1)}, u32[]{:S(2)}, u32[]{:S(2)}) %collective-permute-start.7) | collective-permute-done | bytes 102432 | tf_op jit(solution)/shard_map/ppermute | solution.py:95
  84.2 6.7 %collective-permute-start.8 = (f32[200,128]{1,0:T(8,128)S(1)}, f32[200,128]{1,0:T(8,128)S(1)}, u32[]{:S(2)}, u32[]{:S(2)}) collective-permute-start(f32[200,128]{1,0:T(8,128)S(1)} %add.122), channel_id=1, source_target_pairs={{0,2},{1,3},{2,0},{3,1},{4,6},{5,7},{6,4},{7,5},{8,10},{9,11},{10,... | collective-permute-start | bytes 307208 | tf_op jit(solution)/shard_map/ppermute | solution.py:95
  91.0 2.6 %collective-permute-done.8 = f32[200,128]{1,0:T(8,128)S(1)} collective-permute-done((f32[200,128]{1,0:T(8,128)S(1)}, f32[200,128]{1,0:T(8,128)S(1)}, u32[]{:S(2)}, u32[]{:S(2)}) %collective-permute-start.8) | collective-permute-done | bytes 102432 | tf_op jit(solution)/shard_map/ppermute | solution.py:95
  93.6 4.9 %collective-permute-start.9 = (f32[200,128]{1,0:T(8,128)S(1)}, f32[200,128]{1,0:T(8,128)S(1)}, u32[]{:S(2)}, u32[]{:S(2)}) collective-permute-start(f32[200,128]{1,0:T(8,128)S(1)} %add.123), channel_id=1, source_target_pairs={{0,4},{1,5},{2,6},{3,7},{4,0},{5,1},{6,2},{7,3},{8,12},{9,13},{10,... | collective-permute-start | bytes 307208 | tf_op jit(solution)/shard_map/ppermute | solution.py:95
  98.5 6.1 %collective-permute-done.9 = f32[200,128]{1,0:T(8,128)S(1)} collective-permute-done((f32[200,128]{1,0:T(8,128)S(1)}, f32[200,128]{1,0:T(8,128)S(1)}, u32[]{:S(2)}, u32[]{:S(2)}) %collective-permute-start.9) | collective-permute-done | bytes 102432 | tf_op jit(solution)/shard_map/ppermute | solution.py:95
  104.6 4.4 %collective-permute-start.10 = (f32[200,128]{1,0:T(8,128)S(1)}, f32[200,128]{1,0:T(8,128)S(1)}, u32[]{:S(2)}, u32[]{:S(2)}) collective-permute-start(f32[200,128]{1,0:T(8,128)S(1)} %add.124), channel_id=1, source_target_pairs={{0,384},{8,392},{16,400},{24,408},{32,416},{40,424},{48,432},{56,4... | collective-permute-start | bytes 307208 | tf_op jit(solution)/shard_map/ppermute | solution.py:98
  112.3 1.9 %collective-permute-start.11 = (f32[400,128]{1,0:T(8,128)S(1)}, f32[400,128]{1,0:T(8,128)S(1)}, u32[]{:S(2)}, u32[]{:S(2)}) collective-permute-start(f32[400,128]{1,0:T(8,128)S(1)} %get-tuple-element.15), channel_id=1, source_target_pairs={{0,128},{8,136},{16,144},{24,152},{32,160},{40,168},{48,176},{56,1... | collective-permute-start | bytes 614408 | tf_op jit(solution)/shard_map/ppermute | solution.py:98
  121.3 12.1 %collective-permute-start.12 = (f32[800,128]{1,0:T(8,128)S(1)}, f32[800,128]{1,0:T(8,128)S(1)}, u32[]{:S(2)}, u32[]{:S(2)}) collective-permute-start(f32[800,128]{1,0:T(8,128)S(1)} %get-tuple-element.11), channel_id=1, source_target_pairs={{0,8},{8,0},{16,24},{24,16},{32,40},{40,32},{48,56},{56,48},{64,72... | collective-permute-start | bytes 1228808 | tf_op jit(solution)/shard_map/ppermute | solution.py:98
  133.4 1.7 %convolution_select_fusion = f32[32,16,5,128]{3,1,2,0:T(8,128)S(1)} fusion(bf16[3,3,128,128]{3,2,1,0:T(8,128)(2,1)S(1)} %copy-done, bf16[32,2,7,2,128]{4,2,1,3,0:T(8,128)(2,1)S(1)} %slice.39, bf16[32,2,8,5,128]{4,2,1,3,0:T(8,128)(2,1)S(1)} %copy.27, pred[16,5]{0,1:T(8,128)(4,1)S(1)} %copy-done.12), kind=kOutput, calls=%fused_computation.7 | convolution fusion | flops 742326272 | bytes 2490448 | tf_op jit(solution)/shard_map/conv_general_dilated | solution.py:22
  135.6 1.4 %fusion.19 = bf16[1,2,32,32,128]{4,3,2,1,0:T(8,128)(2,1)} fusion(f32[32,2,32,128]{3,0,2,1:T(8,128)S(1)} %slice.40, bf16[1,2,32,32,128]{4,3,2,1,0:T(8,128)(2,1)S(1)} %copy-done.1), kind=kLoop, calls=%fused_computation.39 | loop fusion | flops 786432 | bytes 2097152 | tf_op jit(solution)/shard_map/broadcast_in_dim | solution.py:144
  (80 shorter events, 19.3 us)
Async XLA Ops:
  0.6 2.9 %copy-start = (bf16[3,3,128,128]{3,2,1,0:T(8,128)(2,1)S(1)}, bf16[3,3,128,128]{3,2,1,0:T(8,128)(2,1)}, u32[]{:S(2)}) copy-start(bf16[3,3,128,128]{3,2,1,0:T(8,128)(2,1)} %param.13) | copy-start | bytes 884740
  0.6 11.4 %collective-permute-start = (bf16[2,32,32,128]{3,2,1,0:T(8,128)(2,1)}, bf16[2,32,32,128]{3,2,1,0:T(8,128)(2,1)}, u32[]{:S(2)}, u32[]{:S(2)}) collective-permute-start(bf16[2,32,32,128]{3,2,1,0:T(8,128)(2,1)} %bitcast.131), channel_id=1, source_target_pairs={{1,0},{2,1},{3,2},{4,3},{5,4},{6,5},{7,6},{9,8},{10,9},{11,10},{12... | collective-permute-start | bytes 1572872 | tf_op jit(solution)/shard_map/ppermute | solution.py:112
  3.4 0.7 copy-start.12
  6.3 1.0 copy-start.2
  7.7 1.9 %copy-start.1 = (bf16[1,2,32,32,128]{4,3,2,1,0:T(8,128)(2,1)S(1)}, bf16[1,2,32,32,128]{4,3,2,1,0:T(8,128)(2,1)}, u32[]{:S(2)}) copy-start(bf16[1,2,32,32,128]{4,3,2,1,0:T(8,128)(2,1)} %param.12) | copy-start | bytes 1572868
  7.7 3.3 %copy-start.7 = (bf16[3,128,128]{2,1,0:T(8,128)(2,1)S(1)}, bf16[3,128,128]{2,1,0:T(8,128)(2,1)}, u32[]{:S(2)}) copy-start(bf16[3,128,128]{2,1,0:T(8,128)(2,1)} %param.15) | copy-start | bytes 294916
  11.0 2.0 %copy-start.3 = (bf16[32,2,32,128]{3,0,2,1:T(8,128)(2,1)S(1)}, bf16[32,2,32,128]{3,0,2,1:T(8,128)(2,1)}, u32[]{:S(2)}) copy-start(bf16[32,2,32,128]{3,0,2,1:T(8,128)(2,1)} %copy-done.2) | copy-start | bytes 1572868
  15.1 1.0 copy-start.6
  15.9 4.2 %copy-start.4 = (bf16[2,32,32,128]{3,1,2,0:T(8,128)(2,1)}, bf16[2,32,32,128]{3,1,2,0:T(8,128)(2,1)S(1)}, u32[]{:S(2)}) copy-start(bf16[2,32,32,128]{3,1,2,0:T(8,128)(2,1)S(1)} %get-tuple-element.5) | copy-start | bytes 1572868
  21.5 10.0 %copy-start.10 = (s32[64]{0:T(128)S(1)}, s32[64]{0:T(128)}, u32[]{:S(2)}) copy-start(s32[64]{0:T(128)} %constant.73.clone) | copy-start | bytes 772
  22.0 14.1 %copy-start.9 = (s32[64]{0:T(128)S(1)}, s32[64]{0:T(128)}, u32[]{:S(2)}) copy-start(s32[64]{0:T(128)} %constant.74.clone) | copy-start | bytes 772
  22.0 10.8 %collective-permute-start.1 = (f32[800,128]{1,0:T(8,128)S(1)}, f32[800,128]{1,0:T(8,128)S(1)}, u32[]{:S(2)}, u32[]{:S(2)}) collective-permute-start(f32[800,128]{1,0:T(8,128)S(1)} %constant_dynamic-slice_fusion.2), channel_id=1, source_target_pairs={{0,8},{8,0},{16,24},{24,16},{32,40},{40,32},{48,56},{56,48},{64,72... | collective-permute-start | bytes 1228808 | tf_op jit(solution)/shard_map/ppermute | solution.py:92
  32.9 8.5 %collective-permute-start.2 = (f32[400,128]{1,0:T(8,128)S(1)}, f32[400,128]{1,0:T(8,128)S(1)}, u32[]{:S(2)}, u32[]{:S(2)}) collective-permute-start(f32[400,128]{1,0:T(8,128)S(1)} %constant_dynamic-slice_fusion.1), channel_id=1, source_target_pairs={{0,128},{8,136},{16,144},{24,152},{32,160},{40,168},{48,176},{56,1... | collective-permute-start | bytes 614408 | tf_op jit(solution)/shard_map/ppermute | solution.py:92
  41.5 6.6 %collective-permute-start.3 = (f32[200,128]{1,0:T(8,128)S(1)}, f32[200,128]{1,0:T(8,128)S(1)}, u32[]{:S(2)}, u32[]{:S(2)}) collective-permute-start(f32[200,128]{1,0:T(8,128)S(1)} %constant_dynamic-slice_fusion), channel_id=1, source_target_pairs={{0,384},{8,392},{16,400},{24,408},{32,416},{40,424},{48,432},{56,4... | collective-permute-start | bytes 307208 | tf_op jit(solution)/shard_map/ppermute | solution.py:92
  48.1 5.4 %collective-permute-start.4 = (f32[200,128]{1,0:T(8,128)S(1)}, f32[200,128]{1,0:T(8,128)S(1)}, u32[]{:S(2)}, u32[]{:S(2)}) collective-permute-start(f32[200,128]{1,0:T(8,128)S(1)} %dynamic-slice_add_fusion.2), channel_id=1, source_target_pairs={{0,32},{8,40},{16,48},{24,56},{32,0},{40,8},{48,16},{56,24},{64,96... | collective-permute-start | bytes 307208 | tf_op jit(solution)/shard_map/ppermute | solution.py:95
  53.5 67.2 %copy-start.5 = (bf16[2,32,32,128]{3,1,2,0:T(8,128)(2,1)S(1)}, bf16[2,32,32,128]{3,1,2,0:T(8,128)(2,1)}, u32[]{:S(2)}) copy-start(bf16[2,32,32,128]{3,1,2,0:T(8,128)(2,1)} %copy-done.4) | copy-start | bytes 1572868
  53.5 6.7 %collective-permute-start.5 = (f32[200,128]{1,0:T(8,128)S(1)}, f32[200,128]{1,0:T(8,128)S(1)}, u32[]{:S(2)}, u32[]{:S(2)}) collective-permute-start(f32[200,128]{1,0:T(8,128)S(1)} %add.119), channel_id=1, source_target_pairs={{0,96},{8,104},{16,112},{24,120},{32,64},{40,72},{48,80},{56,88},{... | collective-permute-start | bytes 307208 | tf_op jit(solution)/shard_map/ppermute | solution.py:95
  60.3 17.0 %collective-permute-start.6 = (f32[200,128]{1,0:T(8,128)S(1)}, f32[200,128]{1,0:T(8,128)S(1)}, u32[]{:S(2)}, u32[]{:S(2)}) collective-permute-start(f32[200,128]{1,0:T(8,128)S(1)} %add.120), channel_id=1, source_target_pairs={{0,16},{8,24},{16,0},{24,8},{32,48},{40,56},{48,32},{56,40},{64,80... | collective-permute-start | bytes 307208 | tf_op jit(solution)/shard_map/ppermute | solution.py:95
  77.3 6.9 %collective-permute-start.7 = (f32[200,128]{1,0:T(8,128)S(1)}, f32[200,128]{1,0:T(8,128)S(1)}, u32[]{:S(2)}, u32[]{:S(2)}) collective-permute-start(f32[200,128]{1,0:T(8,128)S(1)} %add.121), channel_id=1, source_target_pairs={{0,1},{1,0},{2,3},{3,2},{4,5},{5,4},{6,7},{7,6},{8,9},{9,8},{10,11... | collective-permute-start | bytes 307208 | tf_op jit(solution)/shard_map/ppermute | solution.py:95
  84.2 9.3 %collective-permute-start.8 = (f32[200,128]{1,0:T(8,128)S(1)}, f32[200,128]{1,0:T(8,128)S(1)}, u32[]{:S(2)}, u32[]{:S(2)}) collective-permute-start(f32[200,128]{1,0:T(8,128)S(1)} %add.122), channel_id=1, source_target_pairs={{0,2},{1,3},{2,0},{3,1},{4,6},{5,7},{6,4},{7,5},{8,10},{9,11},{10,... | collective-permute-start | bytes 307208 | tf_op jit(solution)/shard_map/ppermute | solution.py:95
  93.6 11.0 %collective-permute-start.9 = (f32[200,128]{1,0:T(8,128)S(1)}, f32[200,128]{1,0:T(8,128)S(1)}, u32[]{:S(2)}, u32[]{:S(2)}) collective-permute-start(f32[200,128]{1,0:T(8,128)S(1)} %add.123), channel_id=1, source_target_pairs={{0,4},{1,5},{2,6},{3,7},{4,0},{5,1},{6,2},{7,3},{8,12},{9,13},{10,... | collective-permute-start | bytes 307208 | tf_op jit(solution)/shard_map/ppermute | solution.py:95
  104.6 7.6 %collective-permute-start.10 = (f32[200,128]{1,0:T(8,128)S(1)}, f32[200,128]{1,0:T(8,128)S(1)}, u32[]{:S(2)}, u32[]{:S(2)}) collective-permute-start(f32[200,128]{1,0:T(8,128)S(1)} %add.124), channel_id=1, source_target_pairs={{0,384},{8,392},{16,400},{24,408},{32,416},{40,424},{48,432},{56,4... | collective-permute-start | bytes 307208 | tf_op jit(solution)/shard_map/ppermute | solution.py:98
  112.3 8.8 %collective-permute-start.11 = (f32[400,128]{1,0:T(8,128)S(1)}, f32[400,128]{1,0:T(8,128)S(1)}, u32[]{:S(2)}, u32[]{:S(2)}) collective-permute-start(f32[400,128]{1,0:T(8,128)S(1)} %get-tuple-element.15), channel_id=1, source_target_pairs={{0,128},{8,136},{16,144},{24,152},{32,160},{40,168},{48,176},{56,1... | collective-permute-start | bytes 614408 | tf_op jit(solution)/shard_map/ppermute | solution.py:98
  121.3 15.8 %collective-permute-start.12 = (f32[800,128]{1,0:T(8,128)S(1)}, f32[800,128]{1,0:T(8,128)S(1)}, u32[]{:S(2)}, u32[]{:S(2)}) collective-permute-start(f32[800,128]{1,0:T(8,128)S(1)} %get-tuple-element.11), channel_id=1, source_target_pairs={{0,8},{8,0},{16,24},{24,16},{32,40},{40,32},{48,56},{56,48},{64,72... | collective-permute-start | bytes 1228808 | tf_op jit(solution)/shard_map/ppermute | solution.py:98
  (2 other events, 1.3 us)

commit v3 on v2

--- a/solution.py
+++ b/solution.py
@@ -69,7 +69,7 @@
     for b in range(2):
         clip_step("x", n_x, 16, GRAY4, b, True)
     for b in range(2):
-        clip_step("y", 4, 4, GRAY4, b, False)
+        clip_step("y", 4, 4, GRAY4, b, True)
     clip_step("zh", 2, 2, (0, 1), 0, False)
     b = 0
     while (1 << b) < n_tm:

time: 140 us -> 150 us (1.071)
  between operations: 14.8 us -> 24.4 us
  waiting for transfers between devices: 28.1 us -> 19.7 us
  starting transfers between devices: 70.1 us -> 76.6 us
    ppermute x6 -> x4, waiting for transfers between devices: 21 us -> 7.42 us  [all_reduce(): x = x + lax.ppermute(x, axis, perm)]
    ppermute x6 -> x4, starting transfers between devices: 35.2 us -> 27.5 us  [all_reduce(): x = x + lax.ppermute(x, axis, perm)]
    ppermute x3 -> x5, starting transfers between devices: 18.4 us -> 26 us  [all_reduce(): other = lax.ppermute(x, axis, perm)]
    ppermute x3 -> x5, starting transfers between devices: 15 us -> 21.7 us  [all_reduce(): x = keep + lax.ppermute(send, axis, perm)]
    ppermute x3 -> x5, waiting for transfers between devices: 0.01 us -> 5.14 us  [all_reduce(): other = lax.ppermute(x, axis, perm)]
    dynamic_slice x3 -> x5, local copies, waits for them, and re-layouts: 1.76 us -> 3.07 us  [all_reduce(): bit = jnp.asarray(bits, jnp.int32)[lax.axis_index(axis)]]
    ppermute x3 -> x5, waiting for transfers between devices: 6.38 us -> 6.49 us  [all_reduce(): x = keep + lax.ppermute(send, axis, perm)]
    unnamed x28 -> x32, local copies, waits for them, and re-layouts: 3.29 us -> 3.3 us
  transfers between devices with their start and end apart: 13 -> 15, of which waited for: 9 -> 11; matrix products, arithmetic and copies ran while one was open for 9% -> 10% of each run, Pallas kernels for 0% -> 0%
where the time goes in v3:
time: 150 us; the launch traced here: 148 us
  starting transfers between devices  76.6 us (51%)
  between operations  24.4 us (16%)
  waiting for transfers between devices  19.7 us (13%)
  matrix products  12.7 us (8%)
  local copies, waits for them, and re-layouts  8.86 us (6%)
  other arithmetic  6.01 us (4%)
    ppermute x4, starting transfers between devices, all_reduce(): x = x + lax.ppermute(x, axis, perm)  27.5 us
    ppermute x5, starting transfers between devices, all_reduce(): other = lax.ppermute(x, axis, perm)  26 us
    ppermute x5, starting transfers between devices, all_reduce(): x = keep + lax.ppermute(send, axis, perm)  21.7 us
    ppermute x4, waiting for transfers between devices, all_reduce(): x = x + lax.ppermute(x, axis, perm)  7.42 us
    ppermute x5, waiting for transfers between devices, all_reduce(): x = keep + lax.ppermute(send, axis, perm)  6.49 us
    ppermute x5, waiting for transfers between devices, all_reduce(): other = lax.ppermute(x, axis, perm)  5.14 us
    transpose x1, matrix products, spatial_weight_grad(): return jnp.transpose(result, (1, 2, 0, 3))  3.98 us
    unnamed x32, local copies, waits for them, and re-layouts  3.3 us
  transfers between devices with their start and end apart: 15, of which 11 were waited for; matrix products, arithmetic and copies ran while one was open for 10% of the time, Pallas kernels for 0%

profile of v3, /device:TPU:1, one launch (start us, length us, event | category | flops | bytes accessed | tf_op | source)
XLA Modules:
  0.0 148.3 jit_solution(8152694388728399385)
XLA Ops:
  4.1 1.9 %multiply_convert_fusion = (bf16[32,16,5,128]{3,1,2,0:T(8,128)(2,1)S(1)}, f32[32,16,5,128]{3,1,2,0:T(8,128)S(1)}, f32[32,16,5,128]{3,1,2,0:T(8,128)S(1)}) fusion(f32[128]{0:T(128)S(1)} %copy-done.8, bf16[3,3,128,128]{3,2,1,0:T(8,128)(2,1)S(1)} %copy-done, bf16[32,2,8,7,128]{4,0,3,2,1:T(8,128)(2,1)S(1)} %fusion.12, pred[16,5]{0,1:T(8,128)(4,1)S(1)} %copy-done.14), kind=kOutput, calls=%fused_computation.11 | convolution fusion | flops 742522880 | bytes 4489808 | tf_op jit(solution)/shard_map/conv_general_dilated | solution.py:13
  16.1 4.0 %fusion.22 = f32[3,3,128,128]{3,2,1,0:T(8,128)S(1)} fusion(bf16[2,32,32,128]{3,2,1,0:T(8,128)(2,1)S(1)} %bitcast.170, bf16[2,32,32,128]{3,1,2,0:T(8,128)(2,1)S(1)} %get-tuple-element.5), kind=kOutput, calls=%fused_computation.44 | convolution fusion | flops 579076096 | bytes 1638400 | tf_op jit(solution)/shard_map/transpose | solution.py:33
  22.0 8.9 %collective-permute-start.1 = (f32[800,128]{1,0:T(8,128)S(1)}, f32[800,128]{1,0:T(8,128)S(1)}, u32[]{:S(2)}, u32[]{:S(2)}) collective-permute-start(f32[800,128]{1,0:T(8,128)S(1)} %constant_dynamic-slice_fusion.4), channel_id=1, source_target_pairs={{0,8},{8,0},{16,24},{24,16},{32,40},{40,32},{48,56},{56,48},{64,72... | collective-permute-start | bytes 1228808 | tf_op jit(solution)/shard_map/ppermute | solution.py:92
  32.9 2.5 %collective-permute-start.2 = (f32[400,128]{1,0:T(8,128)S(1)}, f32[400,128]{1,0:T(8,128)S(1)}, u32[]{:S(2)}, u32[]{:S(2)}) collective-permute-start(f32[400,128]{1,0:T(8,128)S(1)} %constant_dynamic-slice_fusion.3), channel_id=1, source_target_pairs={{0,128},{8,136},{16,144},{24,152},{32,160},{40,168},{48,176},{56,1... | collective-permute-start | bytes 614408 | tf_op jit(solution)/shard_map/ppermute | solution.py:92
  37.3 4.1 %collective-permute-done.2 = f32[400,128]{1,0:T(8,128)S(1)} collective-permute-done((f32[400,128]{1,0:T(8,128)S(1)}, f32[400,128]{1,0:T(8,128)S(1)}, u32[]{:S(2)}, u32[]{:S(2)}) %collective-permute-start.2) | collective-permute-done | bytes 204832 | tf_op jit(solution)/shard_map/ppermute | solution.py:92
  41.5 3.7 %collective-permute-start.3 = (f32[200,128]{1,0:T(8,128)S(1)}, f32[200,128]{1,0:T(8,128)S(1)}, u32[]{:S(2)}, u32[]{:S(2)}) collective-permute-start(f32[200,128]{1,0:T(8,128)S(1)} %constant_dynamic-slice_fusion.2), channel_id=1, source_target_pairs={{0,384},{8,392},{16,400},{24,408},{32,416},{40,424},{48,432},{56,4... | collective-permute-start | bytes 307208 | tf_op jit(solution)/shard_map/ppermute | solution.py:92
  48.2 2.5 %collective-permute-start.4 = (f32[100,128]{1,0:T(8,128)S(1)}, f32[100,128]{1,0:T(8,128)S(1)}, u32[]{:S(2)}, u32[]{:S(2)}) collective-permute-start(f32[100,128]{1,0:T(8,128)S(1)} %constant_dynamic-slice_fusion.1), channel_id=1, source_target_pairs={{0,32},{8,40},{16,48},{24,56},{32,0},{40,8},{48,16},{56,24},{64,96... | collective-permute-start | bytes 153608 | tf_op jit(solution)/shard_map/ppermute | solution.py:92
  53.1 4.1 %collective-permute-start.5 = (f32[50,128]{1,0:T(8,128)S(1)}, f32[50,128]{1,0:T(8,128)S(1)}, u32[]{:S(2)}, u32[]{:S(2)}) collective-permute-start(f32[50,128]{1,0:T(8,128)S(1)} %constant_dynamic-slice_fusion), channel_id=1, source_target_pairs={{0,96},{8,104},{16,112},{24,120},{32,64},{40,72},{48,80},{56,88},{... | collective-permute-start | bytes 76808 | tf_op jit(solution)/shard_map/ppermute | solution.py:92
  59.1 15.0 %collective-permute-start.6 = (f32[50,128]{1,0:T(8,128)S(1)}, f32[50,128]{1,0:T(8,128)S(1)}, u32[]{:S(2)}, u32[]{:S(2)}) collective-permute-start(f32[50,128]{1,0:T(8,128)S(1)} %dynamic-slice_add_fusion.4), channel_id=1, source_target_pairs={{0,16},{8,24},{16,0},{24,8},{32,48},{40,56},{48,32},{56,40},{64,80... | collective-permute-start | bytes 76808 | tf_op jit(solution)/shard_map/ppermute | solution.py:95
  75.3 2.6 %collective-permute-start.7 = (f32[50,128]{1,0:T(8,128)S(1)}, f32[50,128]{1,0:T(8,128)S(1)}, u32[]{:S(2)}, u32[]{:S(2)}) collective-permute-start(f32[50,128]{1,0:T(8,128)S(1)} %add.157), channel_id=1, source_target_pairs={{0,1},{1,0},{2,3},{3,2},{4,5},{5,4},{6,7},{7,6},{8,9},{9,8},{10,11... | collective-permute-start | bytes 76808 | tf_op jit(solution)/shard_map/ppermute | solution.py:95
  77.9 2.0 %collective-permute-done.7 = f32[50,128]{1,0:T(8,128)S(1)} collective-permute-done((f32[50,128]{1,0:T(8,128)S(1)}, f32[50,128]{1,0:T(8,128)S(1)}, u32[]{:S(2)}, u32[]{:S(2)}) %collective-permute-start.7) | collective-permute-done | bytes 25632 | tf_op jit(solution)/shard_map/ppermute | solution.py:95
  79.9 3.7 %collective-permute-start.8 = (f32[50,128]{1,0:T(8,128)S(1)}, f32[50,128]{1,0:T(8,128)S(1)}, u32[]{:S(2)}, u32[]{:S(2)}) collective-permute-start(f32[50,128]{1,0:T(8,128)S(1)} %add.158), channel_id=1, source_target_pairs={{0,2},{1,3},{2,0},{3,1},{4,6},{5,7},{6,4},{7,5},{8,10},{9,11},{10,... | collective-permute-start | bytes 76808 | tf_op jit(solution)/shard_map/ppermute | solution.py:95
  83.6 1.9 %collective-permute-done.8 = f32[50,128]{1,0:T(8,128)S(1)} collective-permute-done((f32[50,128]{1,0:T(8,128)S(1)}, f32[50,128]{1,0:T(8,128)S(1)}, u32[]{:S(2)}, u32[]{:S(2)}) %collective-permute-start.8) | collective-permute-done | bytes 25632 | tf_op jit(solution)/shard_map/ppermute | solution.py:95
  85.5 6.2 %collective-permute-start.9 = (f32[50,128]{1,0:T(8,128)S(1)}, f32[50,128]{1,0:T(8,128)S(1)}, u32[]{:S(2)}, u32[]{:S(2)}) collective-permute-start(f32[50,128]{1,0:T(8,128)S(1)} %add.159), channel_id=1, source_target_pairs={{0,4},{1,5},{2,6},{3,7},{4,0},{5,1},{6,2},{7,3},{8,12},{9,13},{10,... | collective-permute-start | bytes 76808 | tf_op jit(solution)/shard_map/ppermute | solution.py:95
  91.7 2.3 %collective-permute-done.9 = f32[50,128]{1,0:T(8,128)S(1)} collective-permute-done((f32[50,128]{1,0:T(8,128)S(1)}, f32[50,128]{1,0:T(8,128)S(1)}, u32[]{:S(2)}, u32[]{:S(2)}) %collective-permute-start.9) | collective-permute-done | bytes 25632 | tf_op jit(solution)/shard_map/ppermute | solution.py:95
  94.0 4.5 %collective-permute-start.10 = (f32[50,128]{1,0:T(8,128)S(1)}, f32[50,128]{1,0:T(8,128)S(1)}, u32[]{:S(2)}, u32[]{:S(2)}) collective-permute-start(f32[50,128]{1,0:T(8,128)S(1)} %add.160), channel_id=1, source_target_pairs={{0,96},{8,104},{16,112},{24,120},{32,64},{40,72},{48,80},{56,88},{... | collective-permute-start | bytes 76808 | tf_op jit(solution)/shard_map/ppermute | solution.py:98
  108.5 1.9 %collective-permute-start.11 = (f32[100,128]{1,0:T(8,128)S(1)}, f32[100,128]{1,0:T(8,128)S(1)}, u32[]{:S(2)}, u32[]{:S(2)}) collective-permute-start(f32[100,128]{1,0:T(8,128)S(1)} %pad_maximum_fusion.6), channel_id=1, source_target_pairs={{0,32},{8,40},{16,48},{24,56},{32,0},{40,8},{48,16},{56,24},{64,96... | collective-permute-start | bytes 153608 | tf_op jit(solution)/shard_map/ppermute | solution.py:98
  110.5 2.9 %collective-permute-done.11 = f32[100,128]{1,0:T(8,128)S(1)} collective-permute-done((f32[100,128]{1,0:T(8,128)S(1)}, f32[100,128]{1,0:T(8,128)S(1)}, u32[]{:S(2)}, u32[]{:S(2)}) %collective-permute-start.11) | collective-permute-done | bytes 51232 | tf_op jit(solution)/shard_map/ppermute | solution.py:98
  113.4 4.4 %collective-permute-start.12 = (f32[200,128]{1,0:T(8,128)S(1)}, f32[200,128]{1,0:T(8,128)S(1)}, u32[]{:S(2)}, u32[]{:S(2)}) collective-permute-start(f32[200,128]{1,0:T(8,128)S(1)} %pad_maximum_fusion.5), channel_id=1, source_target_pairs={{0,384},{8,392},{16,400},{24,408},{32,416},{40,424},{48,432},{56,4... | collective-permute-start | bytes 307208 | tf_op jit(solution)/shard_map/ppermute | solution.py:98
  117.9 2.2 %collective-permute-done.12 = f32[200,128]{1,0:T(8,128)S(1)} collective-permute-done((f32[200,128]{1,0:T(8,128)S(1)}, f32[200,128]{1,0:T(8,128)S(1)}, u32[]{:S(2)}, u32[]{:S(2)}) %collective-permute-start.12) | collective-permute-done | bytes 102432 | tf_op jit(solution)/shard_map/ppermute | solution.py:98
  120.1 2.1 %collective-permute-start.13 = (f32[400,128]{1,0:T(8,128)S(1)}, f32[400,128]{1,0:T(8,128)S(1)}, u32[]{:S(2)}, u32[]{:S(2)}) collective-permute-start(f32[400,128]{1,0:T(8,128)S(1)} %get-tuple-element.15), channel_id=1, source_target_pairs={{0,128},{8,136},{16,144},{24,152},{32,160},{40,168},{48,176},{56,1... | collective-permute-start | bytes 614408 | tf_op jit(solution)/shard_map/ppermute | solution.py:98
  129.3 13.1 %collective-permute-start.14 = (f32[800,128]{1,0:T(8,128)S(1)}, f32[800,128]{1,0:T(8,128)S(1)}, u32[]{:S(2)}, u32[]{:S(2)}) collective-permute-start(f32[800,128]{1,0:T(8,128)S(1)} %get-tuple-element.11), channel_id=1, source_target_pairs={{0,8},{8,0},{16,24},{24,16},{32,40},{40,32},{48,56},{56,48},{64,72... | collective-permute-start | bytes 1228808 | tf_op jit(solution)/shard_map/ppermute | solution.py:98
  142.5 1.7 %convolution_select_fusion = f32[32,16,5,128]{3,1,2,0:T(8,128)S(1)} fusion(bf16[3,3,128,128]{3,2,1,0:T(8,128)(2,1)S(1)} %copy-done, bf16[32,2,7,2,128]{4,2,1,3,0:T(8,128)(2,1)S(1)} %slice.39, bf16[32,2,8,5,128]{4,2,1,3,0:T(8,128)(2,1)S(1)} %copy.31, pred[16,5]{0,1:T(8,128)(4,1)S(1)} %copy-done.14), kind=kOutput, calls=%fused_computation.7 | convolution fusion | flops 742326272 | bytes 2490448 | tf_op jit(solution)/shard_map/conv_general_dilated | solution.py:22
  144.7 1.4 fusion.19
  (98 shorter events, 24.3 us)
Async XLA Ops:
  0.6 2.9 %copy-start = (bf16[3,3,128,128]{3,2,1,0:T(8,128)(2,1)S(1)}, bf16[3,3,128,128]{3,2,1,0:T(8,128)(2,1)}, u32[]{:S(2)}) copy-start(bf16[3,3,128,128]{3,2,1,0:T(8,128)(2,1)} %param.17) | copy-start | bytes 884740
  0.6 11.4 %collective-permute-start = (bf16[2,32,32,128]{3,2,1,0:T(8,128)(2,1)}, bf16[2,32,32,128]{3,2,1,0:T(8,128)(2,1)}, u32[]{:S(2)}, u32[]{:S(2)}) collective-permute-start(bf16[2,32,32,128]{3,2,1,0:T(8,128)(2,1)} %bitcast.151), channel_id=1, source_target_pairs={{1,0},{2,1},{3,2},{4,3},{5,4},{6,5},{7,6},{9,8},{10,9},{11,10},{12... | collective-permute-start | bytes 1572872 | tf_op jit(solution)/shard_map/ppermute | solution.py:112
  7.7 3.3 %copy-start.7 = (bf16[3,128,128]{2,1,0:T(8,128)(2,1)S(1)}, bf16[3,128,128]{2,1,0:T(8,128)(2,1)}, u32[]{:S(2)}) copy-start(bf16[3,128,128]{2,1,0:T(8,128)(2,1)} %param.19) | copy-start | bytes 294916
  11.0 2.0 %copy-start.3 = (bf16[32,2,32,128]{3,0,2,1:T(8,128)(2,1)S(1)}, bf16[32,2,32,128]{3,0,2,1:T(8,128)(2,1)}, u32[]{:S(2)}) copy-start(bf16[32,2,32,128]{3,0,2,1:T(8,128)(2,1)} %copy-done.2) | copy-start | bytes 1572868
  15.9 4.2 %copy-start.4 = (bf16[2,32,32,128]{3,1,2,0:T(8,128)(2,1)}, bf16[2,32,32,128]{3,1,2,0:T(8,128)(2,1)S(1)}, u32[]{:S(2)}) copy-start(bf16[2,32,32,128]{3,1,2,0:T(8,128)(2,1)S(1)} %get-tuple-element.5) | copy-start | bytes 1572868
  21.5 10.0 %copy-start.12 = (s32[64]{0:T(128)S(1)}, s32[64]{0:T(128)}, u32[]{:S(2)}) copy-start(s32[64]{0:T(128)} %constant.103.clone) | copy-start | bytes 772
  22.0 14.1 %copy-start.11 = (s32[64]{0:T(128)S(1)}, s32[64]{0:T(128)}, u32[]{:S(2)}) copy-start(s32[64]{0:T(128)} %constant.104.clone) | copy-start | bytes 772
  22.0 23.9 %copy-start.10 = (s32[64]{0:T(128)S(1)}, s32[64]{0:T(128)}, u32[]{:S(2)}) copy-start(s32[64]{0:T(128)} %constant.105.clone) | copy-start | bytes 772
  22.0 10.8 %collective-permute-start.1 = (f32[800,128]{1,0:T(8,128)S(1)}, f32[800,128]{1,0:T(8,128)S(1)}, u32[]{:S(2)}, u32[]{:S(2)}) collective-permute-start(f32[800,128]{1,0:T(8,128)S(1)} %constant_dynamic-slice_fusion.4), channel_id=1, source_target_pairs={{0,8},{8,0},{16,24},{24,16},{32,40},{40,32},{48,56},{56,48},{64,72... | collective-permute-start | bytes 1228808 | tf_op jit(solution)/shard_map/ppermute | solution.py:92
  32.8 18.5 %copy-start.9 = (s32[64]{0:T(128)S(1)}, s32[64]{0:T(128)}, u32[]{:S(2)}) copy-start(s32[64]{0:T(128)} %constant.106.clone) | copy-start | bytes 772
  32.9 8.5 %collective-permute-start.2 = (f32[400,128]{1,0:T(8,128)S(1)}, f32[400,128]{1,0:T(8,128)S(1)}, u32[]{:S(2)}, u32[]{:S(2)}) collective-permute-start(f32[400,128]{1,0:T(8,128)S(1)} %constant_dynamic-slice_fusion.3), channel_id=1, source_target_pairs={{0,128},{8,136},{16,144},{24,152},{32,160},{40,168},{48,176},{56,1... | collective-permute-start | bytes 614408 | tf_op jit(solution)/shard_map/ppermute | solution.py:92
  41.5 6.6 %collective-permute-start.3 = (f32[200,128]{1,0:T(8,128)S(1)}, f32[200,128]{1,0:T(8,128)S(1)}, u32[]{:S(2)}, u32[]{:S(2)}) collective-permute-start(f32[200,128]{1,0:T(8,128)S(1)} %constant_dynamic-slice_fusion.2), channel_id=1, source_target_pairs={{0,384},{8,392},{16,400},{24,408},{32,416},{40,424},{48,432},{56,4... | collective-permute-start | bytes 307208 | tf_op jit(solution)/shard_map/ppermute | solution.py:92
  48.2 4.9 %collective-permute-start.4 = (f32[100,128]{1,0:T(8,128)S(1)}, f32[100,128]{1,0:T(8,128)S(1)}, u32[]{:S(2)}, u32[]{:S(2)}) collective-permute-start(f32[100,128]{1,0:T(8,128)S(1)} %constant_dynamic-slice_fusion.1), channel_id=1, source_target_pairs={{0,32},{8,40},{16,48},{24,56},{32,0},{40,8},{48,16},{56,24},{64,96... | collective-permute-start | bytes 153608 | tf_op jit(solution)/shard_map/ppermute | solution.py:92
  53.0 75.7 %copy-start.5 = (bf16[2,32,32,128]{3,1,2,0:T(8,128)(2,1)S(1)}, bf16[2,32,32,128]{3,1,2,0:T(8,128)(2,1)}, u32[]{:S(2)}) copy-start(bf16[2,32,32,128]{3,1,2,0:T(8,128)(2,1)} %copy-done.4) | copy-start | bytes 1572868
  53.1 6.0 %collective-permute-start.5 = (f32[50,128]{1,0:T(8,128)S(1)}, f32[50,128]{1,0:T(8,128)S(1)}, u32[]{:S(2)}, u32[]{:S(2)}) collective-permute-start(f32[50,128]{1,0:T(8,128)S(1)} %constant_dynamic-slice_fusion), channel_id=1, source_target_pairs={{0,96},{8,104},{16,112},{24,120},{32,64},{40,72},{48,80},{56,88},{... | collective-permute-start | bytes 76808 | tf_op jit(solution)/shard_map/ppermute | solution.py:92
  59.1 16.2 %collective-permute-start.6 = (f32[50,128]{1,0:T(8,128)S(1)}, f32[50,128]{1,0:T(8,128)S(1)}, u32[]{:S(2)}, u32[]{:S(2)}) collective-permute-start(f32[50,128]{1,0:T(8,128)S(1)} %dynamic-slice_add_fusion.4), channel_id=1, source_target_pairs={{0,16},{8,24},{16,0},{24,8},{32,48},{40,56},{48,32},{56,40},{64,80... | collective-permute-start | bytes 76808 | tf_op jit(solution)/shard_map/ppermute | solution.py:95
  75.3 4.6 %collective-permute-start.7 = (f32[50,128]{1,0:T(8,128)S(1)}, f32[50,128]{1,0:T(8,128)S(1)}, u32[]{:S(2)}, u32[]{:S(2)}) collective-permute-start(f32[50,128]{1,0:T(8,128)S(1)} %add.157), channel_id=1, source_target_pairs={{0,1},{1,0},{2,3},{3,2},{4,5},{5,4},{6,7},{7,6},{8,9},{9,8},{10,11... | collective-permute-start | bytes 76808 | tf_op jit(solution)/shard_map/ppermute | solution.py:95
  79.9 5.6 %collective-permute-start.8 = (f32[50,128]{1,0:T(8,128)S(1)}, f32[50,128]{1,0:T(8,128)S(1)}, u32[]{:S(2)}, u32[]{:S(2)}) collective-permute-start(f32[50,128]{1,0:T(8,128)S(1)} %add.158), channel_id=1, source_target_pairs={{0,2},{1,3},{2,0},{3,1},{4,6},{5,7},{6,4},{7,5},{8,10},{9,11},{10,... | collective-permute-start | bytes 76808 | tf_op jit(solution)/shard_map/ppermute | solution.py:95
  85.5 8.5 %collective-permute-start.9 = (f32[50,128]{1,0:T(8,128)S(1)}, f32[50,128]{1,0:T(8,128)S(1)}, u32[]{:S(2)}, u32[]{:S(2)}) collective-permute-start(f32[50,128]{1,0:T(8,128)S(1)} %add.159), channel_id=1, source_target_pairs={{0,4},{1,5},{2,6},{3,7},{4,0},{5,1},{6,2},{7,3},{8,12},{9,13},{10,... | collective-permute-start | bytes 76808 | tf_op jit(solution)/shard_map/ppermute | solution.py:95
  94.0 14.5 %collective-permute-start.10 = (f32[50,128]{1,0:T(8,128)S(1)}, f32[50,128]{1,0:T(8,128)S(1)}, u32[]{:S(2)}, u32[]{:S(2)}) collective-permute-start(f32[50,128]{1,0:T(8,128)S(1)} %add.160), channel_id=1, source_target_pairs={{0,96},{8,104},{16,112},{24,120},{32,64},{40,72},{48,80},{56,88},{... | collective-permute-start | bytes 76808 | tf_op jit(solution)/shard_map/ppermute | solution.py:98
  108.5 4.9 %collective-permute-start.11 = (f32[100,128]{1,0:T(8,128)S(1)}, f32[100,128]{1,0:T(8,128)S(1)}, u32[]{:S(2)}, u32[]{:S(2)}) collective-permute-start(f32[100,128]{1,0:T(8,128)S(1)} %pad_maximum_fusion.6), channel_id=1, source_target_pairs={{0,32},{8,40},{16,48},{24,56},{32,0},{40,8},{48,16},{56,24},{64,96... | collective-permute-start | bytes 153608 | tf_op jit(solution)/shard_map/ppermute | solution.py:98
  113.4 6.6 %collective-permute-start.12 = (f32[200,128]{1,0:T(8,128)S(1)}, f32[200,128]{1,0:T(8,128)S(1)}, u32[]{:S(2)}, u32[]{:S(2)}) collective-permute-start(f32[200,128]{1,0:T(8,128)S(1)} %pad_maximum_fusion.5), channel_id=1, source_target_pairs={{0,384},{8,392},{16,400},{24,408},{32,416},{40,424},{48,432},{56,4... | collective-permute-start | bytes 307208 | tf_op jit(solution)/shard_map/ppermute | solution.py:98
  120.1 9.0 %collective-permute-start.13 = (f32[400,128]{1,0:T(8,128)S(1)}, f32[400,128]{1,0:T(8,128)S(1)}, u32[]{:S(2)}, u32[]{:S(2)}) collective-permute-start(f32[400,128]{1,0:T(8,128)S(1)} %get-tuple-element.15), channel_id=1, source_target_pairs={{0,128},{8,136},{16,144},{24,152},{32,160},{40,168},{48,176},{56,1... | collective-permute-start | bytes 614408 | tf_op jit(solution)/shard_map/ppermute | solution.py:98
  129.3 16.8 %collective-permute-start.14 = (f32[800,128]{1,0:T(8,128)S(1)}, f32[800,128]{1,0:T(8,128)S(1)}, u32[]{:S(2)}, u32[]{:S(2)}) collective-permute-start(f32[800,128]{1,0:T(8,128)S(1)} %get-tuple-element.11), channel_id=1, source_target_pairs={{0,8},{8,0},{16,24},{24,16},{32,40},{40,32},{48,56},{56,48},{64,72... | collective-permute-start | bytes 1228808 | tf_op jit(solution)/shard_map/ppermute | solution.py:98
  (6 other events, 6.0 us)

commit v4 on v3

--- a/solution.py
+++ b/solution.py
@@ -50,11 +50,14 @@
     return grad_act, jnp.stack(lag_terms)
 
 
+ZRING = (2, 0, 8, 11, 3, 1, 9, 15, 7, 13, 5, 14, 6, 12, 4, 10)
+
+
 def butterfly_steps(n_clip, n_tm):
     n_x = n_clip // 16
     steps = []
 
-    def clip_step(field, size, stride, labels, bit, halve):
+    def clip_step(size, stride, labels, bit, kind):
         perm, bits = [], []
         pos = {lab: r for r, lab in enumerate(labels)}
         for c in range(n_clip):
@@ -63,28 +66,31 @@
             r2 = pos[lab ^ (1 << bit)]
             perm.append((c, c + (r2 - r) * stride))
             bits.append((lab >> bit) & 1)
-        steps.append(("clip", tuple(perm), tuple(bits), halve))
+        steps.append(("clip", tuple(perm), tuple(bits), kind))
 
-    clip_step("core", 2, 1, (0, 1), 0, True)
+    clip_step(2, 1, (0, 1), 0, "halve")
     for b in range(2):
-        clip_step("x", n_x, 16, GRAY4, b, True)
+        clip_step(n_x, 16, GRAY4, b, "halve")
     for b in range(2):
-        clip_step("y", 4, 4, GRAY4, b, True)
-    clip_step("zh", 2, 2, (0, 1), 0, False)
-    b = 0
-    while (1 << b) < n_tm:
-        perm = tuple((t, t ^ (1 << b)) for t in range(n_tm))
-        bits = tuple((t >> b) & 1 for t in range(n_tm))
-        steps.append(("tm", perm, bits, False))
-        b += 1
+        clip_step(4, 4, GRAY4, b, "add")
+    pos = {lab: p for p, lab in enumerate(ZRING)}
+    for b in range(4):
+        perm = []
+        for c in range(n_clip):
+            zh = (c // 2) % 2
+            for t in range(n_tm):
+                p2 = pos[ZRING[zh * n_tm + t] ^ (1 << b)]
+                c2 = c + (p2 // n_tm - zh) * 2
+                perm.append((c * n_tm + t, c2 * n_tm + p2 % n_tm))
+        steps.append((("clip", "tm"), tuple(perm), None, "add"))
     return steps
 
 
 def all_reduce(x, n_clip, n_tm):
     steps = butterfly_steps(n_clip, n_tm)
     halved = []
-    for axis, perm, bits, halve in steps:
-        if halve:
+    for axis, perm, bits, kind in steps:
+        if kind == "halve":
             bit = jnp.asarray(bits, jnp.int32)[lax.axis_index(axis)]
             h = x.shape[0] // 2
             keep = lax.dynamic_slice_in_dim(x, bit * h, h)

time: 150 us -> 135 us (0.900)
  the two profiles are of different devices: /device:TPU:1 before, /device:TPU:29 now
where the time goes in v4:
time: 135 us; the launch traced here: 134 us
  starting transfers between devices  63.5 us (47%)
  waiting for transfers between devices  29.4 us (22%)
  between operations  14.8 us (11%)
  matrix products  12.7 us (9%)
  local copies, waits for them, and re-layouts  7.5 us (6%)
  other arithmetic  5.95 us (4%)
    ppermute x6, starting transfers between devices, all_reduce(): x = x + lax.ppermute(x, axis, perm)  36.3 us
    ppermute x6, waiting for transfers between devices, all_reduce(): x = x + lax.ppermute(x, axis, perm)  17.9 us
    ppermute x3, starting transfers between devices, all_reduce(): other = lax.ppermute(x, axis, perm)  17.5 us
    ppermute x3, starting transfers between devices, all_reduce(): x = keep + lax.ppermute(send, axis, perm)  8.23 us
    ppermute x3, waiting for transfers between devices, all_reduce(): x = keep + lax.ppermute(send, axis, perm)  6.36 us
    ppermute x1, waiting for transfers between devices, local(): after = lax.ppermute(cot, 'tm', [(t, t - 1) for t in range(1, n_tm)])  4.84 us
    transpose x1, matrix products, spatial_weight_grad(): return jnp.transpose(result, (1, 2, 0, 3))  3.98 us
    unnamed x28, local copies, waits for them, and re-layouts  3.29 us
  transfers between devices with their start and end apart: 13, of which 10 were waited for; matrix products, arithmetic and copies ran while one was open for 10% of the time, Pallas kernels for 0%

profile of v4, /device:TPU:29, one launch (start us, length us, event | category | flops | bytes accessed | tf_op | source)
XLA Modules:
  0.0 133.9 jit_solution(7380789332894091952)
XLA Ops:
  4.1 1.9 %multiply_convert_fusion = (bf16[32,16,5,128]{3,1,2,0:T(8,128)(2,1)S(1)}, f32[32,16,5,128]{3,1,2,0:T(8,128)S(1)}, f32[32,16,5,128]{3,1,2,0:T(8,128)S(1)}) fusion(f32[128]{0:T(128)S(1)} %copy-done.8, bf16[3,3,128,128]{3,2,1,0:T(8,128)(2,1)S(1)} %copy-done, bf16[32,2,8,7,128]{4,0,3,2,1:T(8,128)(2,1)S(1)} %fusion.12, pred[16,5]{0,1:T(8,128)(4,1)S(1)} %copy-done.12), kind=kOutput, calls=%fused_computation.11 | convolution fusion | flops 742522880 | bytes 4489808 | tf_op jit(solution)/shard_map/conv_general_dilated | solution.py:13
  11.3 4.8 %collective-permute-done = bf16[2,32,32,128]{3,2,1,0:T(8,128)(2,1)} collective-permute-done((bf16[2,32,32,128]{3,2,1,0:T(8,128)(2,1)}, bf16[2,32,32,128]{3,2,1,0:T(8,128)(2,1)}, u32[]{:S(2)}, u32[]{:S(2)}) %collective-permute-start) | collective-permute-done | bytes 524320 | tf_op jit(solution)/shard_map/ppermute | solution.py:118
  20.2 4.0 %fusion.22 = f32[3,3,128,128]{3,2,1,0:T(8,128)S(1)} fusion(bf16[2,32,32,128]{3,2,1,0:T(8,128)(2,1)S(1)} %bitcast.150, bf16[2,32,32,128]{3,1,2,0:T(8,128)(2,1)S(1)} %get-tuple-element.5), kind=kOutput, calls=%fused_computation.44 | convolution fusion | flops 579076096 | bytes 1638400 | tf_op jit(solution)/shard_map/transpose | solution.py:33
  26.1 3.3 %collective-permute-start.1 = (f32[800,128]{1,0:T(8,128)S(1)}, f32[800,128]{1,0:T(8,128)S(1)}, u32[]{:S(2)}, u32[]{:S(2)}) collective-permute-start(f32[800,128]{1,0:T(8,128)S(1)} %constant_dynamic-slice_fusion.2), channel_id=1, source_target_pairs={{0,8},{8,0},{16,24},{24,16},{32,40},{40,32},{48,56},{56,48},{64,72... | collective-permute-start | bytes 1228808 | tf_op jit(solution)/shard_map/ppermute | solution.py:98
  31.4 2.8 %collective-permute-start.2 = (f32[400,128]{1,0:T(8,128)S(1)}, f32[400,128]{1,0:T(8,128)S(1)}, u32[]{:S(2)}, u32[]{:S(2)}) collective-permute-start(f32[400,128]{1,0:T(8,128)S(1)} %constant_dynamic-slice_fusion.1), channel_id=1, source_target_pairs={{0,128},{8,136},{16,144},{24,152},{32,160},{40,168},{48,176},{56,1... | collective-permute-start | bytes 614408 | tf_op jit(solution)/shard_map/ppermute | solution.py:98
  36.2 3.8 %collective-permute-done.2 = f32[400,128]{1,0:T(8,128)S(1)} collective-permute-done((f32[400,128]{1,0:T(8,128)S(1)}, f32[400,128]{1,0:T(8,128)S(1)}, u32[]{:S(2)}, u32[]{:S(2)}) %collective-permute-start.2) | collective-permute-done | bytes 204832 | tf_op jit(solution)/shard_map/ppermute | solution.py:98
  40.0 2.2 %collective-permute-start.3 = (f32[200,128]{1,0:T(8,128)S(1)}, f32[200,128]{1,0:T(8,128)S(1)}, u32[]{:S(2)}, u32[]{:S(2)}) collective-permute-start(f32[200,128]{1,0:T(8,128)S(1)} %constant_dynamic-slice_fusion), channel_id=1, source_target_pairs={{0,384},{8,392},{16,400},{24,408},{32,416},{40,424},{48,432},{56,4... | collective-permute-start | bytes 307208 | tf_op jit(solution)/shard_map/ppermute | solution.py:98
  42.8 2.6 %collective-permute-done.3 = f32[200,128]{1,0:T(8,128)S(1)} collective-permute-done((f32[200,128]{1,0:T(8,128)S(1)}, f32[200,128]{1,0:T(8,128)S(1)}, u32[]{:S(2)}, u32[]{:S(2)}) %collective-permute-start.3) | collective-permute-done | bytes 102432 | tf_op jit(solution)/shard_map/ppermute | solution.py:98
  45.4 2.4 %collective-permute-start.4 = (f32[200,128]{1,0:T(8,128)S(1)}, f32[200,128]{1,0:T(8,128)S(1)}, u32[]{:S(2)}, u32[]{:S(2)}) collective-permute-start(f32[200,128]{1,0:T(8,128)S(1)} %dynamic-slice_add_fusion.2), channel_id=1, source_target_pairs={{0,32},{8,40},{16,48},{24,56},{32,0},{40,8},{48,16},{56,24},{64,96... | collective-permute-start | bytes 307208 | tf_op jit(solution)/shard_map/ppermute | solution.py:101
  47.8 3.0 %collective-permute-done.4 = f32[200,128]{1,0:T(8,128)S(1)} collective-permute-done((f32[200,128]{1,0:T(8,128)S(1)}, f32[200,128]{1,0:T(8,128)S(1)}, u32[]{:S(2)}, u32[]{:S(2)}) %collective-permute-start.4) | collective-permute-done | bytes 102432 | tf_op jit(solution)/shard_map/ppermute | solution.py:101
  50.8 2.1 %collective-permute-start.5 = (f32[200,128]{1,0:T(8,128)S(1)}, f32[200,128]{1,0:T(8,128)S(1)}, u32[]{:S(2)}, u32[]{:S(2)}) collective-permute-start(f32[200,128]{1,0:T(8,128)S(1)} %add.119), channel_id=1, source_target_pairs={{0,96},{8,104},{16,112},{24,120},{32,64},{40,72},{48,80},{56,88},{... | collective-permute-start | bytes 307208 | tf_op jit(solution)/shard_map/ppermute | solution.py:101
  52.9 4.7 %collective-permute-done.5 = f32[200,128]{1,0:T(8,128)S(1)} collective-permute-done((f32[200,128]{1,0:T(8,128)S(1)}, f32[200,128]{1,0:T(8,128)S(1)}, u32[]{:S(2)}, u32[]{:S(2)}) %collective-permute-start.5) | collective-permute-done | bytes 102432 | tf_op jit(solution)/shard_map/ppermute | solution.py:101
  57.6 8.8 %collective-permute-start.6 = (f32[200,128]{1,0:T(8,128)S(1)}, f32[200,128]{1,0:T(8,128)S(1)}, u32[]{:S(2)}, u32[]{:S(2)}) collective-permute-start(f32[200,128]{1,0:T(8,128)S(1)} %add.120), channel_id=1, source_target_pairs={{0,4},{1,5},{2,6},{3,23},{4,0},{5,1},{6,2},{7,19},{8,12},{9,13},{1... | collective-permute-start | bytes 307208 | tf_op jit(solution)/shard_map/ppermute | solution.py:101
  66.4 2.7 %collective-permute-done.6 = f32[200,128]{1,0:T(8,128)S(1)} collective-permute-done((f32[200,128]{1,0:T(8,128)S(1)}, f32[200,128]{1,0:T(8,128)S(1)}, u32[]{:S(2)}, u32[]{:S(2)}) %collective-permute-start.6) | collective-permute-done | bytes 102432 | tf_op jit(solution)/shard_map/ppermute | solution.py:101
  69.1 4.2 %collective-permute-start.7 = (f32[200,128]{1,0:T(8,128)S(1)}, f32[200,128]{1,0:T(8,128)S(1)}, u32[]{:S(2)}, u32[]{:S(2)}) collective-permute-start(f32[200,128]{1,0:T(8,128)S(1)} %add.121), channel_id=1, source_target_pairs={{0,1},{1,0},{2,23},{3,6},{4,5},{5,4},{6,3},{7,17},{8,9},{9,8},{10,... | collective-permute-start | bytes 307208 | tf_op jit(solution)/shard_map/ppermute | solution.py:101
  73.4 2.0 %collective-permute-done.7 = f32[200,128]{1,0:T(8,128)S(1)} collective-permute-done((f32[200,128]{1,0:T(8,128)S(1)}, f32[200,128]{1,0:T(8,128)S(1)}, u32[]{:S(2)}, u32[]{:S(2)}) %collective-permute-start.7) | collective-permute-done | bytes 102432 | tf_op jit(solution)/shard_map/ppermute | solution.py:101
  75.4 11.8 %collective-permute-start.8 = (f32[200,128]{1,0:T(8,128)S(1)}, f32[200,128]{1,0:T(8,128)S(1)}, u32[]{:S(2)}, u32[]{:S(2)}) collective-permute-start(f32[200,128]{1,0:T(8,128)S(1)} %add.122), channel_id=1, source_target_pairs={{0,20},{1,22},{2,21},{3,7},{4,16},{5,18},{6,17},{7,3},{8,28},{9,30... | collective-permute-start | bytes 307208 | tf_op jit(solution)/shard_map/ppermute | solution.py:101
  87.2 2.1 %collective-permute-done.8 = f32[200,128]{1,0:T(8,128)S(1)} collective-permute-done((f32[200,128]{1,0:T(8,128)S(1)}, f32[200,128]{1,0:T(8,128)S(1)}, u32[]{:S(2)}, u32[]{:S(2)}) %collective-permute-start.8) | collective-permute-done | bytes 102432 | tf_op jit(solution)/shard_map/ppermute | solution.py:101
  89.4 7.1 %collective-permute-start.9 = (f32[200,128]{1,0:T(8,128)S(1)}, f32[200,128]{1,0:T(8,128)S(1)}, u32[]{:S(2)}, u32[]{:S(2)}) collective-permute-start(f32[200,128]{1,0:T(8,128)S(1)} %add.123), channel_id=1, source_target_pairs={{0,23},{1,2},{2,1},{3,4},{4,3},{5,6},{6,5},{7,16},{8,31},{9,10},{1... | collective-permute-start | bytes 307208 | tf_op jit(solution)/shard_map/ppermute | solution.py:101
  96.4 3.3 %collective-permute-done.9 = f32[200,128]{1,0:T(8,128)S(1)} collective-permute-done((f32[200,128]{1,0:T(8,128)S(1)}, f32[200,128]{1,0:T(8,128)S(1)}, u32[]{:S(2)}, u32[]{:S(2)}) %collective-permute-start.9) | collective-permute-done | bytes 102432 | tf_op jit(solution)/shard_map/ppermute | solution.py:101
  99.8 2.2 %collective-permute-start.10 = (f32[200,128]{1,0:T(8,128)S(1)}, f32[200,128]{1,0:T(8,128)S(1)}, u32[]{:S(2)}, u32[]{:S(2)}) collective-permute-start(f32[200,128]{1,0:T(8,128)S(1)} %add.124), channel_id=1, source_target_pairs={{0,384},{8,392},{16,400},{24,408},{32,416},{40,424},{48,432},{56,4... | collective-permute-start | bytes 307208 | tf_op jit(solution)/shard_map/ppermute | solution.py:104
  105.6 5.0 %collective-permute-start.11 = (f32[400,128]{1,0:T(8,128)S(1)}, f32[400,128]{1,0:T(8,128)S(1)}, u32[]{:S(2)}, u32[]{:S(2)}) collective-permute-start(f32[400,128]{1,0:T(8,128)S(1)} %get-tuple-element.15), channel_id=1, source_target_pairs={{0,128},{8,136},{16,144},{24,152},{32,160},{40,168},{48,176},{56,1... | collective-permute-start | bytes 614408 | tf_op jit(solution)/shard_map/ppermute | solution.py:104
  117.6 10.4 %collective-permute-start.12 = (f32[800,128]{1,0:T(8,128)S(1)}, f32[800,128]{1,0:T(8,128)S(1)}, u32[]{:S(2)}, u32[]{:S(2)}) collective-permute-start(f32[800,128]{1,0:T(8,128)S(1)} %get-tuple-element.11), channel_id=1, source_target_pairs={{0,8},{8,0},{16,24},{24,16},{32,40},{40,32},{48,56},{56,48},{64,72... | collective-permute-start | bytes 1228808 | tf_op jit(solution)/shard_map/ppermute | solution.py:104
  128.0 1.7 %convolution_select_fusion = f32[32,16,5,128]{3,1,2,0:T(8,128)S(1)} fusion(bf16[3,3,128,128]{3,2,1,0:T(8,128)(2,1)S(1)} %copy-done, bf16[32,2,7,2,128]{4,2,1,3,0:T(8,128)(2,1)S(1)} %slice.39, bf16[32,2,8,5,128]{4,2,1,3,0:T(8,128)(2,1)S(1)} %copy.27, pred[16,5]{0,1:T(8,128)(4,1)S(1)} %copy-done.12), kind=kOutput, calls=%fused_computation.7 | convolution fusion | flops 742326272 | bytes 2490448 | tf_op jit(solution)/shard_map/conv_general_dilated | solution.py:22
  (80 shorter events, 20.3 us)
Async XLA Ops:
  0.6 2.9 %copy-start = (bf16[3,3,128,128]{3,2,1,0:T(8,128)(2,1)S(1)}, bf16[3,3,128,128]{3,2,1,0:T(8,128)(2,1)}, u32[]{:S(2)}) copy-start(bf16[3,3,128,128]{3,2,1,0:T(8,128)(2,1)} %param.13) | copy-start | bytes 884740
  0.6 15.5 %collective-permute-start = (bf16[2,32,32,128]{3,2,1,0:T(8,128)(2,1)}, bf16[2,32,32,128]{3,2,1,0:T(8,128)(2,1)}, u32[]{:S(2)}, u32[]{:S(2)}) collective-permute-start(bf16[2,32,32,128]{3,2,1,0:T(8,128)(2,1)} %bitcast.131), channel_id=1, source_target_pairs={{1,0},{2,1},{3,2},{4,3},{5,4},{6,5},{7,6},{9,8},{10,9},{11,10},{12... | collective-permute-start | bytes 1572872 | tf_op jit(solution)/shard_map/ppermute | solution.py:118
  3.4 0.7 copy-start.12
  6.3 1.0 copy-start.2
  7.7 1.9 %copy-start.1 = (bf16[1,2,32,32,128]{4,3,2,1,0:T(8,128)(2,1)S(1)}, bf16[1,2,32,32,128]{4,3,2,1,0:T(8,128)(2,1)}, u32[]{:S(2)}) copy-start(bf16[1,2,32,32,128]{4,3,2,1,0:T(8,128)(2,1)} %param.12) | copy-start | bytes 1572868
  7.7 3.3 %copy-start.7 = (bf16[3,128,128]{2,1,0:T(8,128)(2,1)S(1)}, bf16[3,128,128]{2,1,0:T(8,128)(2,1)}, u32[]{:S(2)}) copy-start(bf16[3,128,128]{2,1,0:T(8,128)(2,1)} %param.15) | copy-start | bytes 294916
  11.0 6.2 %copy-start.3 = (bf16[32,2,32,128]{3,0,2,1:T(8,128)(2,1)S(1)}, bf16[32,2,32,128]{3,0,2,1:T(8,128)(2,1)}, u32[]{:S(2)}) copy-start(bf16[32,2,32,128]{3,0,2,1:T(8,128)(2,1)} %copy-done.2) | copy-start | bytes 1572868
  19.2 1.0 copy-start.6
  20.0 4.2 %copy-start.4 = (bf16[2,32,32,128]{3,1,2,0:T(8,128)(2,1)}, bf16[2,32,32,128]{3,1,2,0:T(8,128)(2,1)S(1)}, u32[]{:S(2)}) copy-start(bf16[2,32,32,128]{3,1,2,0:T(8,128)(2,1)S(1)} %get-tuple-element.5) | copy-start | bytes 1572868
  25.7 4.4 %copy-start.10 = (s32[64]{0:T(128)S(1)}, s32[64]{0:T(128)}, u32[]{:S(2)}) copy-start(s32[64]{0:T(128)} %constant.73.clone) | copy-start | bytes 772
  26.1 8.8 %copy-start.9 = (s32[64]{0:T(128)S(1)}, s32[64]{0:T(128)}, u32[]{:S(2)}) copy-start(s32[64]{0:T(128)} %constant.74.clone) | copy-start | bytes 772
  26.1 5.2 %collective-permute-start.1 = (f32[800,128]{1,0:T(8,128)S(1)}, f32[800,128]{1,0:T(8,128)S(1)}, u32[]{:S(2)}, u32[]{:S(2)}) collective-permute-start(f32[800,128]{1,0:T(8,128)S(1)} %constant_dynamic-slice_fusion.2), channel_id=1, source_target_pairs={{0,8},{8,0},{16,24},{24,16},{32,40},{40,32},{48,56},{56,48},{64,72... | collective-permute-start | bytes 1228808 | tf_op jit(solution)/shard_map/ppermute | solution.py:98
  31.4 8.5 %collective-permute-start.2 = (f32[400,128]{1,0:T(8,128)S(1)}, f32[400,128]{1,0:T(8,128)S(1)}, u32[]{:S(2)}, u32[]{:S(2)}) collective-permute-start(f32[400,128]{1,0:T(8,128)S(1)} %constant_dynamic-slice_fusion.1), channel_id=1, source_target_pairs={{0,128},{8,136},{16,144},{24,152},{32,160},{40,168},{48,176},{56,1... | collective-permute-start | bytes 614408 | tf_op jit(solution)/shard_map/ppermute | solution.py:98
  40.0 5.4 %collective-permute-start.3 = (f32[200,128]{1,0:T(8,128)S(1)}, f32[200,128]{1,0:T(8,128)S(1)}, u32[]{:S(2)}, u32[]{:S(2)}) collective-permute-start(f32[200,128]{1,0:T(8,128)S(1)} %constant_dynamic-slice_fusion), channel_id=1, source_target_pairs={{0,384},{8,392},{16,400},{24,408},{32,416},{40,424},{48,432},{56,4... | collective-permute-start | bytes 307208 | tf_op jit(solution)/shard_map/ppermute | solution.py:98
  45.4 5.4 %collective-permute-start.4 = (f32[200,128]{1,0:T(8,128)S(1)}, f32[200,128]{1,0:T(8,128)S(1)}, u32[]{:S(2)}, u32[]{:S(2)}) collective-permute-start(f32[200,128]{1,0:T(8,128)S(1)} %dynamic-slice_add_fusion.2), channel_id=1, source_target_pairs={{0,32},{8,40},{16,48},{24,56},{32,0},{40,8},{48,16},{56,24},{64,96... | collective-permute-start | bytes 307208 | tf_op jit(solution)/shard_map/ppermute | solution.py:101
  50.8 66.2 %copy-start.5 = (bf16[2,32,32,128]{3,1,2,0:T(8,128)(2,1)S(1)}, bf16[2,32,32,128]{3,1,2,0:T(8,128)(2,1)}, u32[]{:S(2)}) copy-start(bf16[2,32,32,128]{3,1,2,0:T(8,128)(2,1)} %copy-done.4) | copy-start | bytes 1572868
  50.8 6.7 %collective-permute-start.5 = (f32[200,128]{1,0:T(8,128)S(1)}, f32[200,128]{1,0:T(8,128)S(1)}, u32[]{:S(2)}, u32[]{:S(2)}) collective-permute-start(f32[200,128]{1,0:T(8,128)S(1)} %add.119), channel_id=1, source_target_pairs={{0,96},{8,104},{16,112},{24,120},{32,64},{40,72},{48,80},{56,88},{... | collective-permute-start | bytes 307208 | tf_op jit(solution)/shard_map/ppermute | solution.py:101
  57.6 11.5 %collective-permute-start.6 = (f32[200,128]{1,0:T(8,128)S(1)}, f32[200,128]{1,0:T(8,128)S(1)}, u32[]{:S(2)}, u32[]{:S(2)}) collective-permute-start(f32[200,128]{1,0:T(8,128)S(1)} %add.120), channel_id=1, source_target_pairs={{0,4},{1,5},{2,6},{3,23},{4,0},{5,1},{6,2},{7,19},{8,12},{9,13},{1... | collective-permute-start | bytes 307208 | tf_op jit(solution)/shard_map/ppermute | solution.py:101
  69.1 6.3 %collective-permute-start.7 = (f32[200,128]{1,0:T(8,128)S(1)}, f32[200,128]{1,0:T(8,128)S(1)}, u32[]{:S(2)}, u32[]{:S(2)}) collective-permute-start(f32[200,128]{1,0:T(8,128)S(1)} %add.121), channel_id=1, source_target_pairs={{0,1},{1,0},{2,23},{3,6},{4,5},{5,4},{6,3},{7,17},{8,9},{9,8},{10,... | collective-permute-start | bytes 307208 | tf_op jit(solution)/shard_map/ppermute | solution.py:101
  75.4 13.9 %collective-permute-start.8 = (f32[200,128]{1,0:T(8,128)S(1)}, f32[200,128]{1,0:T(8,128)S(1)}, u32[]{:S(2)}, u32[]{:S(2)}) collective-permute-start(f32[200,128]{1,0:T(8,128)S(1)} %add.122), channel_id=1, source_target_pairs={{0,20},{1,22},{2,21},{3,7},{4,16},{5,18},{6,17},{7,3},{8,28},{9,30... | collective-permute-start | bytes 307208 | tf_op jit(solution)/shard_map/ppermute | solution.py:101
  89.4 10.4 %collective-permute-start.9 = (f32[200,128]{1,0:T(8,128)S(1)}, f32[200,128]{1,0:T(8,128)S(1)}, u32[]{:S(2)}, u32[]{:S(2)}) collective-permute-start(f32[200,128]{1,0:T(8,128)S(1)} %add.123), channel_id=1, source_target_pairs={{0,23},{1,2},{2,1},{3,4},{4,3},{5,6},{6,5},{7,16},{8,31},{9,10},{1... | collective-permute-start | bytes 307208 | tf_op jit(solution)/shard_map/ppermute | solution.py:101
  99.8 5.7 %collective-permute-start.10 = (f32[200,128]{1,0:T(8,128)S(1)}, f32[200,128]{1,0:T(8,128)S(1)}, u32[]{:S(2)}, u32[]{:S(2)}) collective-permute-start(f32[200,128]{1,0:T(8,128)S(1)} %add.124), channel_id=1, source_target_pairs={{0,384},{8,392},{16,400},{24,408},{32,416},{40,424},{48,432},{56,4... | collective-permute-start | bytes 307208 | tf_op jit(solution)/shard_map/ppermute | solution.py:104
  105.6 11.9 %collective-permute-start.11 = (f32[400,128]{1,0:T(8,128)S(1)}, f32[400,128]{1,0:T(8,128)S(1)}, u32[]{:S(2)}, u32[]{:S(2)}) collective-permute-start(f32[400,128]{1,0:T(8,128)S(1)} %get-tuple-element.15), channel_id=1, source_target_pairs={{0,128},{8,136},{16,144},{24,152},{32,160},{40,168},{48,176},{56,1... | collective-permute-start | bytes 614408 | tf_op jit(solution)/shard_map/ppermute | solution.py:104
  117.6 14.1 %collective-permute-start.12 = (f32[800,128]{1,0:T(8,128)S(1)}, f32[800,128]{1,0:T(8,128)S(1)}, u32[]{:S(2)}, u32[]{:S(2)}) collective-permute-start(f32[800,128]{1,0:T(8,128)S(1)} %get-tuple-element.11), channel_id=1, source_target_pairs={{0,8},{8,0},{16,24},{24,16},{32,40},{40,32},{48,56},{56,48},{64,72... | collective-permute-start | bytes 1228808 | tf_op jit(solution)/shard_map/ppermute | solution.py:104
  (2 other events, 1.3 us)

commit v5 on v4

--- a/solution.py
+++ b/solution.py
@@ -50,7 +50,7 @@
     return grad_act, jnp.stack(lag_terms)
 
 
-ZRING = (2, 0, 8, 11, 3, 1, 9, 15, 7, 13, 5, 14, 6, 12, 4, 10)
+ZRING = (0, 1, 3, 2, 4, 5, 7, 6, 12, 13, 15, 14, 8, 9, 11, 10)
 
 
 def butterfly_steps(n_clip, n_tm):

time: 135 us -> 133 us (0.985)
  the two profiles are of different devices: /device:TPU:29 before, /device:TPU:125 now
where the time goes in v5:
time: 133 us; the launch traced here: 132 us
  starting transfers between devices  55.8 us (42%)
  waiting for transfers between devices  35.2 us (26%)
  between operations  14.8 us (11%)
  matrix products  12.7 us (10%)
  local copies, waits for them, and re-layouts  7.5 us (6%)
  other arithmetic  5.96 us (4%)
    ppermute x6, waiting for transfers between devices, all_reduce(): x = x + lax.ppermute(x, axis, perm)  23.4 us
    ppermute x3, starting transfers between devices, all_reduce(): other = lax.ppermute(x, axis, perm)  22.9 us
    ppermute x6, starting transfers between devices, all_reduce(): x = x + lax.ppermute(x, axis, perm)  22.6 us
    ppermute x3, starting transfers between devices, all_reduce(): x = keep + lax.ppermute(send, axis, perm)  8.24 us
    ppermute x3, waiting for transfers between devices, all_reduce(): x = keep + lax.ppermute(send, axis, perm)  6.37 us
    ppermute x1, waiting for transfers between devices, local(): after = lax.ppermute(cot, 'tm', [(t, t - 1) for t in range(1, n_tm)])  5.42 us
    transpose x1, matrix products, spatial_weight_grad(): return jnp.transpose(result, (1, 2, 0, 3))  3.98 us
    unnamed x28, local copies, waits for them, and re-layouts  3.29 us
  transfers between devices with their start and end apart: 13, of which 9 were waited for; matrix products, arithmetic and copies ran while one was open for 10% of the time, Pallas kernels for 0%

profile of v5, /device:TPU:125, one launch (start us, length us, event | category | flops | bytes accessed | tf_op | source)
XLA Modules:
  0.0 132.0 jit_solution(11006511583988153657)
XLA Ops:
  0.6 2.1 %collective-permute-start = (bf16[2,32,32,128]{3,2,1,0:T(8,128)(2,1)}, bf16[2,32,32,128]{3,2,1,0:T(8,128)(2,1)}, u32[]{:S(2)}, u32[]{:S(2)}) collective-permute-start(bf16[2,32,32,128]{3,2,1,0:T(8,128)(2,1)} %bitcast.131), channel_id=1, source_target_pairs={{1,0},{2,1},{3,2},{4,3},{5,4},{6,5},{7,6},{9,8},{10,9},{11,10},{12... | collective-permute-start | bytes 1572872 | tf_op jit(solution)/shard_map/ppermute | solution.py:118
  4.7 1.9 %multiply_convert_fusion = (bf16[32,16,5,128]{3,1,2,0:T(8,128)(2,1)S(1)}, f32[32,16,5,128]{3,1,2,0:T(8,128)S(1)}, f32[32,16,5,128]{3,1,2,0:T(8,128)S(1)}) fusion(f32[128]{0:T(128)S(1)} %copy-done.8, bf16[3,3,128,128]{3,2,1,0:T(8,128)(2,1)S(1)} %copy-done, bf16[32,2,8,7,128]{4,0,3,2,1:T(8,128)(2,1)S(1)} %fusion.12, pred[16,5]{0,1:T(8,128)(4,1)S(1)} %copy-done.12), kind=kOutput, calls=%fused_computation.11 | convolution fusion | flops 742522880 | bytes 4489808 | tf_op jit(solution)/shard_map/conv_general_dilated | solution.py:13
  12.0 5.4 %collective-permute-done = bf16[2,32,32,128]{3,2,1,0:T(8,128)(2,1)} collective-permute-done((bf16[2,32,32,128]{3,2,1,0:T(8,128)(2,1)}, bf16[2,32,32,128]{3,2,1,0:T(8,128)(2,1)}, u32[]{:S(2)}, u32[]{:S(2)}) %collective-permute-start) | collective-permute-done | bytes 524320 | tf_op jit(solution)/shard_map/ppermute | solution.py:118
  21.5 4.0 %fusion.22 = f32[3,3,128,128]{3,2,1,0:T(8,128)S(1)} fusion(bf16[2,32,32,128]{3,2,1,0:T(8,128)(2,1)S(1)} %bitcast.150, bf16[2,32,32,128]{3,1,2,0:T(8,128)(2,1)S(1)} %get-tuple-element.5), kind=kOutput, calls=%fused_computation.44 | convolution fusion | flops 579076096 | bytes 1638400 | tf_op jit(solution)/shard_map/transpose | solution.py:33
  27.4 3.3 %collective-permute-start.1 = (f32[800,128]{1,0:T(8,128)S(1)}, f32[800,128]{1,0:T(8,128)S(1)}, u32[]{:S(2)}, u32[]{:S(2)}) collective-permute-start(f32[800,128]{1,0:T(8,128)S(1)} %constant_dynamic-slice_fusion.2), channel_id=1, source_target_pairs={{0,8},{8,0},{16,24},{24,16},{32,40},{40,32},{48,56},{56,48},{64,72... | collective-permute-start | bytes 1228808 | tf_op jit(solution)/shard_map/ppermute | solution.py:98
  32.6 2.8 %collective-permute-start.2 = (f32[400,128]{1,0:T(8,128)S(1)}, f32[400,128]{1,0:T(8,128)S(1)}, u32[]{:S(2)}, u32[]{:S(2)}) collective-permute-start(f32[400,128]{1,0:T(8,128)S(1)} %constant_dynamic-slice_fusion.1), channel_id=1, source_target_pairs={{0,128},{8,136},{16,144},{24,152},{32,160},{40,168},{48,176},{56,1... | collective-permute-start | bytes 614408 | tf_op jit(solution)/shard_map/ppermute | solution.py:98
  37.4 3.8 %collective-permute-done.2 = f32[400,128]{1,0:T(8,128)S(1)} collective-permute-done((f32[400,128]{1,0:T(8,128)S(1)}, f32[400,128]{1,0:T(8,128)S(1)}, u32[]{:S(2)}, u32[]{:S(2)}) %collective-permute-start.2) | collective-permute-done | bytes 204832 | tf_op jit(solution)/shard_map/ppermute | solution.py:98
  41.2 2.2 %collective-permute-start.3 = (f32[200,128]{1,0:T(8,128)S(1)}, f32[200,128]{1,0:T(8,128)S(1)}, u32[]{:S(2)}, u32[]{:S(2)}) collective-permute-start(f32[200,128]{1,0:T(8,128)S(1)} %constant_dynamic-slice_fusion), channel_id=1, source_target_pairs={{0,384},{8,392},{16,400},{24,408},{32,416},{40,424},{48,432},{56,4... | collective-permute-start | bytes 307208 | tf_op jit(solution)/shard_map/ppermute | solution.py:98
  44.0 2.6 %collective-permute-done.3 = f32[200,128]{1,0:T(8,128)S(1)} collective-permute-done((f32[200,128]{1,0:T(8,128)S(1)}, f32[200,128]{1,0:T(8,128)S(1)}, u32[]{:S(2)}, u32[]{:S(2)}) %collective-permute-start.3) | collective-permute-done | bytes 102432 | tf_op jit(solution)/shard_map/ppermute | solution.py:98
  46.6 2.4 %collective-permute-start.4 = (f32[200,128]{1,0:T(8,128)S(1)}, f32[200,128]{1,0:T(8,128)S(1)}, u32[]{:S(2)}, u32[]{:S(2)}) collective-permute-start(f32[200,128]{1,0:T(8,128)S(1)} %dynamic-slice_add_fusion.2), channel_id=1, source_target_pairs={{0,32},{8,40},{16,48},{24,56},{32,0},{40,8},{48,16},{56,24},{64,96... | collective-permute-start | bytes 307208 | tf_op jit(solution)/shard_map/ppermute | solution.py:101
  49.0 3.0 %collective-permute-done.4 = f32[200,128]{1,0:T(8,128)S(1)} collective-permute-done((f32[200,128]{1,0:T(8,128)S(1)}, f32[200,128]{1,0:T(8,128)S(1)}, u32[]{:S(2)}, u32[]{:S(2)}) %collective-permute-start.4) | collective-permute-done | bytes 102432 | tf_op jit(solution)/shard_map/ppermute | solution.py:101
  52.1 2.1 %collective-permute-start.5 = (f32[200,128]{1,0:T(8,128)S(1)}, f32[200,128]{1,0:T(8,128)S(1)}, u32[]{:S(2)}, u32[]{:S(2)}) collective-permute-start(f32[200,128]{1,0:T(8,128)S(1)} %add.119), channel_id=1, source_target_pairs={{0,96},{8,104},{16,112},{24,120},{32,64},{40,72},{48,80},{56,88},{... | collective-permute-start | bytes 307208 | tf_op jit(solution)/shard_map/ppermute | solution.py:101
  54.1 4.7 %collective-permute-done.5 = f32[200,128]{1,0:T(8,128)S(1)} collective-permute-done((f32[200,128]{1,0:T(8,128)S(1)}, f32[200,128]{1,0:T(8,128)S(1)}, u32[]{:S(2)}, u32[]{:S(2)}) %collective-permute-start.5) | collective-permute-done | bytes 102432 | tf_op jit(solution)/shard_map/ppermute | solution.py:101
  58.8 1.9 %collective-permute-start.6 = (f32[200,128]{1,0:T(8,128)S(1)}, f32[200,128]{1,0:T(8,128)S(1)}, u32[]{:S(2)}, u32[]{:S(2)}) collective-permute-start(f32[200,128]{1,0:T(8,128)S(1)} %add.120), channel_id=1, source_target_pairs={{0,1},{1,0},{2,3},{3,2},{4,5},{5,4},{6,7},{7,6},{8,9},{9,8},{10,11... | collective-permute-start | bytes 307208 | tf_op jit(solution)/shard_map/ppermute | solution.py:101
  60.7 3.5 %collective-permute-done.6 = f32[200,128]{1,0:T(8,128)S(1)} collective-permute-done((f32[200,128]{1,0:T(8,128)S(1)}, f32[200,128]{1,0:T(8,128)S(1)}, u32[]{:S(2)}, u32[]{:S(2)}) %collective-permute-start.6) | collective-permute-done | bytes 102432 | tf_op jit(solution)/shard_map/ppermute | solution.py:101
  64.2 1.9 %collective-permute-start.7 = (f32[200,128]{1,0:T(8,128)S(1)}, f32[200,128]{1,0:T(8,128)S(1)}, u32[]{:S(2)}, u32[]{:S(2)}) collective-permute-start(f32[200,128]{1,0:T(8,128)S(1)} %add.121), channel_id=1, source_target_pairs={{0,3},{1,2},{2,1},{3,0},{4,7},{5,6},{6,5},{7,4},{8,11},{9,10},{10,... | collective-permute-start | bytes 307208 | tf_op jit(solution)/shard_map/ppermute | solution.py:101
  66.2 5.3 %collective-permute-done.7 = f32[200,128]{1,0:T(8,128)S(1)} collective-permute-done((f32[200,128]{1,0:T(8,128)S(1)}, f32[200,128]{1,0:T(8,128)S(1)}, u32[]{:S(2)}, u32[]{:S(2)}) %collective-permute-start.7) | collective-permute-done | bytes 102432 | tf_op jit(solution)/shard_map/ppermute | solution.py:101
  71.5 5.9 %collective-permute-start.8 = (f32[200,128]{1,0:T(8,128)S(1)}, f32[200,128]{1,0:T(8,128)S(1)}, u32[]{:S(2)}, u32[]{:S(2)}) collective-permute-start(f32[200,128]{1,0:T(8,128)S(1)} %add.122), channel_id=1, source_target_pairs={{0,4},{1,5},{2,6},{3,7},{4,0},{5,1},{6,2},{7,3},{8,12},{9,13},{10,... | collective-permute-start | bytes 307208 | tf_op jit(solution)/shard_map/ppermute | solution.py:101
  77.4 4.5 %collective-permute-done.8 = f32[200,128]{1,0:T(8,128)S(1)} collective-permute-done((f32[200,128]{1,0:T(8,128)S(1)}, f32[200,128]{1,0:T(8,128)S(1)}, u32[]{:S(2)}, u32[]{:S(2)}) %collective-permute-start.8) | collective-permute-done | bytes 102432 | tf_op jit(solution)/shard_map/ppermute | solution.py:101
  81.9 8.4 %collective-permute-start.9 = (f32[200,128]{1,0:T(8,128)S(1)}, f32[200,128]{1,0:T(8,128)S(1)}, u32[]{:S(2)}, u32[]{:S(2)}) collective-permute-start(f32[200,128]{1,0:T(8,128)S(1)} %add.123), channel_id=1, source_target_pairs={{0,20},{1,21},{2,22},{3,23},{4,16},{5,17},{6,18},{7,19},{8,28},{9,... | collective-permute-start | bytes 307208 | tf_op jit(solution)/shard_map/ppermute | solution.py:101
  90.3 2.4 %collective-permute-done.9 = f32[200,128]{1,0:T(8,128)S(1)} collective-permute-done((f32[200,128]{1,0:T(8,128)S(1)}, f32[200,128]{1,0:T(8,128)S(1)}, u32[]{:S(2)}, u32[]{:S(2)}) %collective-permute-start.9) | collective-permute-done | bytes 102432 | tf_op jit(solution)/shard_map/ppermute | solution.py:101
  92.7 2.2 %collective-permute-start.10 = (f32[200,128]{1,0:T(8,128)S(1)}, f32[200,128]{1,0:T(8,128)S(1)}, u32[]{:S(2)}, u32[]{:S(2)}) collective-permute-start(f32[200,128]{1,0:T(8,128)S(1)} %add.124), channel_id=1, source_target_pairs={{0,384},{8,392},{16,400},{24,408},{32,416},{40,424},{48,432},{56,4... | collective-permute-start | bytes 307208 | tf_op jit(solution)/shard_map/ppermute | solution.py:104
  98.3 5.2 %collective-permute-start.11 = (f32[400,128]{1,0:T(8,128)S(1)}, f32[400,128]{1,0:T(8,128)S(1)}, u32[]{:S(2)}, u32[]{:S(2)}) collective-permute-start(f32[400,128]{1,0:T(8,128)S(1)} %get-tuple-element.15), channel_id=1, source_target_pairs={{0,128},{8,136},{16,144},{24,152},{32,160},{40,168},{48,176},{56,1... | collective-permute-start | bytes 614408 | tf_op jit(solution)/shard_map/ppermute | solution.py:104
  110.6 15.5 %collective-permute-start.12 = (f32[800,128]{1,0:T(8,128)S(1)}, f32[800,128]{1,0:T(8,128)S(1)}, u32[]{:S(2)}, u32[]{:S(2)}) collective-permute-start(f32[800,128]{1,0:T(8,128)S(1)} %get-tuple-element.11), channel_id=1, source_target_pairs={{0,8},{8,0},{16,24},{24,16},{32,40},{40,32},{48,56},{56,48},{64,72... | collective-permute-start | bytes 1228808 | tf_op jit(solution)/shard_map/ppermute | solution.py:104
  (80 shorter events, 20.3 us)
Async XLA Ops:
  0.6 3.5 %copy-start = (bf16[3,3,128,128]{3,2,1,0:T(8,128)(2,1)S(1)}, bf16[3,3,128,128]{3,2,1,0:T(8,128)(2,1)}, u32[]{:S(2)}) copy-start(bf16[3,3,128,128]{3,2,1,0:T(8,128)(2,1)} %param.13) | copy-start | bytes 884740
  0.6 16.7 %collective-permute-start = (bf16[2,32,32,128]{3,2,1,0:T(8,128)(2,1)}, bf16[2,32,32,128]{3,2,1,0:T(8,128)(2,1)}, u32[]{:S(2)}, u32[]{:S(2)}) collective-permute-start(bf16[2,32,32,128]{3,2,1,0:T(8,128)(2,1)} %bitcast.131), channel_id=1, source_target_pairs={{1,0},{2,1},{3,2},{4,3},{5,4},{6,5},{7,6},{9,8},{10,9},{11,10},{12... | collective-permute-start | bytes 1572872 | tf_op jit(solution)/shard_map/ppermute | solution.py:118
  4.0 0.7 copy-start.12
  6.9 1.0 copy-start.2
  8.4 1.9 %copy-start.1 = (bf16[1,2,32,32,128]{4,3,2,1,0:T(8,128)(2,1)S(1)}, bf16[1,2,32,32,128]{4,3,2,1,0:T(8,128)(2,1)}, u32[]{:S(2)}) copy-start(bf16[1,2,32,32,128]{4,3,2,1,0:T(8,128)(2,1)} %param.12) | copy-start | bytes 1572868
  8.4 3.3 %copy-start.7 = (bf16[3,128,128]{2,1,0:T(8,128)(2,1)S(1)}, bf16[3,128,128]{2,1,0:T(8,128)(2,1)}, u32[]{:S(2)}) copy-start(bf16[3,128,128]{2,1,0:T(8,128)(2,1)} %param.15) | copy-start | bytes 294916
  11.6 6.7 %copy-start.3 = (bf16[32,2,32,128]{3,0,2,1:T(8,128)(2,1)S(1)}, bf16[32,2,32,128]{3,0,2,1:T(8,128)(2,1)}, u32[]{:S(2)}) copy-start(bf16[32,2,32,128]{3,0,2,1:T(8,128)(2,1)} %copy-done.2) | copy-start | bytes 1572868
  20.4 1.0 copy-start.6
  21.2 4.2 %copy-start.4 = (bf16[2,32,32,128]{3,1,2,0:T(8,128)(2,1)}, bf16[2,32,32,128]{3,1,2,0:T(8,128)(2,1)S(1)}, u32[]{:S(2)}) copy-start(bf16[2,32,32,128]{3,1,2,0:T(8,128)(2,1)S(1)} %get-tuple-element.5) | copy-start | bytes 1572868
  26.9 4.4 %copy-start.10 = (s32[64]{0:T(128)S(1)}, s32[64]{0:T(128)}, u32[]{:S(2)}) copy-start(s32[64]{0:T(128)} %constant.73.clone) | copy-start | bytes 772
  27.3 8.8 %copy-start.9 = (s32[64]{0:T(128)S(1)}, s32[64]{0:T(128)}, u32[]{:S(2)}) copy-start(s32[64]{0:T(128)} %constant.74.clone) | copy-start | bytes 772
  27.4 5.2 %collective-permute-start.1 = (f32[800,128]{1,0:T(8,128)S(1)}, f32[800,128]{1,0:T(8,128)S(1)}, u32[]{:S(2)}, u32[]{:S(2)}) collective-permute-start(f32[800,128]{1,0:T(8,128)S(1)} %constant_dynamic-slice_fusion.2), channel_id=1, source_target_pairs={{0,8},{8,0},{16,24},{24,16},{32,40},{40,32},{48,56},{56,48},{64,72... | collective-permute-start | bytes 1228808 | tf_op jit(solution)/shard_map/ppermute | solution.py:98
  32.6 8.5 %collective-permute-start.2 = (f32[400,128]{1,0:T(8,128)S(1)}, f32[400,128]{1,0:T(8,128)S(1)}, u32[]{:S(2)}, u32[]{:S(2)}) collective-permute-start(f32[400,128]{1,0:T(8,128)S(1)} %constant_dynamic-slice_fusion.1), channel_id=1, source_target_pairs={{0,128},{8,136},{16,144},{24,152},{32,160},{40,168},{48,176},{56,1... | collective-permute-start | bytes 614408 | tf_op jit(solution)/shard_map/ppermute | solution.py:98
  41.2 5.4 %collective-permute-start.3 = (f32[200,128]{1,0:T(8,128)S(1)}, f32[200,128]{1,0:T(8,128)S(1)}, u32[]{:S(2)}, u32[]{:S(2)}) collective-permute-start(f32[200,128]{1,0:T(8,128)S(1)} %constant_dynamic-slice_fusion), channel_id=1, source_target_pairs={{0,384},{8,392},{16,400},{24,408},{32,416},{40,424},{48,432},{56,4... | collective-permute-start | bytes 307208 | tf_op jit(solution)/shard_map/ppermute | solution.py:98
  46.6 5.4 %collective-permute-start.4 = (f32[200,128]{1,0:T(8,128)S(1)}, f32[200,128]{1,0:T(8,128)S(1)}, u32[]{:S(2)}, u32[]{:S(2)}) collective-permute-start(f32[200,128]{1,0:T(8,128)S(1)} %dynamic-slice_add_fusion.2), channel_id=1, source_target_pairs={{0,32},{8,40},{16,48},{24,56},{32,0},{40,8},{48,16},{56,24},{64,96... | collective-permute-start | bytes 307208 | tf_op jit(solution)/shard_map/ppermute | solution.py:101
  52.0 58.0 %copy-start.5 = (bf16[2,32,32,128]{3,1,2,0:T(8,128)(2,1)S(1)}, bf16[2,32,32,128]{3,1,2,0:T(8,128)(2,1)}, u32[]{:S(2)}) copy-start(bf16[2,32,32,128]{3,1,2,0:T(8,128)(2,1)} %copy-done.4) | copy-start | bytes 1572868
  52.1 6.7 %collective-permute-start.5 = (f32[200,128]{1,0:T(8,128)S(1)}, f32[200,128]{1,0:T(8,128)S(1)}, u32[]{:S(2)}, u32[]{:S(2)}) collective-permute-start(f32[200,128]{1,0:T(8,128)S(1)} %add.119), channel_id=1, source_target_pairs={{0,96},{8,104},{16,112},{24,120},{32,64},{40,72},{48,80},{56,88},{... | collective-permute-start | bytes 307208 | tf_op jit(solution)/shard_map/ppermute | solution.py:101
  58.8 5.4 %collective-permute-start.6 = (f32[200,128]{1,0:T(8,128)S(1)}, f32[200,128]{1,0:T(8,128)S(1)}, u32[]{:S(2)}, u32[]{:S(2)}) collective-permute-start(f32[200,128]{1,0:T(8,128)S(1)} %add.120), channel_id=1, source_target_pairs={{0,1},{1,0},{2,3},{3,2},{4,5},{5,4},{6,7},{7,6},{8,9},{9,8},{10,11... | collective-permute-start | bytes 307208 | tf_op jit(solution)/shard_map/ppermute | solution.py:101
  64.2 7.2 %collective-permute-start.7 = (f32[200,128]{1,0:T(8,128)S(1)}, f32[200,128]{1,0:T(8,128)S(1)}, u32[]{:S(2)}, u32[]{:S(2)}) collective-permute-start(f32[200,128]{1,0:T(8,128)S(1)} %add.121), channel_id=1, source_target_pairs={{0,3},{1,2},{2,1},{3,0},{4,7},{5,6},{6,5},{7,4},{8,11},{9,10},{10,... | collective-permute-start | bytes 307208 | tf_op jit(solution)/shard_map/ppermute | solution.py:101
  71.5 10.4 %collective-permute-start.8 = (f32[200,128]{1,0:T(8,128)S(1)}, f32[200,128]{1,0:T(8,128)S(1)}, u32[]{:S(2)}, u32[]{:S(2)}) collective-permute-start(f32[200,128]{1,0:T(8,128)S(1)} %add.122), channel_id=1, source_target_pairs={{0,4},{1,5},{2,6},{3,7},{4,0},{5,1},{6,2},{7,3},{8,12},{9,13},{10,... | collective-permute-start | bytes 307208 | tf_op jit(solution)/shard_map/ppermute | solution.py:101
  81.9 10.8 %collective-permute-start.9 = (f32[200,128]{1,0:T(8,128)S(1)}, f32[200,128]{1,0:T(8,128)S(1)}, u32[]{:S(2)}, u32[]{:S(2)}) collective-permute-start(f32[200,128]{1,0:T(8,128)S(1)} %add.123), channel_id=1, source_target_pairs={{0,20},{1,21},{2,22},{3,23},{4,16},{5,17},{6,18},{7,19},{8,28},{9,... | collective-permute-start | bytes 307208 | tf_op jit(solution)/shard_map/ppermute | solution.py:101
  92.7 5.5 %collective-permute-start.10 = (f32[200,128]{1,0:T(8,128)S(1)}, f32[200,128]{1,0:T(8,128)S(1)}, u32[]{:S(2)}, u32[]{:S(2)}) collective-permute-start(f32[200,128]{1,0:T(8,128)S(1)} %add.124), channel_id=1, source_target_pairs={{0,384},{8,392},{16,400},{24,408},{32,416},{40,424},{48,432},{56,4... | collective-permute-start | bytes 307208 | tf_op jit(solution)/shard_map/ppermute | solution.py:104
  98.3 12.1 %collective-permute-start.11 = (f32[400,128]{1,0:T(8,128)S(1)}, f32[400,128]{1,0:T(8,128)S(1)}, u32[]{:S(2)}, u32[]{:S(2)}) collective-permute-start(f32[400,128]{1,0:T(8,128)S(1)} %get-tuple-element.15), channel_id=1, source_target_pairs={{0,128},{8,136},{16,144},{24,152},{32,160},{40,168},{48,176},{56,1... | collective-permute-start | bytes 614408 | tf_op jit(solution)/shard_map/ppermute | solution.py:104
  110.6 19.2 %collective-permute-start.12 = (f32[800,128]{1,0:T(8,128)S(1)}, f32[800,128]{1,0:T(8,128)S(1)}, u32[]{:S(2)}, u32[]{:S(2)}) collective-permute-start(f32[800,128]{1,0:T(8,128)S(1)} %get-tuple-element.11), channel_id=1, source_target_pairs={{0,8},{8,0},{16,24},{24,16},{32,40},{40,32},{48,56},{56,48},{64,72... | collective-permute-start | bytes 1228808 | tf_op jit(solution)/shard_map/ppermute | solution.py:104
  (2 other events, 1.3 us)

commit v6 on v5

--- a/solution.py
+++ b/solution.py
@@ -58,15 +58,14 @@
     steps = []
 
     def clip_step(size, stride, labels, bit, kind):
-        perm, bits = [], []
+        perm = []
         pos = {lab: r for r, lab in enumerate(labels)}
         for c in range(n_clip):
             r = (c // stride) % size
             lab = labels[r]
             r2 = pos[lab ^ (1 << bit)]
             perm.append((c, c + (r2 - r) * stride))
-            bits.append((lab >> bit) & 1)
-        steps.append(("clip", tuple(perm), tuple(bits), kind))
+        steps.append(("clip", tuple(perm), (stride, size, labels is GRAY4, bit), kind))
 
     clip_step(2, 1, (0, 1), 0, "halve")
     for b in range(2):
@@ -86,12 +85,20 @@
     return steps
 
 
+def label_bit(axis, where):
+    stride, size, gray, bit = where
+    r = (lax.axis_index(axis) // stride) % size
+    if gray:
+        r = r ^ (r >> 1)
+    return (r >> bit) & 1
+
+
 def all_reduce(x, n_clip, n_tm):
     steps = butterfly_steps(n_clip, n_tm)
     halved = []
     for axis, perm, bits, kind in steps:
         if kind == "halve":
-            bit = jnp.asarray(bits, jnp.int32)[lax.axis_index(axis)]
+            bit = label_bit(axis, bits)
             h = x.shape[0] // 2
             keep = lax.dynamic_slice_in_dim(x, bit * h, h)
             send = lax.dynamic_slice_in_dim(x, (1 - bit) * h, h)
@@ -100,7 +107,7 @@
         else:
             x = x + lax.ppermute(x, axis, perm)
     for axis, perm, bits in halved[::-1]:
-        bit = jnp.asarray(bits, jnp.int32)[lax.axis_index(axis)]
+        bit = label_bit(axis, bits)
         other = lax.ppermute(x, axis, perm)
         both = jnp.stack([x, other])
         first = lax.dynamic_index_in_dim(both, bit, keepdims=False)

time: 133 us -> 130 us (0.977)
  the two profiles are of different devices: /device:TPU:125 before, /device:TPU:1 now
where the time goes in v6:
time: 130 us
  starting transfers between devices  67.8 us (52%)
  waiting for transfers between devices  33.9 us (26%)
  matrix products  13.8 us (11%)
  local copies, waits for them, and re-layouts  7.05 us (5%)
  other arithmetic  5.95 us (5%)
    ppermute x6, starting transfers between devices, all_reduce(): x = x + lax.ppermute(x, axis, perm)  33.1 us
    ppermute x3, starting transfers between devices, all_reduce(): other = lax.ppermute(x, axis, perm)  18.9 us
    ppermute x6, waiting for transfers between devices, all_reduce(): x = x + lax.ppermute(x, axis, perm)  17 us
    ppermute x3, starting transfers between devices, all_reduce(): x = keep + lax.ppermute(send, axis, perm)  14.3 us
    ppermute x3, waiting for transfers between devices, all_reduce(): x = keep + lax.ppermute(send, axis, perm)  10.5 us
    ppermute x3, waiting for transfers between devices, all_reduce(): other = lax.ppermute(x, axis, perm)  6.38 us
    unnamed x24, local copies, waits for them, and re-layouts  4.6 us
    transpose x1, matrix products, spatial_weight_grad(): return jnp.transpose(result, (1, 2, 0, 3))  3.98 us
  transfers between devices with their start and end apart: 13, of which 11 were waited for; matrix products, arithmetic and copies ran while one was open for 9% of the time, Pallas kernels for 0%

profile of v6, /device:TPU:1, one launch (start us, length us, event | category | flops | bytes accessed | tf_op | source)
XLA Modules:
  0.0 129.6 jit_solution(14243129100483985338)
XLA Ops:
  4.1 3.0 %multiply_convert_fusion = (bf16[32,16,5,128]{3,1,2,0:T(8,128)(2,1)S(1)}, f32[32,16,5,128]{3,1,2,0:T(8,128)}, f32[32,16,5,128]{3,1,2,0:T(8,128)S(1)}) fusion(f32[128]{0:T(128)S(1)} %copy-done.9, bf16[3,3,128,128]{3,2,1,0:T(8,128)(2,1)S(1)} %copy-done, bf16[32,2,8,7,128]{4,0,3,2,1:T(8,128)(2,1)S(1)} %fusion.12, pred[16,5]{0,1:T(8,128)(4,1)S(1)} %copy-done.10), kind=kOutput, calls=%fused_computation.11 | convolution fusion | flops 742522880 | bytes 4489808 | tf_op jit(solution)/shard_map/conv_general_dilated | solution.py:13
  16.5 4.0 %fusion.22 = f32[3,3,128,128]{3,2,1,0:T(8,128)S(1)} fusion(bf16[2,32,32,128]{3,2,1,0:T(8,128)(2,1)S(1)} %bitcast.141, bf16[2,32,32,128]{3,1,2,0:T(8,128)(2,1)S(1)} %get-tuple-element.5), kind=kOutput, calls=%fused_computation.44 | convolution fusion | flops 579076096 | bytes 1638400 | tf_op jit(solution)/shard_map/transpose | solution.py:33
  22.4 8.7 %collective-permute-start.1 = (f32[800,128]{1,0:T(8,128)S(1)}, f32[800,128]{1,0:T(8,128)S(1)}, u32[]{:S(2)}, u32[]{:S(2)}) collective-permute-start(f32[800,128]{1,0:T(8,128)S(1)} %constant_dynamic-slice_fusion.2), channel_id=1, source_target_pairs={{0,8},{8,0},{16,24},{24,16},{32,40},{40,32},{48,56},{56,48},{64,72... | collective-permute-start | bytes 1228808 | tf_op jit(solution)/shard_map/ppermute | solution.py:105
  32.6 2.2 %collective-permute-start.2 = (f32[400,128]{1,0:T(8,128)S(1)}, f32[400,128]{1,0:T(8,128)S(1)}, u32[]{:S(2)}, u32[]{:S(2)}) collective-permute-start(f32[400,128]{1,0:T(8,128)S(1)} %constant_dynamic-slice_fusion.1), channel_id=1, source_target_pairs={{0,128},{8,136},{16,144},{24,152},{32,160},{40,168},{48,176},{56,1... | collective-permute-start | bytes 614408 | tf_op jit(solution)/shard_map/ppermute | solution.py:105
  34.8 6.0 %collective-permute-done.2 = f32[400,128]{1,0:T(8,128)S(1)} collective-permute-done((f32[400,128]{1,0:T(8,128)S(1)}, f32[400,128]{1,0:T(8,128)S(1)}, u32[]{:S(2)}, u32[]{:S(2)}) %collective-permute-start.2) | collective-permute-done | bytes 204832 | tf_op jit(solution)/shard_map/ppermute | solution.py:105
  40.8 3.4 %collective-permute-start.3 = (f32[200,128]{1,0:T(8,128)S(1)}, f32[200,128]{1,0:T(8,128)S(1)}, u32[]{:S(2)}, u32[]{:S(2)}) collective-permute-start(f32[200,128]{1,0:T(8,128)S(1)} %constant_dynamic-slice_fusion), channel_id=1, source_target_pairs={{0,384},{8,392},{16,400},{24,408},{32,416},{40,424},{48,432},{56,4... | collective-permute-start | bytes 307208 | tf_op jit(solution)/shard_map/ppermute | solution.py:105
  44.2 3.2 %collective-permute-done.3 = f32[200,128]{1,0:T(8,128)S(1)} collective-permute-done((f32[200,128]{1,0:T(8,128)S(1)}, f32[200,128]{1,0:T(8,128)S(1)}, u32[]{:S(2)}, u32[]{:S(2)}) %collective-permute-start.3) | collective-permute-done | bytes 102432 | tf_op jit(solution)/shard_map/ppermute | solution.py:105
  47.4 2.2 %collective-permute-start.4 = (f32[200,128]{1,0:T(8,128)S(1)}, f32[200,128]{1,0:T(8,128)S(1)}, u32[]{:S(2)}, u32[]{:S(2)}) collective-permute-start(f32[200,128]{1,0:T(8,128)S(1)} %dynamic-slice_add_fusion.2), channel_id=1, source_target_pairs={{0,32},{8,40},{16,48},{24,56},{32,0},{40,8},{48,16},{56,24},{64,96... | collective-permute-start | bytes 307208 | tf_op jit(solution)/shard_map/ppermute | solution.py:108
  49.7 3.2 %collective-permute-done.4 = f32[200,128]{1,0:T(8,128)S(1)} collective-permute-done((f32[200,128]{1,0:T(8,128)S(1)}, f32[200,128]{1,0:T(8,128)S(1)}, u32[]{:S(2)}, u32[]{:S(2)}) %collective-permute-start.4) | collective-permute-done | bytes 102432 | tf_op jit(solution)/shard_map/ppermute | solution.py:108
  52.9 3.8 %collective-permute-start.5 = (f32[200,128]{1,0:T(8,128)S(1)}, f32[200,128]{1,0:T(8,128)S(1)}, u32[]{:S(2)}, u32[]{:S(2)}) collective-permute-start(f32[200,128]{1,0:T(8,128)S(1)} %add.125), channel_id=1, source_target_pairs={{0,96},{8,104},{16,112},{24,120},{32,64},{40,72},{48,80},{56,88},{... | collective-permute-start | bytes 307208 | tf_op jit(solution)/shard_map/ppermute | solution.py:108
  56.7 2.9 %collective-permute-done.5 = f32[200,128]{1,0:T(8,128)S(1)} collective-permute-done((f32[200,128]{1,0:T(8,128)S(1)}, f32[200,128]{1,0:T(8,128)S(1)}, u32[]{:S(2)}, u32[]{:S(2)}) %collective-permute-start.5) | collective-permute-done | bytes 102432 | tf_op jit(solution)/shard_map/ppermute | solution.py:108
  59.6 4.3 %collective-permute-start.6 = (f32[200,128]{1,0:T(8,128)S(1)}, f32[200,128]{1,0:T(8,128)S(1)}, u32[]{:S(2)}, u32[]{:S(2)}) collective-permute-start(f32[200,128]{1,0:T(8,128)S(1)} %add.126), channel_id=1, source_target_pairs={{0,1},{1,0},{2,3},{3,2},{4,5},{5,4},{6,7},{7,6},{8,9},{9,8},{10,11... | collective-permute-start | bytes 307208 | tf_op jit(solution)/shard_map/ppermute | solution.py:108
  63.9 2.0 %collective-permute-done.6 = f32[200,128]{1,0:T(8,128)S(1)} collective-permute-done((f32[200,128]{1,0:T(8,128)S(1)}, f32[200,128]{1,0:T(8,128)S(1)}, u32[]{:S(2)}, u32[]{:S(2)}) %collective-permute-start.6) | collective-permute-done | bytes 102432 | tf_op jit(solution)/shard_map/ppermute | solution.py:108
  66.0 5.6 %collective-permute-start.7 = (f32[200,128]{1,0:T(8,128)S(1)}, f32[200,128]{1,0:T(8,128)S(1)}, u32[]{:S(2)}, u32[]{:S(2)}) collective-permute-start(f32[200,128]{1,0:T(8,128)S(1)} %add.127), channel_id=1, source_target_pairs={{0,3},{1,2},{2,1},{3,0},{4,7},{5,6},{6,5},{7,4},{8,11},{9,10},{10,... | collective-permute-start | bytes 307208 | tf_op jit(solution)/shard_map/ppermute | solution.py:108
  71.6 2.5 %collective-permute-done.7 = f32[200,128]{1,0:T(8,128)S(1)} collective-permute-done((f32[200,128]{1,0:T(8,128)S(1)}, f32[200,128]{1,0:T(8,128)S(1)}, u32[]{:S(2)}, u32[]{:S(2)}) %collective-permute-start.7) | collective-permute-done | bytes 102432 | tf_op jit(solution)/shard_map/ppermute | solution.py:108
  74.1 7.1 %collective-permute-start.8 = (f32[200,128]{1,0:T(8,128)S(1)}, f32[200,128]{1,0:T(8,128)S(1)}, u32[]{:S(2)}, u32[]{:S(2)}) collective-permute-start(f32[200,128]{1,0:T(8,128)S(1)} %add.128), channel_id=1, source_target_pairs={{0,4},{1,5},{2,6},{3,7},{4,0},{5,1},{6,2},{7,3},{8,12},{9,13},{10,... | collective-permute-start | bytes 307208 | tf_op jit(solution)/shard_map/ppermute | solution.py:108
  81.3 2.5 %collective-permute-done.8 = f32[200,128]{1,0:T(8,128)S(1)} collective-permute-done((f32[200,128]{1,0:T(8,128)S(1)}, f32[200,128]{1,0:T(8,128)S(1)}, u32[]{:S(2)}, u32[]{:S(2)}) %collective-permute-start.8) | collective-permute-done | bytes 102432 | tf_op jit(solution)/shard_map/ppermute | solution.py:108
  83.8 10.0 %collective-permute-start.9 = (f32[200,128]{1,0:T(8,128)S(1)}, f32[200,128]{1,0:T(8,128)S(1)}, u32[]{:S(2)}, u32[]{:S(2)}) collective-permute-start(f32[200,128]{1,0:T(8,128)S(1)} %add.129), channel_id=1, source_target_pairs={{0,20},{1,21},{2,22},{3,23},{4,16},{5,17},{6,18},{7,19},{8,28},{9,... | collective-permute-start | bytes 307208 | tf_op jit(solution)/shard_map/ppermute | solution.py:108
  93.9 3.9 %collective-permute-done.9 = f32[200,128]{1,0:T(8,128)S(1)} collective-permute-done((f32[200,128]{1,0:T(8,128)S(1)}, f32[200,128]{1,0:T(8,128)S(1)}, u32[]{:S(2)}, u32[]{:S(2)}) %collective-permute-start.9) | collective-permute-done | bytes 102432 | tf_op jit(solution)/shard_map/ppermute | solution.py:108
  97.7 4.4 %collective-permute-start.10 = (f32[200,128]{1,0:T(8,128)S(1)}, f32[200,128]{1,0:T(8,128)S(1)}, u32[]{:S(2)}, u32[]{:S(2)}) collective-permute-start(f32[200,128]{1,0:T(8,128)S(1)} %add.130), channel_id=1, source_target_pairs={{0,384},{8,392},{16,400},{24,408},{32,416},{40,424},{48,432},{56,4... | collective-permute-start | bytes 307208 | tf_op jit(solution)/shard_map/ppermute | solution.py:111
  102.1 2.2 %collective-permute-done.10 = f32[200,128]{1,0:T(8,128)S(1)} collective-permute-done((f32[200,128]{1,0:T(8,128)S(1)}, f32[200,128]{1,0:T(8,128)S(1)}, u32[]{:S(2)}, u32[]{:S(2)}) %collective-permute-start.10) | collective-permute-done | bytes 102432 | tf_op jit(solution)/shard_map/ppermute | solution.py:111
  104.5 1.9 %collective-permute-start.11 = (f32[400,128]{1,0:T(8,128)S(1)}, f32[400,128]{1,0:T(8,128)S(1)}, u32[]{:S(2)}, u32[]{:S(2)}) collective-permute-start(f32[400,128]{1,0:T(8,128)S(1)} %get-tuple-element.15), channel_id=1, source_target_pairs={{0,128},{8,136},{16,144},{24,152},{32,160},{40,168},{48,176},{56,1... | collective-permute-start | bytes 614408 | tf_op jit(solution)/shard_map/ppermute | solution.py:111
  106.8 4.2 %collective-permute-done.11 = f32[400,128]{1,0:T(8,128)S(1)} collective-permute-done((f32[400,128]{1,0:T(8,128)S(1)}, f32[400,128]{1,0:T(8,128)S(1)}, u32[]{:S(2)}, u32[]{:S(2)}) %collective-permute-start.11) | collective-permute-done | bytes 204832 | tf_op jit(solution)/shard_map/ppermute | solution.py:111
  111.1 12.6 %collective-permute-start.12 = (f32[800,128]{1,0:T(8,128)S(1)}, f32[800,128]{1,0:T(8,128)S(1)}, u32[]{:S(2)}, u32[]{:S(2)}) collective-permute-start(f32[800,128]{1,0:T(8,128)S(1)} %get-tuple-element.11), channel_id=1, source_target_pairs={{0,8},{8,0},{16,24},{24,16},{32,40},{40,32},{48,56},{56,48},{64,72... | collective-permute-start | bytes 1228808 | tf_op jit(solution)/shard_map/ppermute | solution.py:111
  (73 shorter events, 22.5 us)
Async XLA Ops:
  0.6 2.9 %copy-start = (bf16[3,3,128,128]{3,2,1,0:T(8,128)(2,1)S(1)}, bf16[3,3,128,128]{3,2,1,0:T(8,128)(2,1)}, u32[]{:S(2)}) copy-start(bf16[3,3,128,128]{3,2,1,0:T(8,128)(2,1)} %param.7) | copy-start | bytes 884740
  0.6 11.8 %collective-permute-start = (bf16[2,32,32,128]{3,2,1,0:T(8,128)(2,1)}, bf16[2,32,32,128]{3,2,1,0:T(8,128)(2,1)}, u32[]{:S(2)}, u32[]{:S(2)}) collective-permute-start(bf16[2,32,32,128]{3,2,1,0:T(8,128)(2,1)} %bitcast.122), channel_id=1, source_target_pairs={{1,0},{2,1},{3,2},{4,3},{5,4},{6,5},{7,6},{9,8},{10,9},{11,10},{12... | collective-permute-start | bytes 1572872 | tf_op jit(solution)/shard_map/ppermute | solution.py:125
  3.4 0.7 copy-start.9
  3.4 0.7 copy-start.10
  7.3 1.0 copy-start.2
  8.4 1.3 %copy-start.6 = (f32[32,16,5,128]{3,1,2,0:T(8,128)S(1)}, f32[32,16,5,128]{3,1,2,0:T(8,128)}, u32[]{:S(2)}) copy-start(f32[32,16,5,128]{3,1,2,0:T(8,128)} %get-tuple-element.7) | copy-start | bytes 3932164
  9.7 1.0 copy-start.1
  9.7 2.4 %copy-start.8 = (bf16[3,128,128]{2,1,0:T(8,128)(2,1)S(1)}, bf16[3,128,128]{2,1,0:T(8,128)(2,1)}, u32[]{:S(2)}) copy-start(bf16[3,128,128]{2,1,0:T(8,128)(2,1)} %param.9) | copy-start | bytes 294916
  12.1 1.3 %copy-start.3 = (bf16[32,2,32,128]{3,0,2,1:T(8,128)(2,1)S(1)}, bf16[32,2,32,128]{3,0,2,1:T(8,128)(2,1)}, u32[]{:S(2)}) copy-start(bf16[32,2,32,128]{3,0,2,1:T(8,128)(2,1)} %copy-done.2) | copy-start | bytes 1572868
  15.5 1.0 copy-start.7
  16.3 4.2 %copy-start.4 = (bf16[2,32,32,128]{3,1,2,0:T(8,128)(2,1)}, bf16[2,32,32,128]{3,1,2,0:T(8,128)(2,1)S(1)}, u32[]{:S(2)}) copy-start(bf16[2,32,32,128]{3,1,2,0:T(8,128)(2,1)S(1)} %get-tuple-element.5) | copy-start | bytes 1572868
  22.4 10.1 %collective-permute-start.1 = (f32[800,128]{1,0:T(8,128)S(1)}, f32[800,128]{1,0:T(8,128)S(1)}, u32[]{:S(2)}, u32[]{:S(2)}) collective-permute-start(f32[800,128]{1,0:T(8,128)S(1)} %constant_dynamic-slice_fusion.2), channel_id=1, source_target_pairs={{0,8},{8,0},{16,24},{24,16},{32,40},{40,32},{48,56},{56,48},{64,72... | collective-permute-start | bytes 1228808 | tf_op jit(solution)/shard_map/ppermute | solution.py:105
  32.6 8.2 %collective-permute-start.2 = (f32[400,128]{1,0:T(8,128)S(1)}, f32[400,128]{1,0:T(8,128)S(1)}, u32[]{:S(2)}, u32[]{:S(2)}) collective-permute-start(f32[400,128]{1,0:T(8,128)S(1)} %constant_dynamic-slice_fusion.1), channel_id=1, source_target_pairs={{0,128},{8,136},{16,144},{24,152},{32,160},{40,168},{48,176},{56,1... | collective-permute-start | bytes 614408 | tf_op jit(solution)/shard_map/ppermute | solution.py:105
  40.8 6.6 %collective-permute-start.3 = (f32[200,128]{1,0:T(8,128)S(1)}, f32[200,128]{1,0:T(8,128)S(1)}, u32[]{:S(2)}, u32[]{:S(2)}) collective-permute-start(f32[200,128]{1,0:T(8,128)S(1)} %constant_dynamic-slice_fusion), channel_id=1, source_target_pairs={{0,384},{8,392},{16,400},{24,408},{32,416},{40,424},{48,432},{56,4... | collective-permute-start | bytes 307208 | tf_op jit(solution)/shard_map/ppermute | solution.py:105
  47.4 5.4 %collective-permute-start.4 = (f32[200,128]{1,0:T(8,128)S(1)}, f32[200,128]{1,0:T(8,128)S(1)}, u32[]{:S(2)}, u32[]{:S(2)}) collective-permute-start(f32[200,128]{1,0:T(8,128)S(1)} %dynamic-slice_add_fusion.2), channel_id=1, source_target_pairs={{0,32},{8,40},{16,48},{24,56},{32,0},{40,8},{48,16},{56,24},{64,96... | collective-permute-start | bytes 307208 | tf_op jit(solution)/shard_map/ppermute | solution.py:108
  52.9 53.5 %copy-start.5 = (bf16[2,32,32,128]{3,1,2,0:T(8,128)(2,1)S(1)}, bf16[2,32,32,128]{3,1,2,0:T(8,128)(2,1)}, u32[]{:S(2)}) copy-start(bf16[2,32,32,128]{3,1,2,0:T(8,128)(2,1)} %copy-done.4) | copy-start | bytes 1572868
  52.9 6.7 %collective-permute-start.5 = (f32[200,128]{1,0:T(8,128)S(1)}, f32[200,128]{1,0:T(8,128)S(1)}, u32[]{:S(2)}, u32[]{:S(2)}) collective-permute-start(f32[200,128]{1,0:T(8,128)S(1)} %add.125), channel_id=1, source_target_pairs={{0,96},{8,104},{16,112},{24,120},{32,64},{40,72},{48,80},{56,88},{... | collective-permute-start | bytes 307208 | tf_op jit(solution)/shard_map/ppermute | solution.py:108
  59.6 6.3 %collective-permute-start.6 = (f32[200,128]{1,0:T(8,128)S(1)}, f32[200,128]{1,0:T(8,128)S(1)}, u32[]{:S(2)}, u32[]{:S(2)}) collective-permute-start(f32[200,128]{1,0:T(8,128)S(1)} %add.126), channel_id=1, source_target_pairs={{0,1},{1,0},{2,3},{3,2},{4,5},{5,4},{6,7},{7,6},{8,9},{9,8},{10,11... | collective-permute-start | bytes 307208 | tf_op jit(solution)/shard_map/ppermute | solution.py:108
  66.0 8.2 %collective-permute-start.7 = (f32[200,128]{1,0:T(8,128)S(1)}, f32[200,128]{1,0:T(8,128)S(1)}, u32[]{:S(2)}, u32[]{:S(2)}) collective-permute-start(f32[200,128]{1,0:T(8,128)S(1)} %add.127), channel_id=1, source_target_pairs={{0,3},{1,2},{2,1},{3,0},{4,7},{5,6},{6,5},{7,4},{8,11},{9,10},{10,... | collective-permute-start | bytes 307208 | tf_op jit(solution)/shard_map/ppermute | solution.py:108
  74.1 9.6 %collective-permute-start.8 = (f32[200,128]{1,0:T(8,128)S(1)}, f32[200,128]{1,0:T(8,128)S(1)}, u32[]{:S(2)}, u32[]{:S(2)}) collective-permute-start(f32[200,128]{1,0:T(8,128)S(1)} %add.128), channel_id=1, source_target_pairs={{0,4},{1,5},{2,6},{3,7},{4,0},{5,1},{6,2},{7,3},{8,12},{9,13},{10,... | collective-permute-start | bytes 307208 | tf_op jit(solution)/shard_map/ppermute | solution.py:108
  83.8 13.9 %collective-permute-start.9 = (f32[200,128]{1,0:T(8,128)S(1)}, f32[200,128]{1,0:T(8,128)S(1)}, u32[]{:S(2)}, u32[]{:S(2)}) collective-permute-start(f32[200,128]{1,0:T(8,128)S(1)} %add.129), channel_id=1, source_target_pairs={{0,20},{1,21},{2,22},{3,23},{4,16},{5,17},{6,18},{7,19},{8,28},{9,... | collective-permute-start | bytes 307208 | tf_op jit(solution)/shard_map/ppermute | solution.py:108
  97.7 6.6 %collective-permute-start.10 = (f32[200,128]{1,0:T(8,128)S(1)}, f32[200,128]{1,0:T(8,128)S(1)}, u32[]{:S(2)}, u32[]{:S(2)}) collective-permute-start(f32[200,128]{1,0:T(8,128)S(1)} %add.130), channel_id=1, source_target_pairs={{0,384},{8,392},{16,400},{24,408},{32,416},{40,424},{48,432},{56,4... | collective-permute-start | bytes 307208 | tf_op jit(solution)/shard_map/ppermute | solution.py:111
  104.5 6.5 %collective-permute-start.11 = (f32[400,128]{1,0:T(8,128)S(1)}, f32[400,128]{1,0:T(8,128)S(1)}, u32[]{:S(2)}, u32[]{:S(2)}) collective-permute-start(f32[400,128]{1,0:T(8,128)S(1)} %get-tuple-element.15), channel_id=1, source_target_pairs={{0,128},{8,136},{16,144},{24,152},{32,160},{40,168},{48,176},{56,1... | collective-permute-start | bytes 614408 | tf_op jit(solution)/shard_map/ppermute | solution.py:111
  111.1 16.2 %collective-permute-start.12 = (f32[800,128]{1,0:T(8,128)S(1)}, f32[800,128]{1,0:T(8,128)S(1)}, u32[]{:S(2)}, u32[]{:S(2)}) collective-permute-start(f32[800,128]{1,0:T(8,128)S(1)} %get-tuple-element.11), channel_id=1, source_target_pairs={{0,8},{8,0},{16,24},{24,16},{32,40},{40,32},{48,56},{56,48},{64,72... | collective-permute-start | bytes 1228808 | tf_op jit(solution)/shard_map/ppermute | solution.py:111

commit v7 on v6

--- a/solution.py
+++ b/solution.py
@@ -73,7 +73,7 @@
     for b in range(2):
         clip_step(4, 4, GRAY4, b, "add")
     pos = {lab: p for p, lab in enumerate(ZRING)}
-    for b in range(4):
+    for b in (3, 2, 1, 0):
         perm = []
         for c in range(n_clip):
             zh = (c // 2) % 2

time: 130 us -> 133 us (1.023)
  waiting for transfers between devices: 33.9 us -> 42.6 us
  starting transfers between devices: 67.8 us -> 62.1 us
    ppermute x6, waiting for transfers between devices: 17 us -> 25.8 us  [all_reduce(): x = x + lax.ppermute(x, axis, perm)]
    ppermute x6, starting transfers between devices: 33.1 us -> 27 us  [all_reduce(): x = x + lax.ppermute(x, axis, perm)]
where the time goes in v7:
time: 133 us
  starting transfers between devices  62.1 us (47%)
  waiting for transfers between devices  42.6 us (32%)
  matrix products  13.8 us (10%)
  local copies, waits for them, and re-layouts  7.05 us (5%)
  other arithmetic  5.95 us (4%)
    ppermute x6, starting transfers between devices, all_reduce(): x = x + lax.ppermute(x, axis, perm)  27 us
    ppermute x6, waiting for transfers between devices, all_reduce(): x = x + lax.ppermute(x, axis, perm)  25.8 us
    ppermute x3, starting transfers between devices, all_reduce(): other = lax.ppermute(x, axis, perm)  19.4 us
    ppermute x3, starting transfers between devices, all_reduce(): x = keep + lax.ppermute(send, axis, perm)  14.3 us
    ppermute x3, waiting for transfers between devices, all_reduce(): x = keep + lax.ppermute(send, axis, perm)  10.5 us
    ppermute x3, waiting for transfers between devices, all_reduce(): other = lax.ppermute(x, axis, perm)  6.38 us
    unnamed x24, local copies, waits for them, and re-layouts  4.6 us
    transpose x1, matrix products, spatial_weight_grad(): return jnp.transpose(result, (1, 2, 0, 3))  3.98 us
  transfers between devices with their start and end apart: 13, of which 11 were waited for; matrix products, arithmetic and copies ran while one was open for 9% of the time, Pallas kernels for 0%

profile of v7, /device:TPU:1, one launch (start us, length us, event | category | flops | bytes accessed | tf_op | source)
XLA Modules:
  0.0 132.7 jit_solution(6940918326098170664)
XLA Ops:
  4.1 3.0 %multiply_convert_fusion = (bf16[32,16,5,128]{3,1,2,0:T(8,128)(2,1)S(1)}, f32[32,16,5,128]{3,1,2,0:T(8,128)}, f32[32,16,5,128]{3,1,2,0:T(8,128)S(1)}) fusion(f32[128]{0:T(128)S(1)} %copy-done.9, bf16[3,3,128,128]{3,2,1,0:T(8,128)(2,1)S(1)} %copy-done, bf16[32,2,8,7,128]{4,0,3,2,1:T(8,128)(2,1)S(1)} %fusion.12, pred[16,5]{0,1:T(8,128)(4,1)S(1)} %copy-done.10), kind=kOutput, calls=%fused_computation.11 | convolution fusion | flops 742522880 | bytes 4489808 | tf_op jit(solution)/shard_map/conv_general_dilated | solution.py:13
  16.5 4.0 %fusion.22 = f32[3,3,128,128]{3,2,1,0:T(8,128)S(1)} fusion(bf16[2,32,32,128]{3,2,1,0:T(8,128)(2,1)S(1)} %bitcast.141, bf16[2,32,32,128]{3,1,2,0:T(8,128)(2,1)S(1)} %get-tuple-element.5), kind=kOutput, calls=%fused_computation.44 | convolution fusion | flops 579076096 | bytes 1638400 | tf_op jit(solution)/shard_map/transpose | solution.py:33
  22.4 8.7 %collective-permute-start.1 = (f32[800,128]{1,0:T(8,128)S(1)}, f32[800,128]{1,0:T(8,128)S(1)}, u32[]{:S(2)}, u32[]{:S(2)}) collective-permute-start(f32[800,128]{1,0:T(8,128)S(1)} %constant_dynamic-slice_fusion.2), channel_id=1, source_target_pairs={{0,8},{8,0},{16,24},{24,16},{32,40},{40,32},{48,56},{56,48},{64,72... | collective-permute-start | bytes 1228808 | tf_op jit(solution)/shard_map/ppermute | solution.py:105
  32.6 2.2 %collective-permute-start.2 = (f32[400,128]{1,0:T(8,128)S(1)}, f32[400,128]{1,0:T(8,128)S(1)}, u32[]{:S(2)}, u32[]{:S(2)}) collective-permute-start(f32[400,128]{1,0:T(8,128)S(1)} %constant_dynamic-slice_fusion.1), channel_id=1, source_target_pairs={{0,128},{8,136},{16,144},{24,152},{32,160},{40,168},{48,176},{56,1... | collective-permute-start | bytes 614408 | tf_op jit(solution)/shard_map/ppermute | solution.py:105
  34.8 6.0 %collective-permute-done.2 = f32[400,128]{1,0:T(8,128)S(1)} collective-permute-done((f32[400,128]{1,0:T(8,128)S(1)}, f32[400,128]{1,0:T(8,128)S(1)}, u32[]{:S(2)}, u32[]{:S(2)}) %collective-permute-start.2) | collective-permute-done | bytes 204832 | tf_op jit(solution)/shard_map/ppermute | solution.py:105
  40.8 3.4 %collective-permute-start.3 = (f32[200,128]{1,0:T(8,128)S(1)}, f32[200,128]{1,0:T(8,128)S(1)}, u32[]{:S(2)}, u32[]{:S(2)}) collective-permute-start(f32[200,128]{1,0:T(8,128)S(1)} %constant_dynamic-slice_fusion), channel_id=1, source_target_pairs={{0,384},{8,392},{16,400},{24,408},{32,416},{40,424},{48,432},{56,4... | collective-permute-start | bytes 307208 | tf_op jit(solution)/shard_map/ppermute | solution.py:105
  44.2 3.2 %collective-permute-done.3 = f32[200,128]{1,0:T(8,128)S(1)} collective-permute-done((f32[200,128]{1,0:T(8,128)S(1)}, f32[200,128]{1,0:T(8,128)S(1)}, u32[]{:S(2)}, u32[]{:S(2)}) %collective-permute-start.3) | collective-permute-done | bytes 102432 | tf_op jit(solution)/shard_map/ppermute | solution.py:105
  47.4 2.2 %collective-permute-start.4 = (f32[200,128]{1,0:T(8,128)S(1)}, f32[200,128]{1,0:T(8,128)S(1)}, u32[]{:S(2)}, u32[]{:S(2)}) collective-permute-start(f32[200,128]{1,0:T(8,128)S(1)} %dynamic-slice_add_fusion.2), channel_id=1, source_target_pairs={{0,32},{8,40},{16,48},{24,56},{32,0},{40,8},{48,16},{56,24},{64,96... | collective-permute-start | bytes 307208 | tf_op jit(solution)/shard_map/ppermute | solution.py:108
  49.7 3.2 %collective-permute-done.4 = f32[200,128]{1,0:T(8,128)S(1)} collective-permute-done((f32[200,128]{1,0:T(8,128)S(1)}, f32[200,128]{1,0:T(8,128)S(1)}, u32[]{:S(2)}, u32[]{:S(2)}) %collective-permute-start.4) | collective-permute-done | bytes 102432 | tf_op jit(solution)/shard_map/ppermute | solution.py:108
  52.9 3.8 %collective-permute-start.5 = (f32[200,128]{1,0:T(8,128)S(1)}, f32[200,128]{1,0:T(8,128)S(1)}, u32[]{:S(2)}, u32[]{:S(2)}) collective-permute-start(f32[200,128]{1,0:T(8,128)S(1)} %add.125), channel_id=1, source_target_pairs={{0,96},{8,104},{16,112},{24,120},{32,64},{40,72},{48,80},{56,88},{... | collective-permute-start | bytes 307208 | tf_op jit(solution)/shard_map/ppermute | solution.py:108
  56.7 2.9 %collective-permute-done.5 = f32[200,128]{1,0:T(8,128)S(1)} collective-permute-done((f32[200,128]{1,0:T(8,128)S(1)}, f32[200,128]{1,0:T(8,128)S(1)}, u32[]{:S(2)}, u32[]{:S(2)}) %collective-permute-start.5) | collective-permute-done | bytes 102432 | tf_op jit(solution)/shard_map/ppermute | solution.py:108
  59.6 11.4 %collective-permute-start.6 = (f32[200,128]{1,0:T(8,128)S(1)}, f32[200,128]{1,0:T(8,128)S(1)}, u32[]{:S(2)}, u32[]{:S(2)}) collective-permute-start(f32[200,128]{1,0:T(8,128)S(1)} %add.126), channel_id=1, source_target_pairs={{0,20},{1,21},{2,22},{3,23},{4,16},{5,17},{6,18},{7,19},{8,28},{9,... | collective-permute-start | bytes 307208 | tf_op jit(solution)/shard_map/ppermute | solution.py:108
  71.0 4.8 %collective-permute-done.6 = f32[200,128]{1,0:T(8,128)S(1)} collective-permute-done((f32[200,128]{1,0:T(8,128)S(1)}, f32[200,128]{1,0:T(8,128)S(1)}, u32[]{:S(2)}, u32[]{:S(2)}) %collective-permute-start.6) | collective-permute-done | bytes 102432 | tf_op jit(solution)/shard_map/ppermute | solution.py:108
  75.8 5.7 %collective-permute-start.7 = (f32[200,128]{1,0:T(8,128)S(1)}, f32[200,128]{1,0:T(8,128)S(1)}, u32[]{:S(2)}, u32[]{:S(2)}) collective-permute-start(f32[200,128]{1,0:T(8,128)S(1)} %add.127), channel_id=1, source_target_pairs={{0,4},{1,5},{2,6},{3,7},{4,0},{5,1},{6,2},{7,3},{8,12},{9,13},{10,... | collective-permute-start | bytes 307208 | tf_op jit(solution)/shard_map/ppermute | solution.py:108
  81.5 6.2 %collective-permute-done.7 = f32[200,128]{1,0:T(8,128)S(1)} collective-permute-done((f32[200,128]{1,0:T(8,128)S(1)}, f32[200,128]{1,0:T(8,128)S(1)}, u32[]{:S(2)}, u32[]{:S(2)}) %collective-permute-start.7) | collective-permute-done | bytes 102432 | tf_op jit(solution)/shard_map/ppermute | solution.py:108
  87.7 1.9 %collective-permute-start.8 = (f32[200,128]{1,0:T(8,128)S(1)}, f32[200,128]{1,0:T(8,128)S(1)}, u32[]{:S(2)}, u32[]{:S(2)}) collective-permute-start(f32[200,128]{1,0:T(8,128)S(1)} %add.128), channel_id=1, source_target_pairs={{0,3},{1,2},{2,1},{3,0},{4,7},{5,6},{6,5},{7,4},{8,11},{9,10},{10,... | collective-permute-start | bytes 307208 | tf_op jit(solution)/shard_map/ppermute | solution.py:108
  89.6 5.3 %collective-permute-done.8 = f32[200,128]{1,0:T(8,128)S(1)} collective-permute-done((f32[200,128]{1,0:T(8,128)S(1)}, f32[200,128]{1,0:T(8,128)S(1)}, u32[]{:S(2)}, u32[]{:S(2)}) %collective-permute-start.8) | collective-permute-done | bytes 102432 | tf_op jit(solution)/shard_map/ppermute | solution.py:108
  94.9 1.9 %collective-permute-start.9 = (f32[200,128]{1,0:T(8,128)S(1)}, f32[200,128]{1,0:T(8,128)S(1)}, u32[]{:S(2)}, u32[]{:S(2)}) collective-permute-start(f32[200,128]{1,0:T(8,128)S(1)} %add.129), channel_id=1, source_target_pairs={{0,1},{1,0},{2,3},{3,2},{4,5},{5,4},{6,7},{7,6},{8,9},{9,8},{10,11... | collective-permute-start | bytes 307208 | tf_op jit(solution)/shard_map/ppermute | solution.py:108
  96.9 3.5 %collective-permute-done.9 = f32[200,128]{1,0:T(8,128)S(1)} collective-permute-done((f32[200,128]{1,0:T(8,128)S(1)}, f32[200,128]{1,0:T(8,128)S(1)}, u32[]{:S(2)}, u32[]{:S(2)}) %collective-permute-start.9) | collective-permute-done | bytes 102432 | tf_op jit(solution)/shard_map/ppermute | solution.py:108
  100.4 4.4 %collective-permute-start.10 = (f32[200,128]{1,0:T(8,128)S(1)}, f32[200,128]{1,0:T(8,128)S(1)}, u32[]{:S(2)}, u32[]{:S(2)}) collective-permute-start(f32[200,128]{1,0:T(8,128)S(1)} %add.130), channel_id=1, source_target_pairs={{0,384},{8,392},{16,400},{24,408},{32,416},{40,424},{48,432},{56,4... | collective-permute-start | bytes 307208 | tf_op jit(solution)/shard_map/ppermute | solution.py:111
  104.8 2.2 %collective-permute-done.10 = f32[200,128]{1,0:T(8,128)S(1)} collective-permute-done((f32[200,128]{1,0:T(8,128)S(1)}, f32[200,128]{1,0:T(8,128)S(1)}, u32[]{:S(2)}, u32[]{:S(2)}) %collective-permute-start.10) | collective-permute-done | bytes 102432 | tf_op jit(solution)/shard_map/ppermute | solution.py:111
  107.1 1.9 %collective-permute-start.11 = (f32[400,128]{1,0:T(8,128)S(1)}, f32[400,128]{1,0:T(8,128)S(1)}, u32[]{:S(2)}, u32[]{:S(2)}) collective-permute-start(f32[400,128]{1,0:T(8,128)S(1)} %get-tuple-element.15), channel_id=1, source_target_pairs={{0,128},{8,136},{16,144},{24,152},{32,160},{40,168},{48,176},{56,1... | collective-permute-start | bytes 614408 | tf_op jit(solution)/shard_map/ppermute | solution.py:111
  109.4 4.2 %collective-permute-done.11 = f32[400,128]{1,0:T(8,128)S(1)} collective-permute-done((f32[400,128]{1,0:T(8,128)S(1)}, f32[400,128]{1,0:T(8,128)S(1)}, u32[]{:S(2)}, u32[]{:S(2)}) %collective-permute-start.11) | collective-permute-done | bytes 204832 | tf_op jit(solution)/shard_map/ppermute | solution.py:111
  113.7 13.1 %collective-permute-start.12 = (f32[800,128]{1,0:T(8,128)S(1)}, f32[800,128]{1,0:T(8,128)S(1)}, u32[]{:S(2)}, u32[]{:S(2)}) collective-permute-start(f32[800,128]{1,0:T(8,128)S(1)} %get-tuple-element.11), channel_id=1, source_target_pairs={{0,8},{8,0},{16,24},{24,16},{32,40},{40,32},{48,56},{56,48},{64,72... | collective-permute-start | bytes 1228808 | tf_op jit(solution)/shard_map/ppermute | solution.py:111
  (73 shorter events, 22.5 us)
Async XLA Ops:
  0.6 2.9 %copy-start = (bf16[3,3,128,128]{3,2,1,0:T(8,128)(2,1)S(1)}, bf16[3,3,128,128]{3,2,1,0:T(8,128)(2,1)}, u32[]{:S(2)}) copy-start(bf16[3,3,128,128]{3,2,1,0:T(8,128)(2,1)} %param.7) | copy-start | bytes 884740
  0.6 11.8 %collective-permute-start = (bf16[2,32,32,128]{3,2,1,0:T(8,128)(2,1)}, bf16[2,32,32,128]{3,2,1,0:T(8,128)(2,1)}, u32[]{:S(2)}, u32[]{:S(2)}) collective-permute-start(bf16[2,32,32,128]{3,2,1,0:T(8,128)(2,1)} %bitcast.122), channel_id=1, source_target_pairs={{1,0},{2,1},{3,2},{4,3},{5,4},{6,5},{7,6},{9,8},{10,9},{11,10},{12... | collective-permute-start | bytes 1572872 | tf_op jit(solution)/shard_map/ppermute | solution.py:125
  3.4 0.7 copy-start.9
  3.4 0.7 copy-start.10
  7.3 1.0 copy-start.2
  8.4 1.3 copy-start.6
  9.7 1.0 copy-start.1
  9.7 2.4 %copy-start.8 = (bf16[3,128,128]{2,1,0:T(8,128)(2,1)S(1)}, bf16[3,128,128]{2,1,0:T(8,128)(2,1)}, u32[]{:S(2)}) copy-start(bf16[3,128,128]{2,1,0:T(8,128)(2,1)} %param.9) | copy-start | bytes 294916
  12.1 1.3 copy-start.3
  15.5 1.0 copy-start.7
  16.3 4.2 %copy-start.4 = (bf16[2,32,32,128]{3,1,2,0:T(8,128)(2,1)}, bf16[2,32,32,128]{3,1,2,0:T(8,128)(2,1)S(1)}, u32[]{:S(2)}) copy-start(bf16[2,32,32,128]{3,1,2,0:T(8,128)(2,1)S(1)} %get-tuple-element.5) | copy-start | bytes 1572868
  22.4 10.1 %collective-permute-start.1 = (f32[800,128]{1,0:T(8,128)S(1)}, f32[800,128]{1,0:T(8,128)S(1)}, u32[]{:S(2)}, u32[]{:S(2)}) collective-permute-start(f32[800,128]{1,0:T(8,128)S(1)} %constant_dynamic-slice_fusion.2), channel_id=1, source_target_pairs={{0,8},{8,0},{16,24},{24,16},{32,40},{40,32},{48,56},{56,48},{64,72... | collective-permute-start | bytes 1228808 | tf_op jit(solution)/shard_map/ppermute | solution.py:105
  32.6 8.2 %collective-permute-start.2 = (f32[400,128]{1,0:T(8,128)S(1)}, f32[400,128]{1,0:T(8,128)S(1)}, u32[]{:S(2)}, u32[]{:S(2)}) collective-permute-start(f32[400,128]{1,0:T(8,128)S(1)} %constant_dynamic-slice_fusion.1), channel_id=1, source_target_pairs={{0,128},{8,136},{16,144},{24,152},{32,160},{40,168},{48,176},{56,1... | collective-permute-start | bytes 614408 | tf_op jit(solution)/shard_map/ppermute | solution.py:105
  40.8 6.6 %collective-permute-start.3 = (f32[200,128]{1,0:T(8,128)S(1)}, f32[200,128]{1,0:T(8,128)S(1)}, u32[]{:S(2)}, u32[]{:S(2)}) collective-permute-start(f32[200,128]{1,0:T(8,128)S(1)} %constant_dynamic-slice_fusion), channel_id=1, source_target_pairs={{0,384},{8,392},{16,400},{24,408},{32,416},{40,424},{48,432},{56,4... | collective-permute-start | bytes 307208 | tf_op jit(solution)/shard_map/ppermute | solution.py:105
  47.4 5.4 %collective-permute-start.4 = (f32[200,128]{1,0:T(8,128)S(1)}, f32[200,128]{1,0:T(8,128)S(1)}, u32[]{:S(2)}, u32[]{:S(2)}) collective-permute-start(f32[200,128]{1,0:T(8,128)S(1)} %dynamic-slice_add_fusion.2), channel_id=1, source_target_pairs={{0,32},{8,40},{16,48},{24,56},{32,0},{40,8},{48,16},{56,24},{64,96... | collective-permute-start | bytes 307208 | tf_op jit(solution)/shard_map/ppermute | solution.py:108
  52.9 56.1 %copy-start.5 = (bf16[2,32,32,128]{3,1,2,0:T(8,128)(2,1)S(1)}, bf16[2,32,32,128]{3,1,2,0:T(8,128)(2,1)}, u32[]{:S(2)}) copy-start(bf16[2,32,32,128]{3,1,2,0:T(8,128)(2,1)} %copy-done.4) | copy-start | bytes 1572868
  52.9 6.7 %collective-permute-start.5 = (f32[200,128]{1,0:T(8,128)S(1)}, f32[200,128]{1,0:T(8,128)S(1)}, u32[]{:S(2)}, u32[]{:S(2)}) collective-permute-start(f32[200,128]{1,0:T(8,128)S(1)} %add.125), channel_id=1, source_target_pairs={{0,96},{8,104},{16,112},{24,120},{32,64},{40,72},{48,80},{56,88},{... | collective-permute-start | bytes 307208 | tf_op jit(solution)/shard_map/ppermute | solution.py:108
  59.6 16.2 %collective-permute-start.6 = (f32[200,128]{1,0:T(8,128)S(1)}, f32[200,128]{1,0:T(8,128)S(1)}, u32[]{:S(2)}, u32[]{:S(2)}) collective-permute-start(f32[200,128]{1,0:T(8,128)S(1)} %add.126), channel_id=1, source_target_pairs={{0,20},{1,21},{2,22},{3,23},{4,16},{5,17},{6,18},{7,19},{8,28},{9,... | collective-permute-start | bytes 307208 | tf_op jit(solution)/shard_map/ppermute | solution.py:108
  75.8 11.9 %collective-permute-start.7 = (f32[200,128]{1,0:T(8,128)S(1)}, f32[200,128]{1,0:T(8,128)S(1)}, u32[]{:S(2)}, u32[]{:S(2)}) collective-permute-start(f32[200,128]{1,0:T(8,128)S(1)} %add.127), channel_id=1, source_target_pairs={{0,4},{1,5},{2,6},{3,7},{4,0},{5,1},{6,2},{7,3},{8,12},{9,13},{10,... | collective-permute-start | bytes 307208 | tf_op jit(solution)/shard_map/ppermute | solution.py:108
  87.7 7.2 %collective-permute-start.8 = (f32[200,128]{1,0:T(8,128)S(1)}, f32[200,128]{1,0:T(8,128)S(1)}, u32[]{:S(2)}, u32[]{:S(2)}) collective-permute-start(f32[200,128]{1,0:T(8,128)S(1)} %add.128), channel_id=1, source_target_pairs={{0,3},{1,2},{2,1},{3,0},{4,7},{5,6},{6,5},{7,4},{8,11},{9,10},{10,... | collective-permute-start | bytes 307208 | tf_op jit(solution)/shard_map/ppermute | solution.py:108
  94.9 5.4 %collective-permute-start.9 = (f32[200,128]{1,0:T(8,128)S(1)}, f32[200,128]{1,0:T(8,128)S(1)}, u32[]{:S(2)}, u32[]{:S(2)}) collective-permute-start(f32[200,128]{1,0:T(8,128)S(1)} %add.129), channel_id=1, source_target_pairs={{0,1},{1,0},{2,3},{3,2},{4,5},{5,4},{6,7},{7,6},{8,9},{9,8},{10,11... | collective-permute-start | bytes 307208 | tf_op jit(solution)/shard_map/ppermute | solution.py:108
  100.4 6.6 %collective-permute-start.10 = (f32[200,128]{1,0:T(8,128)S(1)}, f32[200,128]{1,0:T(8,128)S(1)}, u32[]{:S(2)}, u32[]{:S(2)}) collective-permute-start(f32[200,128]{1,0:T(8,128)S(1)} %add.130), channel_id=1, source_target_pairs={{0,384},{8,392},{16,400},{24,408},{32,416},{40,424},{48,432},{56,4... | collective-permute-start | bytes 307208 | tf_op jit(solution)/shard_map/ppermute | solution.py:111
  107.1 6.5 %collective-permute-start.11 = (f32[400,128]{1,0:T(8,128)S(1)}, f32[400,128]{1,0:T(8,128)S(1)}, u32[]{:S(2)}, u32[]{:S(2)}) collective-permute-start(f32[400,128]{1,0:T(8,128)S(1)} %get-tuple-element.15), channel_id=1, source_target_pairs={{0,128},{8,136},{16,144},{24,152},{32,160},{40,168},{48,176},{56,1... | collective-permute-start | bytes 614408 | tf_op jit(solution)/shard_map/ppermute | solution.py:111
  113.7 16.7 %collective-permute-start.12 = (f32[800,128]{1,0:T(8,128)S(1)}, f32[800,128]{1,0:T(8,128)S(1)}, u32[]{:S(2)}, u32[]{:S(2)}) collective-permute-start(f32[800,128]{1,0:T(8,128)S(1)} %get-tuple-element.11), channel_id=1, source_target_pairs={{0,8},{8,0},{16,24},{24,16},{32,40},{40,32},{48,56},{56,48},{64,72... | collective-permute-start | bytes 1228808 | tf_op jit(solution)/shard_map/ppermute | solution.py:111

commit v8 on v6

--- a/solution.py
+++ b/solution.py
@@ -26,11 +26,21 @@
 
 
 def spatial_weight_grad(frames, grads):
-    result = lax.conv_general_dilated(
-        frames, grads, (1, 1), ((1, 1), (1, 1)), dimension_numbers=("CHWN", "IHWO", "NHWC"),
-        preferred_element_type=jnp.float32,
-    )
-    return jnp.transpose(result, (1, 2, 0, 3))
+    count, height, width, chan = frames.shape
+    padded = jnp.pad(frames, ((0, 0), (1, 1), (1, 1), (0, 0)))
+    flat_grads = grads.reshape(-1, chan)
+    result = []
+    for i in range(3):
+        row_terms = []
+        for j in range(3):
+            window = padded[:, i : i + height, j : j + width, :].reshape(-1, chan)
+            row_terms.append(
+                lax.dot_general(
+                    window, flat_grads, (((0,), (0,)), ((), ())), preferred_element_type=jnp.float32
+                )
+            )
+        result.append(jnp.stack(row_terms))
+    return jnp.stack(result)
 
 
 def temporal_back(act, later, temporal_w):

time: 130 us -> 129 us (level)
  starting transfers between devices: 67.8 us -> 60.2 us
  waiting for transfers between devices: 33.9 us -> 40.1 us
  local copies, waits for them, and re-layouts: 7.05 us -> 9.52 us
  matrix products: 13.8 us -> 11.8 us
    ppermute x6, starting transfers between devices: 33.1 us -> 28.3 us  [all_reduce(): x = x + lax.ppermute(x, axis, perm)]
    transpose x1 -> x0, matrix products: 3.98 us -> none  [spatial_weight_grad(): return jnp.transpose(result, (1, 2, 0, 3))]
    ppermute x6, waiting for transfers between devices: 17 us -> 20.8 us  [all_reduce(): x = x + lax.ppermute(x, axis, perm)]
    dot_general x0 -> x9, matrix products: none -> 3.65 us  [spatial_weight_grad(): lax.dot_general(window, flat_grads, (((0,), (0,)), ((), ())), preferred_e...]
    ppermute x3, starting transfers between devices: 14.3 us -> 12.6 us  [all_reduce(): x = keep + lax.ppermute(send, axis, perm)]
    ppermute x3, waiting for transfers between devices: 10.5 us -> 12.2 us  [all_reduce(): x = keep + lax.ppermute(send, axis, perm)]
    unnamed x24, local copies, waits for them, and re-layouts: 4.6 us -> 6.11 us
  transfers between devices with their start and end apart: 13 -> 13, of which waited for: 11 -> 11; matrix products, arithmetic and copies ran while one was open for 9% -> 10% of each run, Pallas kernels for 0% -> 0%
where the time goes in v8:
time: 129 us; the launch traced here: 128 us
  starting transfers between devices  60.2 us (47%)
  waiting for transfers between devices  40.1 us (31%)
  matrix products  11.8 us (9%)
  local copies, waits for them, and re-layouts  9.52 us (7%)
  other arithmetic  5.12 us (4%)
    ppermute x6, starting transfers between devices, all_reduce(): x = x + lax.ppermute(x, axis, perm)  28.3 us
    ppermute x6, waiting for transfers between devices, all_reduce(): x = x + lax.ppermute(x, axis, perm)  20.8 us
    ppermute x3, starting transfers between devices, all_reduce(): other = lax.ppermute(x, axis, perm)  17.9 us
    ppermute x3, starting transfers between devices, all_reduce(): x = keep + lax.ppermute(send, axis, perm)  12.6 us
    ppermute x3, waiting for transfers between devices, all_reduce(): x = keep + lax.ppermute(send, axis, perm)  12.2 us
    ppermute x3, waiting for transfers between devices, all_reduce(): other = lax.ppermute(x, axis, perm)  7.08 us
    unnamed x24, local copies, waits for them, and re-layouts  6.11 us
    dot_general x9, matrix products, spatial_weight_grad(): lax.dot_general(window, flat_grads, (((0,), (0,)), ((), ())), preferred_e...  3.65 us
  transfers between devices with their start and end apart: 13, of which 11 were waited for; matrix products, arithmetic and copies ran while one was open for 10% of the time, Pallas kernels for 0%

profile of v8, /device:TPU:1, one launch (start us, length us, event | category | flops | bytes accessed | tf_op | source)
XLA Modules:
  0.0 127.9 jit_solution(15317411942059029832)
XLA Ops:
  4.1 3.5 %multiply_convert_fusion = (bf16[32,16,5,128]{3,1,2,0:T(8,128)(2,1)S(1)}, f32[32,16,5,128]{3,1,2,0:T(8,128)}, f32[32,16,5,128]{3,1,2,0:T(8,128)}) fusion(f32[128]{0:T(128)S(1)} %copy-done.9, bf16[3,3,128,128]{3,2,1,0:T(8,128)(2,1)S(1)} %copy-done, bf16[32,2,8,7,128]{4,0,3,2,1:T(8,128)(2,1)S(1)} %fusion.9, pred[16,5]{0,1:T(8,128)(4,1)S(1)} %copy-done.10), kind=kOutput, calls=%fused_computation.10 | convolution fusion | flops 742522880 | bytes 4489808 | tf_op jit(solution)/shard_map/conv_general_dilated | solution.py:13
  22.4 8.7 %collective-permute-start.1 = (f32[800,128]{1,0:T(8,128)S(1)}, f32[800,128]{1,0:T(8,128)S(1)}, u32[]{:S(2)}, u32[]{:S(2)}) collective-permute-start(f32[800,128]{1,0:T(8,128)S(1)} %constant_dynamic-slice_fusion.2), channel_id=1, source_target_pairs={{0,8},{8,0},{16,24},{24,16},{32,40},{40,32},{48,56},{56,48},{64,72... | collective-permute-start | bytes 1228808 | tf_op jit(solution)/shard_map/ppermute | solution.py:115
  32.5 1.9 %collective-permute-start.2 = (f32[400,128]{1,0:T(8,128)S(1)}, f32[400,128]{1,0:T(8,128)S(1)}, u32[]{:S(2)}, u32[]{:S(2)}) collective-permute-start(f32[400,128]{1,0:T(8,128)S(1)} %constant_dynamic-slice_fusion.1), channel_id=1, source_target_pairs={{0,128},{8,136},{16,144},{24,152},{32,160},{40,168},{48,176},{56,1... | collective-permute-start | bytes 614408 | tf_op jit(solution)/shard_map/ppermute | solution.py:115
  34.5 6.2 %collective-permute-done.2 = f32[400,128]{1,0:T(8,128)S(1)} collective-permute-done((f32[400,128]{1,0:T(8,128)S(1)}, f32[400,128]{1,0:T(8,128)S(1)}, u32[]{:S(2)}, u32[]{:S(2)}) %collective-permute-start.2) | collective-permute-done | bytes 204832 | tf_op jit(solution)/shard_map/ppermute | solution.py:115
  40.8 1.9 %collective-permute-start.3 = (f32[200,128]{1,0:T(8,128)S(1)}, f32[200,128]{1,0:T(8,128)S(1)}, u32[]{:S(2)}, u32[]{:S(2)}) collective-permute-start(f32[200,128]{1,0:T(8,128)S(1)} %constant_dynamic-slice_fusion), channel_id=1, source_target_pairs={{0,384},{8,392},{16,400},{24,408},{32,416},{40,424},{48,432},{56,4... | collective-permute-start | bytes 307208 | tf_op jit(solution)/shard_map/ppermute | solution.py:115
  42.7 4.7 %collective-permute-done.3 = f32[200,128]{1,0:T(8,128)S(1)} collective-permute-done((f32[200,128]{1,0:T(8,128)S(1)}, f32[200,128]{1,0:T(8,128)S(1)}, u32[]{:S(2)}, u32[]{:S(2)}) %collective-permute-start.3) | collective-permute-done | bytes 102432 | tf_op jit(solution)/shard_map/ppermute | solution.py:115
  47.4 1.9 %collective-permute-start.4 = (f32[200,128]{1,0:T(8,128)S(1)}, f32[200,128]{1,0:T(8,128)S(1)}, u32[]{:S(2)}, u32[]{:S(2)}) collective-permute-start(f32[200,128]{1,0:T(8,128)S(1)} %dynamic-slice_add_fusion.2), channel_id=1, source_target_pairs={{0,32},{8,40},{16,48},{24,56},{32,0},{40,8},{48,16},{56,24},{64,96... | collective-permute-start | bytes 307208 | tf_op jit(solution)/shard_map/ppermute | solution.py:118
  49.3 3.5 %collective-permute-done.4 = f32[200,128]{1,0:T(8,128)S(1)} collective-permute-done((f32[200,128]{1,0:T(8,128)S(1)}, f32[200,128]{1,0:T(8,128)S(1)}, u32[]{:S(2)}, u32[]{:S(2)}) %collective-permute-start.4) | collective-permute-done | bytes 102432 | tf_op jit(solution)/shard_map/ppermute | solution.py:118
  52.8 2.1 %collective-permute-start.5 = (f32[200,128]{1,0:T(8,128)S(1)}, f32[200,128]{1,0:T(8,128)S(1)}, u32[]{:S(2)}, u32[]{:S(2)}) collective-permute-start(f32[200,128]{1,0:T(8,128)S(1)} %add.127), channel_id=1, source_target_pairs={{0,96},{8,104},{16,112},{24,120},{32,64},{40,72},{48,80},{56,88},{... | collective-permute-start | bytes 307208 | tf_op jit(solution)/shard_map/ppermute | solution.py:118
  54.9 4.5 %collective-permute-done.5 = f32[200,128]{1,0:T(8,128)S(1)} collective-permute-done((f32[200,128]{1,0:T(8,128)S(1)}, f32[200,128]{1,0:T(8,128)S(1)}, u32[]{:S(2)}, u32[]{:S(2)}) %collective-permute-start.5) | collective-permute-done | bytes 102432 | tf_op jit(solution)/shard_map/ppermute | solution.py:118
  59.4 4.3 %collective-permute-start.6 = (f32[200,128]{1,0:T(8,128)S(1)}, f32[200,128]{1,0:T(8,128)S(1)}, u32[]{:S(2)}, u32[]{:S(2)}) collective-permute-start(f32[200,128]{1,0:T(8,128)S(1)} %add.128), channel_id=1, source_target_pairs={{0,1},{1,0},{2,3},{3,2},{4,5},{5,4},{6,7},{7,6},{8,9},{9,8},{10,11... | collective-permute-start | bytes 307208 | tf_op jit(solution)/shard_map/ppermute | solution.py:118
  63.7 2.0 %collective-permute-done.6 = f32[200,128]{1,0:T(8,128)S(1)} collective-permute-done((f32[200,128]{1,0:T(8,128)S(1)}, f32[200,128]{1,0:T(8,128)S(1)}, u32[]{:S(2)}, u32[]{:S(2)}) %collective-permute-start.6) | collective-permute-done | bytes 102432 | tf_op jit(solution)/shard_map/ppermute | solution.py:118
  65.8 4.1 %collective-permute-start.7 = (f32[200,128]{1,0:T(8,128)S(1)}, f32[200,128]{1,0:T(8,128)S(1)}, u32[]{:S(2)}, u32[]{:S(2)}) collective-permute-start(f32[200,128]{1,0:T(8,128)S(1)} %add.129), channel_id=1, source_target_pairs={{0,3},{1,2},{2,1},{3,0},{4,7},{5,6},{6,5},{7,4},{8,11},{9,10},{10,... | collective-permute-start | bytes 307208 | tf_op jit(solution)/shard_map/ppermute | solution.py:118
  69.9 3.2 %collective-permute-done.7 = f32[200,128]{1,0:T(8,128)S(1)} collective-permute-done((f32[200,128]{1,0:T(8,128)S(1)}, f32[200,128]{1,0:T(8,128)S(1)}, u32[]{:S(2)}, u32[]{:S(2)}) %collective-permute-start.7) | collective-permute-done | bytes 102432 | tf_op jit(solution)/shard_map/ppermute | solution.py:118
  73.1 6.4 %collective-permute-start.8 = (f32[200,128]{1,0:T(8,128)S(1)}, f32[200,128]{1,0:T(8,128)S(1)}, u32[]{:S(2)}, u32[]{:S(2)}) collective-permute-start(f32[200,128]{1,0:T(8,128)S(1)} %add.130), channel_id=1, source_target_pairs={{0,4},{1,5},{2,6},{3,7},{4,0},{5,1},{6,2},{7,3},{8,12},{9,13},{10,... | collective-permute-start | bytes 307208 | tf_op jit(solution)/shard_map/ppermute | solution.py:118
  79.5 3.1 %collective-permute-done.8 = f32[200,128]{1,0:T(8,128)S(1)} collective-permute-done((f32[200,128]{1,0:T(8,128)S(1)}, f32[200,128]{1,0:T(8,128)S(1)}, u32[]{:S(2)}, u32[]{:S(2)}) %collective-permute-start.8) | collective-permute-done | bytes 102432 | tf_op jit(solution)/shard_map/ppermute | solution.py:118
  82.7 9.4 %collective-permute-start.9 = (f32[200,128]{1,0:T(8,128)S(1)}, f32[200,128]{1,0:T(8,128)S(1)}, u32[]{:S(2)}, u32[]{:S(2)}) collective-permute-start(f32[200,128]{1,0:T(8,128)S(1)} %add.131), channel_id=1, source_target_pairs={{0,20},{1,21},{2,22},{3,23},{4,16},{5,17},{6,18},{7,19},{8,28},{9,... | collective-permute-start | bytes 307208 | tf_op jit(solution)/shard_map/ppermute | solution.py:118
  92.1 4.5 %collective-permute-done.9 = f32[200,128]{1,0:T(8,128)S(1)} collective-permute-done((f32[200,128]{1,0:T(8,128)S(1)}, f32[200,128]{1,0:T(8,128)S(1)}, u32[]{:S(2)}, u32[]{:S(2)}) %collective-permute-start.9) | collective-permute-done | bytes 102432 | tf_op jit(solution)/shard_map/ppermute | solution.py:118
  96.6 4.2 %collective-permute-start.10 = (f32[200,128]{1,0:T(8,128)S(1)}, f32[200,128]{1,0:T(8,128)S(1)}, u32[]{:S(2)}, u32[]{:S(2)}) collective-permute-start(f32[200,128]{1,0:T(8,128)S(1)} %add.132), channel_id=1, source_target_pairs={{0,384},{8,392},{16,400},{24,408},{32,416},{40,424},{48,432},{56,4... | collective-permute-start | bytes 307208 | tf_op jit(solution)/shard_map/ppermute | solution.py:121
  100.8 2.7 %collective-permute-done.10 = f32[200,128]{1,0:T(8,128)S(1)} collective-permute-done((f32[200,128]{1,0:T(8,128)S(1)}, f32[200,128]{1,0:T(8,128)S(1)}, u32[]{:S(2)}, u32[]{:S(2)}) %collective-permute-start.10) | collective-permute-done | bytes 102432 | tf_op jit(solution)/shard_map/ppermute | solution.py:121
  103.6 1.9 %collective-permute-start.11 = (f32[400,128]{1,0:T(8,128)S(1)}, f32[400,128]{1,0:T(8,128)S(1)}, u32[]{:S(2)}, u32[]{:S(2)}) collective-permute-start(f32[400,128]{1,0:T(8,128)S(1)} %get-tuple-element.15), channel_id=1, source_target_pairs={{0,128},{8,136},{16,144},{24,152},{32,160},{40,168},{48,176},{56,1... | collective-permute-start | bytes 614408 | tf_op jit(solution)/shard_map/ppermute | solution.py:121
  105.7 4.4 %collective-permute-done.11 = f32[400,128]{1,0:T(8,128)S(1)} collective-permute-done((f32[400,128]{1,0:T(8,128)S(1)}, f32[400,128]{1,0:T(8,128)S(1)}, u32[]{:S(2)}, u32[]{:S(2)}) %collective-permute-start.11) | collective-permute-done | bytes 204832 | tf_op jit(solution)/shard_map/ppermute | solution.py:121
  110.3 11.7 %collective-permute-start.12 = (f32[800,128]{1,0:T(8,128)S(1)}, f32[800,128]{1,0:T(8,128)S(1)}, u32[]{:S(2)}, u32[]{:S(2)}) collective-permute-start(f32[800,128]{1,0:T(8,128)S(1)} %get-tuple-element.11), channel_id=1, source_target_pairs={{0,8},{8,0},{16,24},{24,16},{32,40},{40,32},{48,56},{56,48},{64,72... | collective-permute-start | bytes 1228808 | tf_op jit(solution)/shard_map/ppermute | solution.py:121
  122.0 1.7 %convolution_select_fusion = f32[32,16,5,128]{3,1,2,0:T(8,128)S(1)} fusion(bf16[3,3,128,128]{3,2,1,0:T(8,128)(2,1)S(1)} %copy-done, bf16[32,2,8,7,128]{4,0,3,2,1:T(8,128)(2,1)S(1)} %fusion.10, pred[16,5]{0,1:T(8,128)(4,1)S(1)} %copy-done.10), kind=kOutput, calls=%fused_computation.6 | convolution fusion | flops 739573760 | bytes 2523216 | tf_op jit(solution)/shard_map/conv_general_dilated | solution.py:22
  (85 shorter events, 24.0 us)
Async XLA Ops:
  0.6 2.9 %copy-start = (bf16[3,3,128,128]{3,2,1,0:T(8,128)(2,1)S(1)}, bf16[3,3,128,128]{3,2,1,0:T(8,128)(2,1)}, u32[]{:S(2)}) copy-start(bf16[3,3,128,128]{3,2,1,0:T(8,128)(2,1)} %param.7) | copy-start | bytes 884740
  0.6 13.3 %collective-permute-start = (bf16[2,32,32,128]{3,2,1,0:T(8,128)(2,1)}, bf16[2,32,32,128]{3,2,1,0:T(8,128)(2,1)S(1)}, u32[]{:S(2)}, u32[]{:S(2)}) collective-permute-start(bf16[2,32,32,128]{3,2,1,0:T(8,128)(2,1)} %bitcast.181), channel_id=1, source_target_pairs={{1,0},{2,1},{3,2},{4,3},{5,4},{6,5},{7,6},{9,8},{10,9},{11,10},{12... | collective-permute-start | bytes 1572872 | tf_op jit(solution)/shard_map/ppermute | solution.py:135
  3.4 0.7 copy-start.9
  3.4 0.7 copy-start.10
  7.7 1.7 %copy-start.7 = (f32[32,16,5,128]{3,1,2,0:T(8,128)S(1)}, f32[32,16,5,128]{3,1,2,0:T(8,128)}, u32[]{:S(2)}) copy-start(f32[32,16,5,128]{3,1,2,0:T(8,128)} %get-tuple-element.7) | copy-start | bytes 3932164
  7.8 6.2 %copy-start.4 = (bf16[32,2,32,128]{3,0,2,1:T(8,128)(2,1)}, bf16[32,2,32,128]{3,0,2,1:T(8,128)(2,1)S(1)}, u32[]{:S(2)}) copy-start(bf16[32,2,32,128]{3,0,2,1:T(8,128)(2,1)S(1)} %slice.74) | copy-start | bytes 1572868
  9.4 1.3 %copy-start.6 = (f32[32,16,5,128]{3,1,2,0:T(8,128)S(1)}, f32[32,16,5,128]{3,1,2,0:T(8,128)}, u32[]{:S(2)}) copy-start(f32[32,16,5,128]{3,1,2,0:T(8,128)} %get-tuple-element.8) | copy-start | bytes 3932164
  10.7 1.5 %copy-start.1 = (bf16[1,2,32,32,128]{4,3,2,1,0:T(8,128)(2,1)S(1)}, bf16[1,2,32,32,128]{4,3,2,1,0:T(8,128)(2,1)}, u32[]{:S(2)}) copy-start(bf16[1,2,32,32,128]{4,3,2,1,0:T(8,128)(2,1)} %param.6) | copy-start | bytes 1572868
  10.7 2.9 %copy-start.8 = (bf16[3,128,128]{2,1,0:T(8,128)(2,1)S(1)}, bf16[3,128,128]{2,1,0:T(8,128)(2,1)}, u32[]{:S(2)}) copy-start(bf16[3,128,128]{2,1,0:T(8,128)(2,1)} %param.9) | copy-start | bytes 294916
  14.7 1.3 %copy-start.2 = (f32[32,16,5,128]{3,0,2,1:T(8,128)S(1)}, f32[32,16,5,128]{3,0,2,1:T(8,128)}, u32[]{:S(2)}) copy-start(f32[32,16,5,128]{3,0,2,1:T(8,128)} %copy.33) | copy-start | bytes 3932164
  16.0 1.0 copy-start.3
  20.4 1.0 copy-start.5
  22.4 10.1 %collective-permute-start.1 = (f32[800,128]{1,0:T(8,128)S(1)}, f32[800,128]{1,0:T(8,128)S(1)}, u32[]{:S(2)}, u32[]{:S(2)}) collective-permute-start(f32[800,128]{1,0:T(8,128)S(1)} %constant_dynamic-slice_fusion.2), channel_id=1, source_target_pairs={{0,8},{8,0},{16,24},{24,16},{32,40},{40,32},{48,56},{56,48},{64,72... | collective-permute-start | bytes 1228808 | tf_op jit(solution)/shard_map/ppermute | solution.py:115
  32.5 8.2 %collective-permute-start.2 = (f32[400,128]{1,0:T(8,128)S(1)}, f32[400,128]{1,0:T(8,128)S(1)}, u32[]{:S(2)}, u32[]{:S(2)}) collective-permute-start(f32[400,128]{1,0:T(8,128)S(1)} %constant_dynamic-slice_fusion.1), channel_id=1, source_target_pairs={{0,128},{8,136},{16,144},{24,152},{32,160},{40,168},{48,176},{56,1... | collective-permute-start | bytes 614408 | tf_op jit(solution)/shard_map/ppermute | solution.py:115
  40.8 6.6 %collective-permute-start.3 = (f32[200,128]{1,0:T(8,128)S(1)}, f32[200,128]{1,0:T(8,128)S(1)}, u32[]{:S(2)}, u32[]{:S(2)}) collective-permute-start(f32[200,128]{1,0:T(8,128)S(1)} %constant_dynamic-slice_fusion), channel_id=1, source_target_pairs={{0,384},{8,392},{16,400},{24,408},{32,416},{40,424},{48,432},{56,4... | collective-permute-start | bytes 307208 | tf_op jit(solution)/shard_map/ppermute | solution.py:115
  47.4 5.4 %collective-permute-start.4 = (f32[200,128]{1,0:T(8,128)S(1)}, f32[200,128]{1,0:T(8,128)S(1)}, u32[]{:S(2)}, u32[]{:S(2)}) collective-permute-start(f32[200,128]{1,0:T(8,128)S(1)} %dynamic-slice_add_fusion.2), channel_id=1, source_target_pairs={{0,32},{8,40},{16,48},{24,56},{32,0},{40,8},{48,16},{56,24},{64,96... | collective-permute-start | bytes 307208 | tf_op jit(solution)/shard_map/ppermute | solution.py:118
  52.8 6.6 %collective-permute-start.5 = (f32[200,128]{1,0:T(8,128)S(1)}, f32[200,128]{1,0:T(8,128)S(1)}, u32[]{:S(2)}, u32[]{:S(2)}) collective-permute-start(f32[200,128]{1,0:T(8,128)S(1)} %add.127), channel_id=1, source_target_pairs={{0,96},{8,104},{16,112},{24,120},{32,64},{40,72},{48,80},{56,88},{... | collective-permute-start | bytes 307208 | tf_op jit(solution)/shard_map/ppermute | solution.py:118
  59.4 6.3 %collective-permute-start.6 = (f32[200,128]{1,0:T(8,128)S(1)}, f32[200,128]{1,0:T(8,128)S(1)}, u32[]{:S(2)}, u32[]{:S(2)}) collective-permute-start(f32[200,128]{1,0:T(8,128)S(1)} %add.128), channel_id=1, source_target_pairs={{0,1},{1,0},{2,3},{3,2},{4,5},{5,4},{6,7},{7,6},{8,9},{9,8},{10,11... | collective-permute-start | bytes 307208 | tf_op jit(solution)/shard_map/ppermute | solution.py:118
  65.8 7.3 %collective-permute-start.7 = (f32[200,128]{1,0:T(8,128)S(1)}, f32[200,128]{1,0:T(8,128)S(1)}, u32[]{:S(2)}, u32[]{:S(2)}) collective-permute-start(f32[200,128]{1,0:T(8,128)S(1)} %add.129), channel_id=1, source_target_pairs={{0,3},{1,2},{2,1},{3,0},{4,7},{5,6},{6,5},{7,4},{8,11},{9,10},{10,... | collective-permute-start | bytes 307208 | tf_op jit(solution)/shard_map/ppermute | solution.py:118
  73.1 9.5 %collective-permute-start.8 = (f32[200,128]{1,0:T(8,128)S(1)}, f32[200,128]{1,0:T(8,128)S(1)}, u32[]{:S(2)}, u32[]{:S(2)}) collective-permute-start(f32[200,128]{1,0:T(8,128)S(1)} %add.130), channel_id=1, source_target_pairs={{0,4},{1,5},{2,6},{3,7},{4,0},{5,1},{6,2},{7,3},{8,12},{9,13},{10,... | collective-permute-start | bytes 307208 | tf_op jit(solution)/shard_map/ppermute | solution.py:118
  82.7 13.9 %collective-permute-start.9 = (f32[200,128]{1,0:T(8,128)S(1)}, f32[200,128]{1,0:T(8,128)S(1)}, u32[]{:S(2)}, u32[]{:S(2)}) collective-permute-start(f32[200,128]{1,0:T(8,128)S(1)} %add.131), channel_id=1, source_target_pairs={{0,20},{1,21},{2,22},{3,23},{4,16},{5,17},{6,18},{7,19},{8,28},{9,... | collective-permute-start | bytes 307208 | tf_op jit(solution)/shard_map/ppermute | solution.py:118
  96.6 6.9 %collective-permute-start.10 = (f32[200,128]{1,0:T(8,128)S(1)}, f32[200,128]{1,0:T(8,128)S(1)}, u32[]{:S(2)}, u32[]{:S(2)}) collective-permute-start(f32[200,128]{1,0:T(8,128)S(1)} %add.132), channel_id=1, source_target_pairs={{0,384},{8,392},{16,400},{24,408},{32,416},{40,424},{48,432},{56,4... | collective-permute-start | bytes 307208 | tf_op jit(solution)/shard_map/ppermute | solution.py:121
  103.6 6.5 %collective-permute-start.11 = (f32[400,128]{1,0:T(8,128)S(1)}, f32[400,128]{1,0:T(8,128)S(1)}, u32[]{:S(2)}, u32[]{:S(2)}) collective-permute-start(f32[400,128]{1,0:T(8,128)S(1)} %get-tuple-element.15), channel_id=1, source_target_pairs={{0,128},{8,136},{16,144},{24,152},{32,160},{40,168},{48,176},{56,1... | collective-permute-start | bytes 614408 | tf_op jit(solution)/shard_map/ppermute | solution.py:121
  110.3 15.4 %collective-permute-start.12 = (f32[800,128]{1,0:T(8,128)S(1)}, f32[800,128]{1,0:T(8,128)S(1)}, u32[]{:S(2)}, u32[]{:S(2)}) collective-permute-start(f32[800,128]{1,0:T(8,128)S(1)} %get-tuple-element.11), channel_id=1, source_target_pairs={{0,8},{8,0},{16,24},{24,16},{32,40},{40,32},{48,56},{56,48},{64,72... | collective-permute-start | bytes 1228808 | tf_op jit(solution)/shard_map/ppermute | solution.py:121

commit v9 on v8

--- a/solution.py
+++ b/solution.py
@@ -147,7 +147,7 @@
     n_sw = 9 * chan
     n_tw = 3 * chan
     rows = n_sw + n_tw + 1
-    quantum = 64
+    quantum = 8
     padded_rows = -(-rows // quantum) * quantum
     packed = jnp.concatenate(
         [

time: 129 us -> 126 us (0.977)
  waiting for transfers between devices: 40.1 us -> 37.5 us
    ppermute x3, waiting for transfers between devices: 7.08 us -> 4.69 us  [all_reduce(): other = lax.ppermute(x, axis, perm)]
  transfers between devices with their start and end apart: 13 -> 13, of which waited for: 11 -> 11; matrix products, arithmetic and copies ran while one was open for 10% -> 11% of each run, Pallas kernels for 0% -> 0%
where the time goes in v9:
time: 126 us; the launch traced here: 125 us
  starting transfers between devices  60.2 us (48%)
  waiting for transfers between devices  37.5 us (30%)
  matrix products  11.8 us (9%)
  local copies, waits for them, and re-layouts  9.32 us (7%)
  other arithmetic  5.19 us (4%)
    ppermute x6, starting transfers between devices, all_reduce(): x = x + lax.ppermute(x, axis, perm)  28.3 us
    ppermute x6, waiting for transfers between devices, all_reduce(): x = x + lax.ppermute(x, axis, perm)  20.7 us
    ppermute x3, starting transfers between devices, all_reduce(): other = lax.ppermute(x, axis, perm)  17.9 us
    ppermute x3, starting transfers between devices, all_reduce(): x = keep + lax.ppermute(send, axis, perm)  12.6 us
    ppermute x3, waiting for transfers between devices, all_reduce(): x = keep + lax.ppermute(send, axis, perm)  12.1 us
    unnamed x24, local copies, waits for them, and re-layouts  6.11 us
    ppermute x3, waiting for transfers between devices, all_reduce(): other = lax.ppermute(x, axis, perm)  4.69 us
    dot_general x9, matrix products, spatial_weight_grad(): lax.dot_general(window, flat_grads, (((0,), (0,)), ((), ())), preferred_e...  3.65 us
  transfers between devices with their start and end apart: 13, of which 11 were waited for; matrix products, arithmetic and copies ran while one was open for 11% of the time, Pallas kernels for 0%

profile of v9, /device:TPU:1, one launch (start us, length us, event | category | flops | bytes accessed | tf_op | source)
XLA Modules:
  0.0 125.2 jit_solution(7503895057265443757)
XLA Ops:
  4.1 3.5 %multiply_convert_fusion = (bf16[32,16,5,128]{3,1,2,0:T(8,128)(2,1)S(1)}, f32[32,16,5,128]{3,1,2,0:T(8,128)}, f32[32,16,5,128]{3,1,2,0:T(8,128)}) fusion(f32[128]{0:T(128)S(1)} %copy-done.9, bf16[3,3,128,128]{3,2,1,0:T(8,128)(2,1)S(1)} %copy-done, bf16[32,2,8,7,128]{4,0,3,2,1:T(8,128)(2,1)S(1)} %fusion.9, pred[16,5]{0,1:T(8,128)(4,1)S(1)} %copy-done.10), kind=kOutput, calls=%fused_computation.10 | convolution fusion | flops 742522880 | bytes 4489808 | tf_op jit(solution)/shard_map/conv_general_dilated | solution.py:13
  22.2 8.7 %collective-permute-start.1 = (f32[772,128]{1,0:T(8,128)S(1)}, f32[772,128]{1,0:T(8,128)S(1)}, u32[]{:S(2)}, u32[]{:S(2)}) collective-permute-start(f32[772,128]{1,0:T(8,128)S(1)} %constant_dynamic-slice_fusion.2), channel_id=1, source_target_pairs={{0,8},{8,0},{16,24},{24,16},{32,40},{40,32},{48,56},{56,48},{64,72... | collective-permute-start | bytes 1185800 | tf_op jit(solution)/shard_map/ppermute | solution.py:115
  32.4 1.9 %collective-permute-start.2 = (f32[386,128]{1,0:T(8,128)S(1)}, f32[386,128]{1,0:T(8,128)S(1)}, u32[]{:S(2)}, u32[]{:S(2)}) collective-permute-start(f32[386,128]{1,0:T(8,128)S(1)} %constant_dynamic-slice_fusion.1), channel_id=1, source_target_pairs={{0,128},{8,136},{16,144},{24,152},{32,160},{40,168},{48,176},{56,1... | collective-permute-start | bytes 592904 | tf_op jit(solution)/shard_map/ppermute | solution.py:115
  34.3 6.1 %collective-permute-done.2 = f32[386,128]{1,0:T(8,128)S(1)} collective-permute-done((f32[386,128]{1,0:T(8,128)S(1)}, f32[386,128]{1,0:T(8,128)S(1)}, u32[]{:S(2)}, u32[]{:S(2)}) %collective-permute-start.2) | collective-permute-done | bytes 197664 | tf_op jit(solution)/shard_map/ppermute | solution.py:115
  40.5 1.9 %collective-permute-start.3 = (f32[193,128]{1,0:T(8,128)S(1)}, f32[193,128]{1,0:T(8,128)S(1)}, u32[]{:S(2)}, u32[]{:S(2)}) collective-permute-start(f32[193,128]{1,0:T(8,128)S(1)} %constant_dynamic-slice_fusion), channel_id=1, source_target_pairs={{0,384},{8,392},{16,400},{24,408},{32,416},{40,424},{48,432},{56,4... | collective-permute-start | bytes 296456 | tf_op jit(solution)/shard_map/ppermute | solution.py:115
  42.4 4.7 %collective-permute-done.3 = f32[193,128]{1,0:T(8,128)S(1)} collective-permute-done((f32[193,128]{1,0:T(8,128)S(1)}, f32[193,128]{1,0:T(8,128)S(1)}, u32[]{:S(2)}, u32[]{:S(2)}) %collective-permute-start.3) | collective-permute-done | bytes 98848 | tf_op jit(solution)/shard_map/ppermute | solution.py:115
  47.1 1.9 %collective-permute-start.4 = (f32[193,128]{1,0:T(8,128)S(1)}, f32[193,128]{1,0:T(8,128)S(1)}, u32[]{:S(2)}, u32[]{:S(2)}) collective-permute-start(f32[193,128]{1,0:T(8,128)S(1)} %dynamic-slice_add_fusion.2), channel_id=1, source_target_pairs={{0,32},{8,40},{16,48},{24,56},{32,0},{40,8},{48,16},{56,24},{64,96... | collective-permute-start | bytes 296456 | tf_op jit(solution)/shard_map/ppermute | solution.py:118
  49.1 3.5 %collective-permute-done.4 = f32[193,128]{1,0:T(8,128)S(1)} collective-permute-done((f32[193,128]{1,0:T(8,128)S(1)}, f32[193,128]{1,0:T(8,128)S(1)}, u32[]{:S(2)}, u32[]{:S(2)}) %collective-permute-start.4) | collective-permute-done | bytes 98848 | tf_op jit(solution)/shard_map/ppermute | solution.py:118
  52.5 2.1 %collective-permute-start.5 = (f32[193,128]{1,0:T(8,128)S(1)}, f32[193,128]{1,0:T(8,128)S(1)}, u32[]{:S(2)}, u32[]{:S(2)}) collective-permute-start(f32[193,128]{1,0:T(8,128)S(1)} %add.127), channel_id=1, source_target_pairs={{0,96},{8,104},{16,112},{24,120},{32,64},{40,72},{48,80},{56,88},{... | collective-permute-start | bytes 296456 | tf_op jit(solution)/shard_map/ppermute | solution.py:118
  54.7 4.5 %collective-permute-done.5 = f32[193,128]{1,0:T(8,128)S(1)} collective-permute-done((f32[193,128]{1,0:T(8,128)S(1)}, f32[193,128]{1,0:T(8,128)S(1)}, u32[]{:S(2)}, u32[]{:S(2)}) %collective-permute-start.5) | collective-permute-done | bytes 98848 | tf_op jit(solution)/shard_map/ppermute | solution.py:118
  59.2 4.3 %collective-permute-start.6 = (f32[193,128]{1,0:T(8,128)S(1)}, f32[193,128]{1,0:T(8,128)S(1)}, u32[]{:S(2)}, u32[]{:S(2)}) collective-permute-start(f32[193,128]{1,0:T(8,128)S(1)} %add.128), channel_id=1, source_target_pairs={{0,1},{1,0},{2,3},{3,2},{4,5},{5,4},{6,7},{7,6},{8,9},{9,8},{10,11... | collective-permute-start | bytes 296456 | tf_op jit(solution)/shard_map/ppermute | solution.py:118
  63.5 2.0 %collective-permute-done.6 = f32[193,128]{1,0:T(8,128)S(1)} collective-permute-done((f32[193,128]{1,0:T(8,128)S(1)}, f32[193,128]{1,0:T(8,128)S(1)}, u32[]{:S(2)}, u32[]{:S(2)}) %collective-permute-start.6) | collective-permute-done | bytes 98848 | tf_op jit(solution)/shard_map/ppermute | solution.py:118
  65.5 4.1 %collective-permute-start.7 = (f32[193,128]{1,0:T(8,128)S(1)}, f32[193,128]{1,0:T(8,128)S(1)}, u32[]{:S(2)}, u32[]{:S(2)}) collective-permute-start(f32[193,128]{1,0:T(8,128)S(1)} %add.129), channel_id=1, source_target_pairs={{0,3},{1,2},{2,1},{3,0},{4,7},{5,6},{6,5},{7,4},{8,11},{9,10},{10,... | collective-permute-start | bytes 296456 | tf_op jit(solution)/shard_map/ppermute | solution.py:118
  69.6 3.2 %collective-permute-done.7 = f32[193,128]{1,0:T(8,128)S(1)} collective-permute-done((f32[193,128]{1,0:T(8,128)S(1)}, f32[193,128]{1,0:T(8,128)S(1)}, u32[]{:S(2)}, u32[]{:S(2)}) %collective-permute-start.7) | collective-permute-done | bytes 98848 | tf_op jit(solution)/shard_map/ppermute | solution.py:118
  72.8 6.4 %collective-permute-start.8 = (f32[193,128]{1,0:T(8,128)S(1)}, f32[193,128]{1,0:T(8,128)S(1)}, u32[]{:S(2)}, u32[]{:S(2)}) collective-permute-start(f32[193,128]{1,0:T(8,128)S(1)} %add.130), channel_id=1, source_target_pairs={{0,4},{1,5},{2,6},{3,7},{4,0},{5,1},{6,2},{7,3},{8,12},{9,13},{10,... | collective-permute-start | bytes 296456 | tf_op jit(solution)/shard_map/ppermute | solution.py:118
  79.3 3.1 %collective-permute-done.8 = f32[193,128]{1,0:T(8,128)S(1)} collective-permute-done((f32[193,128]{1,0:T(8,128)S(1)}, f32[193,128]{1,0:T(8,128)S(1)}, u32[]{:S(2)}, u32[]{:S(2)}) %collective-permute-start.8) | collective-permute-done | bytes 98848 | tf_op jit(solution)/shard_map/ppermute | solution.py:118
  82.4 9.4 %collective-permute-start.9 = (f32[193,128]{1,0:T(8,128)S(1)}, f32[193,128]{1,0:T(8,128)S(1)}, u32[]{:S(2)}, u32[]{:S(2)}) collective-permute-start(f32[193,128]{1,0:T(8,128)S(1)} %add.131), channel_id=1, source_target_pairs={{0,20},{1,21},{2,22},{3,23},{4,16},{5,17},{6,18},{7,19},{8,28},{9,... | collective-permute-start | bytes 296456 | tf_op jit(solution)/shard_map/ppermute | solution.py:118
  91.9 4.4 %collective-permute-done.9 = f32[193,128]{1,0:T(8,128)S(1)} collective-permute-done((f32[193,128]{1,0:T(8,128)S(1)}, f32[193,128]{1,0:T(8,128)S(1)}, u32[]{:S(2)}, u32[]{:S(2)}) %collective-permute-start.9) | collective-permute-done | bytes 98848 | tf_op jit(solution)/shard_map/ppermute | solution.py:118
  96.3 4.2 %collective-permute-start.10 = (f32[193,128]{1,0:T(8,128)S(1)}, f32[193,128]{1,0:T(8,128)S(1)}, u32[]{:S(2)}, u32[]{:S(2)}) collective-permute-start(f32[193,128]{1,0:T(8,128)S(1)} %add.132), channel_id=1, source_target_pairs={{0,384},{8,392},{16,400},{24,408},{32,416},{40,424},{48,432},{56,4... | collective-permute-start | bytes 296456 | tf_op jit(solution)/shard_map/ppermute | solution.py:121
  100.7 2.6 %collective-permute-done.10 = f32[193,128]{1,0:T(8,128)S(1)} collective-permute-done((f32[193,128]{1,0:T(8,128)S(1)}, f32[193,128]{1,0:T(8,128)S(1)}, u32[]{:S(2)}, u32[]{:S(2)}) %collective-permute-start.10) | collective-permute-done | bytes 98848 | tf_op jit(solution)/shard_map/ppermute | solution.py:121
  103.3 2.1 %collective-permute-start.11 = (f32[386,128]{1,0:T(8,128)S(1)}, f32[386,128]{1,0:T(8,128)S(1)}, u32[]{:S(2)}, u32[]{:S(2)}) collective-permute-start(f32[386,128]{1,0:T(8,128)S(1)} %pad_maximum_fusion.4), channel_id=1, source_target_pairs={{0,128},{8,136},{16,144},{24,152},{32,160},{40,168},{48,176},{56,1... | collective-permute-start | bytes 592904 | tf_op jit(solution)/shard_map/ppermute | solution.py:121
  105.4 1.7 %convolution_select_fusion = f32[32,16,5,128]{3,1,2,0:T(8,128)S(1)} fusion(bf16[3,3,128,128]{3,2,1,0:T(8,128)(2,1)S(1)} %copy-done, bf16[32,2,8,7,128]{4,0,3,2,1:T(8,128)(2,1)S(1)} %fusion.10, pred[16,5]{0,1:T(8,128)(4,1)S(1)} %copy-done.10), kind=kOutput, calls=%fused_computation.6 | convolution fusion | flops 739573760 | bytes 2523216 | tf_op jit(solution)/shard_map/conv_general_dilated | solution.py:22
  107.7 2.1 %collective-permute-done.11 = f32[386,128]{1,0:T(8,128)S(1)} collective-permute-done((f32[386,128]{1,0:T(8,128)S(1)}, f32[386,128]{1,0:T(8,128)S(1)}, u32[]{:S(2)}, u32[]{:S(2)}) %collective-permute-start.11) | collective-permute-done | bytes 197664 | tf_op jit(solution)/shard_map/ppermute | solution.py:121
  109.9 11.6 %collective-permute-start.12 = (f32[772,128]{1,0:T(8,128)S(1)}, f32[772,128]{1,0:T(8,128)S(1)}, u32[]{:S(2)}, u32[]{:S(2)}) collective-permute-start(f32[772,128]{1,0:T(8,128)S(1)} %pad_maximum_fusion.3), channel_id=1, source_target_pairs={{0,8},{8,0},{16,24},{24,16},{32,40},{40,32},{48,56},{56,48},{64,72... | collective-permute-start | bytes 1185800 | tf_op jit(solution)/shard_map/ppermute | solution.py:121
  (87 shorter events, 23.9 us)
Async XLA Ops:
  0.6 2.9 %copy-start = (bf16[3,3,128,128]{3,2,1,0:T(8,128)(2,1)S(1)}, bf16[3,3,128,128]{3,2,1,0:T(8,128)(2,1)}, u32[]{:S(2)}) copy-start(bf16[3,3,128,128]{3,2,1,0:T(8,128)(2,1)} %param.7) | copy-start | bytes 884740
  0.6 13.3 %collective-permute-start = (bf16[2,32,32,128]{3,2,1,0:T(8,128)(2,1)}, bf16[2,32,32,128]{3,2,1,0:T(8,128)(2,1)S(1)}, u32[]{:S(2)}, u32[]{:S(2)}) collective-permute-start(bf16[2,32,32,128]{3,2,1,0:T(8,128)(2,1)} %bitcast.181), channel_id=1, source_target_pairs={{1,0},{2,1},{3,2},{4,3},{5,4},{6,5},{7,6},{9,8},{10,9},{11,10},{12... | collective-permute-start | bytes 1572872 | tf_op jit(solution)/shard_map/ppermute | solution.py:135
  3.4 0.7 copy-start.9
  3.4 0.7 copy-start.10
  7.7 1.7 %copy-start.7 = (f32[32,16,5,128]{3,1,2,0:T(8,128)S(1)}, f32[32,16,5,128]{3,1,2,0:T(8,128)}, u32[]{:S(2)}) copy-start(f32[32,16,5,128]{3,1,2,0:T(8,128)} %get-tuple-element.7) | copy-start | bytes 3932164
  7.8 6.2 %copy-start.4 = (bf16[32,2,32,128]{3,0,2,1:T(8,128)(2,1)}, bf16[32,2,32,128]{3,0,2,1:T(8,128)(2,1)S(1)}, u32[]{:S(2)}) copy-start(bf16[32,2,32,128]{3,0,2,1:T(8,128)(2,1)S(1)} %slice.74) | copy-start | bytes 1572868
  9.4 1.3 %copy-start.6 = (f32[32,16,5,128]{3,1,2,0:T(8,128)S(1)}, f32[32,16,5,128]{3,1,2,0:T(8,128)}, u32[]{:S(2)}) copy-start(f32[32,16,5,128]{3,1,2,0:T(8,128)} %get-tuple-element.8) | copy-start | bytes 3932164
  10.7 1.5 %copy-start.1 = (bf16[1,2,32,32,128]{4,3,2,1,0:T(8,128)(2,1)S(1)}, bf16[1,2,32,32,128]{4,3,2,1,0:T(8,128)(2,1)}, u32[]{:S(2)}) copy-start(bf16[1,2,32,32,128]{4,3,2,1,0:T(8,128)(2,1)} %param.6) | copy-start | bytes 1572868
  10.7 2.9 %copy-start.8 = (bf16[3,128,128]{2,1,0:T(8,128)(2,1)S(1)}, bf16[3,128,128]{2,1,0:T(8,128)(2,1)}, u32[]{:S(2)}) copy-start(bf16[3,128,128]{2,1,0:T(8,128)(2,1)} %param.9) | copy-start | bytes 294916
  14.7 1.3 %copy-start.2 = (f32[32,16,5,128]{3,0,2,1:T(8,128)S(1)}, f32[32,16,5,128]{3,0,2,1:T(8,128)}, u32[]{:S(2)}) copy-start(f32[32,16,5,128]{3,0,2,1:T(8,128)} %copy.33) | copy-start | bytes 3932164
  16.0 1.0 copy-start.3
  20.4 1.0 copy-start.5
  22.2 10.1 %collective-permute-start.1 = (f32[772,128]{1,0:T(8,128)S(1)}, f32[772,128]{1,0:T(8,128)S(1)}, u32[]{:S(2)}, u32[]{:S(2)}) collective-permute-start(f32[772,128]{1,0:T(8,128)S(1)} %constant_dynamic-slice_fusion.2), channel_id=1, source_target_pairs={{0,8},{8,0},{16,24},{24,16},{32,40},{40,32},{48,56},{56,48},{64,72... | collective-permute-start | bytes 1185800 | tf_op jit(solution)/shard_map/ppermute | solution.py:115
  32.4 8.1 %collective-permute-start.2 = (f32[386,128]{1,0:T(8,128)S(1)}, f32[386,128]{1,0:T(8,128)S(1)}, u32[]{:S(2)}, u32[]{:S(2)}) collective-permute-start(f32[386,128]{1,0:T(8,128)S(1)} %constant_dynamic-slice_fusion.1), channel_id=1, source_target_pairs={{0,128},{8,136},{16,144},{24,152},{32,160},{40,168},{48,176},{56,1... | collective-permute-start | bytes 592904 | tf_op jit(solution)/shard_map/ppermute | solution.py:115
  40.5 6.6 %collective-permute-start.3 = (f32[193,128]{1,0:T(8,128)S(1)}, f32[193,128]{1,0:T(8,128)S(1)}, u32[]{:S(2)}, u32[]{:S(2)}) collective-permute-start(f32[193,128]{1,0:T(8,128)S(1)} %constant_dynamic-slice_fusion), channel_id=1, source_target_pairs={{0,384},{8,392},{16,400},{24,408},{32,416},{40,424},{48,432},{56,4... | collective-permute-start | bytes 296456 | tf_op jit(solution)/shard_map/ppermute | solution.py:115
  47.1 5.4 %collective-permute-start.4 = (f32[193,128]{1,0:T(8,128)S(1)}, f32[193,128]{1,0:T(8,128)S(1)}, u32[]{:S(2)}, u32[]{:S(2)}) collective-permute-start(f32[193,128]{1,0:T(8,128)S(1)} %dynamic-slice_add_fusion.2), channel_id=1, source_target_pairs={{0,32},{8,40},{16,48},{24,56},{32,0},{40,8},{48,16},{56,24},{64,96... | collective-permute-start | bytes 296456 | tf_op jit(solution)/shard_map/ppermute | solution.py:118
  52.5 6.6 %collective-permute-start.5 = (f32[193,128]{1,0:T(8,128)S(1)}, f32[193,128]{1,0:T(8,128)S(1)}, u32[]{:S(2)}, u32[]{:S(2)}) collective-permute-start(f32[193,128]{1,0:T(8,128)S(1)} %add.127), channel_id=1, source_target_pairs={{0,96},{8,104},{16,112},{24,120},{32,64},{40,72},{48,80},{56,88},{... | collective-permute-start | bytes 296456 | tf_op jit(solution)/shard_map/ppermute | solution.py:118
  59.2 6.3 %collective-permute-start.6 = (f32[193,128]{1,0:T(8,128)S(1)}, f32[193,128]{1,0:T(8,128)S(1)}, u32[]{:S(2)}, u32[]{:S(2)}) collective-permute-start(f32[193,128]{1,0:T(8,128)S(1)} %add.128), channel_id=1, source_target_pairs={{0,1},{1,0},{2,3},{3,2},{4,5},{5,4},{6,7},{7,6},{8,9},{9,8},{10,11... | collective-permute-start | bytes 296456 | tf_op jit(solution)/shard_map/ppermute | solution.py:118
  65.5 7.3 %collective-permute-start.7 = (f32[193,128]{1,0:T(8,128)S(1)}, f32[193,128]{1,0:T(8,128)S(1)}, u32[]{:S(2)}, u32[]{:S(2)}) collective-permute-start(f32[193,128]{1,0:T(8,128)S(1)} %add.129), channel_id=1, source_target_pairs={{0,3},{1,2},{2,1},{3,0},{4,7},{5,6},{6,5},{7,4},{8,11},{9,10},{10,... | collective-permute-start | bytes 296456 | tf_op jit(solution)/shard_map/ppermute | solution.py:118
  72.8 9.5 %collective-permute-start.8 = (f32[193,128]{1,0:T(8,128)S(1)}, f32[193,128]{1,0:T(8,128)S(1)}, u32[]{:S(2)}, u32[]{:S(2)}) collective-permute-start(f32[193,128]{1,0:T(8,128)S(1)} %add.130), channel_id=1, source_target_pairs={{0,4},{1,5},{2,6},{3,7},{4,0},{5,1},{6,2},{7,3},{8,12},{9,13},{10,... | collective-permute-start | bytes 296456 | tf_op jit(solution)/shard_map/ppermute | solution.py:118
  82.4 13.9 %collective-permute-start.9 = (f32[193,128]{1,0:T(8,128)S(1)}, f32[193,128]{1,0:T(8,128)S(1)}, u32[]{:S(2)}, u32[]{:S(2)}) collective-permute-start(f32[193,128]{1,0:T(8,128)S(1)} %add.131), channel_id=1, source_target_pairs={{0,20},{1,21},{2,22},{3,23},{4,16},{5,17},{6,18},{7,19},{8,28},{9,... | collective-permute-start | bytes 296456 | tf_op jit(solution)/shard_map/ppermute | solution.py:118
  96.3 6.9 %collective-permute-start.10 = (f32[193,128]{1,0:T(8,128)S(1)}, f32[193,128]{1,0:T(8,128)S(1)}, u32[]{:S(2)}, u32[]{:S(2)}) collective-permute-start(f32[193,128]{1,0:T(8,128)S(1)} %add.132), channel_id=1, source_target_pairs={{0,384},{8,392},{16,400},{24,408},{32,416},{40,424},{48,432},{56,4... | collective-permute-start | bytes 296456 | tf_op jit(solution)/shard_map/ppermute | solution.py:121
  103.3 6.5 %collective-permute-start.11 = (f32[386,128]{1,0:T(8,128)S(1)}, f32[386,128]{1,0:T(8,128)S(1)}, u32[]{:S(2)}, u32[]{:S(2)}) collective-permute-start(f32[386,128]{1,0:T(8,128)S(1)} %pad_maximum_fusion.4), channel_id=1, source_target_pairs={{0,128},{8,136},{16,144},{24,152},{32,160},{40,168},{48,176},{56,1... | collective-permute-start | bytes 592904 | tf_op jit(solution)/shard_map/ppermute | solution.py:121
  109.9 13.0 %collective-permute-start.12 = (f32[772,128]{1,0:T(8,128)S(1)}, f32[772,128]{1,0:T(8,128)S(1)}, u32[]{:S(2)}, u32[]{:S(2)}) collective-permute-start(f32[772,128]{1,0:T(8,128)S(1)} %pad_maximum_fusion.3), channel_id=1, source_target_pairs={{0,8},{8,0},{16,24},{24,16},{32,40},{40,32},{48,56},{56,48},{64,72... | collective-permute-start | bytes 1185800 | tf_op jit(solution)/shard_map/ppermute | solution.py:121
